TPU v7x, 128 devices: a whole 4x4x4 slice. The times are simulated.
128 devices in a mesh: row: 8 (over x, core), col: 16 (over z, y).
Axes of the slice: x: 4, y: 4, z: 4, core: 2. Of those that a mesh axis runs over, the one named last changes fastest.
Arguments:
- rhs: float32 [24, 32768], P(None, 'col'), may hold values from -6 to 6
- noise_var: float32 [32768], P('col'), may hold values from 0.9 to 3.6
- block_rows: int32 [8, 2], P('row'), may hold values from 0 to 15, as said below
- kernel_blocks: bfloat16 [8, 16, 2, 1, 2048, 2048], P('row', 'col'), may hold values from -0.0078125 to 0.0078125
Outputs:
- solution_field: float32 [24, 32768], P(None, 'col')
- residual: float32 [24, 32768], P(None, 'col')
Inputs may be any that keep to these rules, and one draw needn't show every extreme that they name: Each of the 16 block rows appears exactly once in block_rows.
All inputs are finite; a program needn't handle non-finite values.
Results may differ from a plain program's by a relative error of at most 0.024.
Values may be sent and summed in bfloat16 or wider, within the bound.
No kernel may reach another device: no remote copies, remote signals or barrier semaphores. Data moves between devices by JAX's collectives and lax.ppermute only.
A program may use at most 128 MiB of HBM per device.

v0:
```python
import jax
import jax.numpy as jnp
from jax import lax
from jax.sharding import PartitionSpec as P

ITERS = 8


def fetch_rows(slab_bf, row_blocks, width):
    pieces = []
    gathered = lax.all_gather(slab_bf, "col", axis=1, tiled=True)
    for k in range(row_blocks.shape[0]):
        pieces.append(lax.dynamic_slice_in_dim(gathered, row_blocks[k] * width, width, 1))
    return pieces


def kernel_terms(slab_bf, row_blocks, blocks):
    col_blocks = blocks.shape[1]
    width = blocks.shape[2]
    vectors = slab_bf.shape[0]
    col_ids = lax.axis_index("col") * col_blocks + jnp.arange(col_blocks, dtype=jnp.int32)
    fetched = fetch_rows(slab_bf, row_blocks, width)
    forward_list = []
    mirrored = [jnp.zeros((vectors, width), jnp.float32)]
    for k in range(row_blocks.shape[0]):
        used = col_ids[0] >= row_blocks[k]
        forward = lax.dot_general(
            slab_bf, blocks[k, 0], (((1,), (1,)), ((), ())), preferred_element_type=jnp.float32
        )
        forward_sum = jnp.where(used, forward, 0.0)
        product = jnp.dot(fetched[k], blocks[k, 0], preferred_element_type=jnp.float32)
        mirrored[0] = mirrored[0] + jnp.where(used, product, 0.0)
        forward_list.append(forward_sum)
    row_sums = lax.psum(jnp.stack(forward_list).astype(jnp.bfloat16), "col").astype(jnp.float32)
    terms = jnp.stack(mirrored, axis=1)
    for k in range(row_blocks.shape[0]):
        select = (col_ids == row_blocks[k]).astype(jnp.float32)
        terms = terms + select[None, :, None] * row_sums[k][:, None, :]
    return terms.reshape(vectors, col_blocks * width)


def slab_total(value):
    return lax.psum(value, "col")


def on_device(rhs, noise_var, block_rows, kernel_blocks):
    blocks = kernel_blocks[0, 0]
    row_blocks = block_rows[0]
    solution = jnp.zeros_like(rhs)
    residual = rhs
    direction = rhs
    norm_now = slab_total(jnp.sum(residual * residual, axis=1))
    for step in range(ITERS):
        terms = kernel_terms(direction.astype(jnp.bfloat16), row_blocks, blocks)
        image = noise_var[None, :] * direction + lax.psum(terms, "row")
        curvature = slab_total(jnp.sum(direction * image, axis=1))
        alpha = norm_now / curvature
        solution = solution + alpha[:, None] * direction
        residual = residual - alpha[:, None] * image
        norm_next = slab_total(jnp.sum(residual * residual, axis=1))
        direction = residual + (norm_next / norm_now)[:, None] * direction
        norm_now = norm_next
    return (solution, residual)


def solution(mesh):
    return jax.shard_map(
        on_device,
        mesh=mesh,
        in_specs=(
            P(None, "col"),
            P("col"),
            P("row", None),
            P("row", "col", None, None, None, None),
        ),
        out_specs=(P(None, "col"), P(None, "col")),
        check_vma=False,
    )
```

profile of v0, /device:TPU:1, one launch (start us, length us, event | category | flops | bytes accessed | tf_op | source)
XLA Modules:
  0.0 2268.4 jit_solution(17030411046813902307)
XLA Ops:
  26.4 82.3 %all-reduce.18.cloned.1.call-done = bf16[2,24,2048]{2,1,0:T(8,128)(2,1)} async-done(((bf16[2,24,2048]{2,1,0:T(8,128)(2,1)}), bf16[2,24,2048]{2,1,0:T(8,128)(2,1)}) %all-reduce.18.cloned.1.call-update) | async-done | bytes 196624 | tf_op jit(solution)/shard_map/psum | solution.py:34
  109.7 45.5 %all-gather.9.cloned.1.call-done = bf16[24,32768]{1,0:T(8,128)(2,1)} async-done(((bf16[24,2048]{1,0:T(8,128)(2,1)}), bf16[24,32768]{1,0:T(8,128)(2,1)}) %all-gather.9.cloned.1.call-update) | async-done | bytes 1572880 | tf_op jit(solution)/shard_map/all_gather | solution.py:11
  165.3 58.5 %all-reduce.20.cloned.1.call-done = f32[24,2048]{1,0:T(8,128)} async-done(((f32[24,2048]{1,0:T(8,128)}), f32[24,2048]{1,0:T(8,128)}) %all-reduce.20.cloned.1.call-update) | async-done | bytes 196624 | tf_op jit(solution)/shard_map/psum | solution.py:55
  224.9 33.7 %all-reduce = (f32[24]{0:T(128)S(1)}, f32[24]{0:T(128)S(1)}) all-reduce(f32[24]{0:T(128)S(1)} %get-tuple-element.3, f32[24]{0:T(128)S(1)} %get-tuple-element.2), channel_id=1, replica_groups=mesh['row'=8,'col'=16] {'col'}, use_global_device_ids=true, to_apply=%region_1.0 | all-reduce | flops 48 | bytes 384 | tf_op jit(solution)/shard_map/psum | solution.py:43
  302.2 93.0 %all-reduce.22.cloned.1.call-done = bf16[2,24,2048]{2,1,0:T(8,128)(2,1)} async-done(((bf16[2,24,2048]{2,1,0:T(8,128)(2,1)}), bf16[2,24,2048]{2,1,0:T(8,128)(2,1)}) %all-reduce.22.cloned.1.call-update) | async-done | bytes 196624 | tf_op jit(solution)/shard_map/psum | solution.py:34
  396.2 45.4 %all-gather.11.cloned.1.call-done = bf16[24,32768]{1,0:T(8,128)(2,1)} async-done(((bf16[24,2048]{1,0:T(8,128)(2,1)}), bf16[24,32768]{1,0:T(8,128)(2,1)}) %all-gather.11.cloned.1.call-update) | async-done | bytes 1572880 | tf_op jit(solution)/shard_map/all_gather | solution.py:11
  451.7 58.5 %all-reduce.24.cloned.1.call-done = f32[24,2048]{1,0:T(8,128)} async-done(((f32[24,2048]{1,0:T(8,128)}), f32[24,2048]{1,0:T(8,128)}) %all-reduce.24.cloned.1.call-update) | async-done | bytes 196624 | tf_op jit(solution)/shard_map/psum | solution.py:55
  511.4 33.7 %psum.231 = f32[24]{0:T(128)S(1)} all-reduce(f32[24]{0:T(128)S(1)} %multiply_reduce_fusion.12), channel_id=1, replica_groups=mesh['row'=8,'col'=16] {'col'}, use_global_device_ids=true, to_apply=%region_11.12 | all-reduce | flops 24 | bytes 192 | tf_op jit(solution)/shard_map/psum | solution.py:43
  587.8 93.0 %all-reduce.26.cloned.1.call-done = bf16[2,24,2048]{2,1,0:T(8,128)(2,1)} async-done(((bf16[2,24,2048]{2,1,0:T(8,128)(2,1)}), bf16[2,24,2048]{2,1,0:T(8,128)(2,1)}) %all-reduce.26.cloned.1.call-update) | async-done | bytes 196624 | tf_op jit(solution)/shard_map/psum | solution.py:34
  681.8 45.5 %all-gather.13.cloned.1.call-done = bf16[24,32768]{1,0:T(8,128)(2,1)} async-done(((bf16[24,2048]{1,0:T(8,128)(2,1)}), bf16[24,32768]{1,0:T(8,128)(2,1)}) %all-gather.13.cloned.1.call-update) | async-done | bytes 1572880 | tf_op jit(solution)/shard_map/all_gather | solution.py:11
  737.4 58.5 %all-reduce.28.cloned.1.call-done = f32[24,2048]{1,0:T(8,128)} async-done(((f32[24,2048]{1,0:T(8,128)}), f32[24,2048]{1,0:T(8,128)}) %all-reduce.28.cloned.1.call-update) | async-done | bytes 196624 | tf_op jit(solution)/shard_map/psum | solution.py:55
  797.0 33.7 %psum.235 = f32[24]{0:T(128)S(1)} all-reduce(f32[24]{0:T(128)S(1)} %multiply_reduce_fusion.10), channel_id=1, replica_groups=mesh['row'=8,'col'=16] {'col'}, use_global_device_ids=true, to_apply=%region_17.18 | all-reduce | flops 24 | bytes 192 | tf_op jit(solution)/shard_map/psum | solution.py:43
  873.6 93.0 %all-reduce.30.cloned.1.call-done = bf16[2,24,2048]{2,1,0:T(8,128)(2,1)} async-done(((bf16[2,24,2048]{2,1,0:T(8,128)(2,1)}), bf16[2,24,2048]{2,1,0:T(8,128)(2,1)}) %all-reduce.30.cloned.1.call-update) | async-done | bytes 196624 | tf_op jit(solution)/shard_map/psum | solution.py:34
  967.6 45.6 %all-gather.15.cloned.1.call-done = bf16[24,32768]{1,0:T(8,128)(2,1)} async-done(((bf16[24,2048]{1,0:T(8,128)(2,1)}), bf16[24,32768]{1,0:T(8,128)(2,1)}) %all-gather.15.cloned.1.call-update) | async-done | bytes 1572880 | tf_op jit(solution)/shard_map/all_gather | solution.py:11
  1023.2 58.5 %all-reduce.32.cloned.1.call-done = f32[24,2048]{1,0:T(8,128)} async-done(((f32[24,2048]{1,0:T(8,128)}), f32[24,2048]{1,0:T(8,128)}) %all-reduce.32.cloned.1.call-update) | async-done | bytes 196624 | tf_op jit(solution)/shard_map/psum | solution.py:55
  1082.8 33.7 %psum.239 = f32[24]{0:T(128)S(1)} all-reduce(f32[24]{0:T(128)S(1)} %multiply_reduce_fusion.8), channel_id=1, replica_groups=mesh['row'=8,'col'=16] {'col'}, use_global_device_ids=true, to_apply=%region_23.24 | all-reduce | flops 24 | bytes 192 | tf_op jit(solution)/shard_map/psum | solution.py:43
  1159.5 92.8 %all-reduce.34.cloned.1.call-done = bf16[2,24,2048]{2,1,0:T(8,128)(2,1)} async-done(((bf16[2,24,2048]{2,1,0:T(8,128)(2,1)}), bf16[2,24,2048]{2,1,0:T(8,128)(2,1)}) %all-reduce.34.cloned.1.call-update) | async-done | bytes 196624 | tf_op jit(solution)/shard_map/psum | solution.py:34
  1253.2 45.4 %all-gather.17.cloned.1.call-done = bf16[24,32768]{1,0:T(8,128)(2,1)} async-done(((bf16[24,2048]{1,0:T(8,128)(2,1)}), bf16[24,32768]{1,0:T(8,128)(2,1)}) %all-gather.17.cloned.1.call-update) | async-done | bytes 1572880 | tf_op jit(solution)/shard_map/all_gather | solution.py:11
  1308.7 58.5 %all-reduce.36.cloned.1.call-done = f32[24,2048]{1,0:T(8,128)} async-done(((f32[24,2048]{1,0:T(8,128)}), f32[24,2048]{1,0:T(8,128)}) %all-reduce.36.cloned.1.call-update) | async-done | bytes 196624 | tf_op jit(solution)/shard_map/psum | solution.py:55
  1368.3 33.7 %psum.243 = f32[24]{0:T(128)S(1)} all-reduce(f32[24]{0:T(128)S(1)} %multiply_reduce_fusion.6), channel_id=1, replica_groups=mesh['row'=8,'col'=16] {'col'}, use_global_device_ids=true, to_apply=%region_29.30 | all-reduce | flops 24 | bytes 192 | tf_op jit(solution)/shard_map/psum | solution.py:43
  1444.5 93.2 %all-reduce.38.cloned.1.call-done = bf16[2,24,2048]{2,1,0:T(8,128)(2,1)} async-done(((bf16[2,24,2048]{2,1,0:T(8,128)(2,1)}), bf16[2,24,2048]{2,1,0:T(8,128)(2,1)}) %all-reduce.38.cloned.1.call-update) | async-done | bytes 196624 | tf_op jit(solution)/shard_map/psum | solution.py:34
  1538.7 45.4 %all-gather.19.cloned.1.call-done = bf16[24,32768]{1,0:T(8,128)(2,1)} async-done(((bf16[24,2048]{1,0:T(8,128)(2,1)}), bf16[24,32768]{1,0:T(8,128)(2,1)}) %all-gather.19.cloned.1.call-update) | async-done | bytes 1572880 | tf_op jit(solution)/shard_map/all_gather | solution.py:11
  1594.1 58.5 %all-reduce.40.cloned.1.call-done = f32[24,2048]{1,0:T(8,128)} async-done(((f32[24,2048]{1,0:T(8,128)}), f32[24,2048]{1,0:T(8,128)}) %all-reduce.40.cloned.1.call-update) | async-done | bytes 196624 | tf_op jit(solution)/shard_map/psum | solution.py:55
  1653.7 33.7 %psum.247 = f32[24]{0:T(128)S(1)} all-reduce(f32[24]{0:T(128)S(1)} %multiply_reduce_fusion.4), channel_id=1, replica_groups=mesh['row'=8,'col'=16] {'col'}, use_global_device_ids=true, to_apply=%region_35.36 | all-reduce | flops 24 | bytes 192 | tf_op jit(solution)/shard_map/psum | solution.py:43
  1730.1 93.2 %all-reduce.42.cloned.1.call-done = bf16[2,24,2048]{2,1,0:T(8,128)(2,1)} async-done(((bf16[2,24,2048]{2,1,0:T(8,128)(2,1)}), bf16[2,24,2048]{2,1,0:T(8,128)(2,1)}) %all-reduce.42.cloned.1.call-update) | async-done | bytes 196624 | tf_op jit(solution)/shard_map/psum | solution.py:34
  1824.3 45.4 %all-gather.21.cloned.1.call-done = bf16[24,32768]{1,0:T(8,128)(2,1)} async-done(((bf16[24,2048]{1,0:T(8,128)(2,1)}), bf16[24,32768]{1,0:T(8,128)(2,1)}) %all-gather.21.cloned.1.call-update) | async-done | bytes 1572880 | tf_op jit(solution)/shard_map/all_gather | solution.py:11
  1879.7 58.5 %all-reduce.44.cloned.1.call-done = f32[24,2048]{1,0:T(8,128)} async-done(((f32[24,2048]{1,0:T(8,128)}), f32[24,2048]{1,0:T(8,128)}) %all-reduce.44.cloned.1.call-update) | async-done | bytes 196624 | tf_op jit(solution)/shard_map/psum | solution.py:55
  1939.3 33.7 %psum.251 = f32[24]{0:T(128)S(1)} all-reduce(f32[24]{0:T(128)S(1)} %multiply_reduce_fusion.2), channel_id=1, replica_groups=mesh['row'=8,'col'=16] {'col'}, use_global_device_ids=true, to_apply=%region_41.42 | all-reduce | flops 24 | bytes 192 | tf_op jit(solution)/shard_map/psum | solution.py:43
  2015.9 92.8 %all-reduce.46.cloned.1.call-done = bf16[2,24,2048]{2,1,0:T(8,128)(2,1)} async-done(((bf16[2,24,2048]{2,1,0:T(8,128)(2,1)}), bf16[2,24,2048]{2,1,0:T(8,128)(2,1)}) %all-reduce.46.cloned.1.call-update) | async-done | bytes 196624 | tf_op jit(solution)/shard_map/psum | solution.py:34
  2109.7 45.6 %all-gather.23.cloned.1.call-done = bf16[24,32768]{1,0:T(8,128)(2,1)} async-done(((bf16[24,2048]{1,0:T(8,128)(2,1)}), bf16[24,32768]{1,0:T(8,128)(2,1)}) %all-gather.23.cloned.1.call-update) | async-done | bytes 1572880 | tf_op jit(solution)/shard_map/all_gather | solution.py:11
  2165.3 58.6 %all-reduce.48.cloned.1.call-done = f32[24,2048]{1,0:T(8,128)} async-done(((f32[24,2048]{1,0:T(8,128)}), f32[24,2048]{1,0:T(8,128)}) %all-reduce.48.cloned.1.call-update) | async-done | bytes 196624 | tf_op jit(solution)/shard_map/psum | solution.py:55
  2225.0 33.7 %psum.255 = f32[24]{0:T(128)S(1)} all-reduce(f32[24]{0:T(128)S(1)} %multiply_reduce_fusion), channel_id=1, replica_groups=mesh['row'=8,'col'=16] {'col'}, use_global_device_ids=true, to_apply=%region_47.48 | all-reduce | flops 24 | bytes 192 | tf_op jit(solution)/shard_map/psum | solution.py:43
  (166 shorter events, 414.9 us)
Async XLA Ops:
  7.2 101.6 %all-reduce.18.cloned.1.call-start = ((), (), s32[]{:S(2)}) async-start(), calls=%async_computation.1 | async-start | bytes 393216 | tf_op jit(solution)/shard_map/psum | solution.py:34
  9.6 12.7 copy-start.7
  23.0 132.3 %all-gather.9.cloned.1.call-start = ((), (), s32[]{:S(2)}) async-start(), calls=%async_computation | async-start | bytes 1671168 | tf_op jit(solution)/shard_map/all_gather | solution.py:11
  23.7 200.1 %all-reduce.20.cloned.1.call-start = ((), (), s32[]{:S(2)}) async-start(), calls=%async_computation.2 | async-start | bytes 393216 | tf_op jit(solution)/shard_map/psum | solution.py:55
  109.7 114.1 %copy-start = (f32[24,2048]{1,0:T(8,128)S(1)}, f32[24,2048]{1,0:T(8,128)}, u32[]{:S(2)}) copy-start(f32[24,2048]{1,0:T(8,128)} %param.4) | copy-start | bytes 589828
  109.7 114.1 %copy-start.2 = (f32[2048]{0:T(1024)S(1)}, f32[2048]{0:T(1024)}, u32[]{:S(2)}) copy-start(f32[2048]{0:T(1024)} %param.5) | copy-start | bytes 24580
  165.2 230.0 %all-reduce.22.cloned.1.call-start = ((), (), s32[]{:S(2)}) async-start(), calls=%async_computation.4 | async-start | bytes 393216 | tf_op jit(solution)/shard_map/psum | solution.py:34
  289.3 11.4 copy-start.10
  301.4 140.2 %all-gather.11.cloned.1.call-start = ((), (), s32[]{:S(2)}) async-start(), calls=%async_computation.3 | async-start | bytes 1671168 | tf_op jit(solution)/shard_map/all_gather | solution.py:11
  302.0 208.2 %all-reduce.24.cloned.1.call-start = ((), (), s32[]{:S(2)}) async-start(), calls=%async_computation.5 | async-start | bytes 393216 | tf_op jit(solution)/shard_map/psum | solution.py:55
  396.2 114.0 %copy-start.1 = (f32[24,2048]{1,0:T(8,128)S(1)}, f32[24,2048]{1,0:T(8,128)}, u32[]{:S(2)}) copy-start(f32[24,2048]{1,0:T(8,128)} %all-reduce.20.cloned.1.call-done) | copy-start | bytes 589828
  451.6 229.2 %all-reduce.26.cloned.1.call-start = ((), (), s32[]{:S(2)}) async-start(), calls=%async_computation.7 | async-start | bytes 393216 | tf_op jit(solution)/shard_map/psum | solution.py:34
  574.9 11.4 copy-start.9
  587.0 140.3 %all-gather.13.cloned.1.call-start = ((), (), s32[]{:S(2)}) async-start(), calls=%async_computation.6 | async-start | bytes 1671168 | tf_op jit(solution)/shard_map/all_gather | solution.py:11
  587.8 208.2 %all-reduce.28.cloned.1.call-start = ((), (), s32[]{:S(2)}) async-start(), calls=%async_computation.8 | async-start | bytes 393216 | tf_op jit(solution)/shard_map/psum | solution.py:55
  737.4 229.3 %all-reduce.30.cloned.1.call-start = ((), (), s32[]{:S(2)}) async-start(), calls=%async_computation.10 | async-start | bytes 393216 | tf_op jit(solution)/shard_map/psum | solution.py:34
  872.8 140.3 %all-gather.15.cloned.1.call-start = ((), (), s32[]{:S(2)}) async-start(), calls=%async_computation.9 | async-start | bytes 1671168 | tf_op jit(solution)/shard_map/all_gather | solution.py:11
  873.6 208.2 %all-reduce.32.cloned.1.call-start = ((), (), s32[]{:S(2)}) async-start(), calls=%async_computation.11 | async-start | bytes 393216 | tf_op jit(solution)/shard_map/psum | solution.py:55
  1023.2 229.1 %all-reduce.34.cloned.1.call-start = ((), (), s32[]{:S(2)}) async-start(), calls=%async_computation.13 | async-start | bytes 393216 | tf_op jit(solution)/shard_map/psum | solution.py:34
  1158.4 140.2 %all-gather.17.cloned.1.call-start = ((), (), s32[]{:S(2)}) async-start(), calls=%async_computation.12 | async-start | bytes 1671168 | tf_op jit(solution)/shard_map/all_gather | solution.py:11
  1159.0 208.2 %all-reduce.36.cloned.1.call-start = ((), (), s32[]{:S(2)}) async-start(), calls=%async_computation.14 | async-start | bytes 393216 | tf_op jit(solution)/shard_map/psum | solution.py:55
  1308.6 229.1 %all-reduce.38.cloned.1.call-start = ((), (), s32[]{:S(2)}) async-start(), calls=%async_computation.16 | async-start | bytes 393216 | tf_op jit(solution)/shard_map/psum | solution.py:34
  1431.7 11.4 copy-start.5
  1443.9 140.2 %all-gather.19.cloned.1.call-start = ((), (), s32[]{:S(2)}) async-start(), calls=%async_computation.15 | async-start | bytes 1671168 | tf_op jit(solution)/shard_map/all_gather | solution.py:11
  1444.5 208.2 %all-reduce.40.cloned.1.call-start = ((), (), s32[]{:S(2)}) async-start(), calls=%async_computation.17 | async-start | bytes 393216 | tf_op jit(solution)/shard_map/psum | solution.py:55
  1594.1 229.2 %all-reduce.42.cloned.1.call-start = ((), (), s32[]{:S(2)}) async-start(), calls=%async_computation.19 | async-start | bytes 393216 | tf_op jit(solution)/shard_map/psum | solution.py:34
  1717.4 11.4 copy-start.6
  1729.5 140.2 %all-gather.21.cloned.1.call-start = ((), (), s32[]{:S(2)}) async-start(), calls=%async_computation.18 | async-start | bytes 1671168 | tf_op jit(solution)/shard_map/all_gather | solution.py:11
  1730.1 208.2 %all-reduce.44.cloned.1.call-start = ((), (), s32[]{:S(2)}) async-start(), calls=%async_computation.20 | async-start | bytes 393216 | tf_op jit(solution)/shard_map/psum | solution.py:55
  1879.7 229.1 %all-reduce.46.cloned.1.call-start = ((), (), s32[]{:S(2)}) async-start(), calls=%async_computation.22 | async-start | bytes 393216 | tf_op jit(solution)/shard_map/psum | solution.py:34
  2014.9 140.3 %all-gather.23.cloned.1.call-start = ((), (), s32[]{:S(2)}) async-start(), calls=%async_computation.21 | async-start | bytes 1671168 | tf_op jit(solution)/shard_map/all_gather | solution.py:11
  2015.7 208.2 %all-reduce.48.cloned.1.call-start = ((), (), s32[]{:S(2)}) async-start(), calls=%async_computation.23 | async-start | bytes 393216 | tf_op jit(solution)/shard_map/psum | solution.py:55
  (3 other events, 34.2 us)
Sparse Core Ops, SparseCore 0:
  23.1 85.5 all-reduce.17
  111.4 43.7 all-gather.8
  165.4 58.4 all-reduce.19
  301.5 93.6 all-reduce.21
  397.8 43.7 all-gather.10
  451.7 58.4 all-reduce.23
  587.1 93.6 all-reduce.25
  683.6 43.7 all-gather.12
  737.5 58.4 all-reduce.27
  873.0 93.6 all-reduce.29
  969.4 43.7 all-gather.14
  1023.3 58.4 all-reduce.31
  1158.6 93.6 all-reduce.33
  1254.8 43.7 all-gather.16
  1308.8 58.4 all-reduce.35
  1444.0 93.6 all-reduce.37
  1540.3 43.7 all-gather.18
  1594.2 58.4 all-reduce.39
  1729.6 93.6 all-reduce.41
  1825.9 43.7 all-gather.20
  1879.8 58.4 all-reduce.43
  2015.1 93.6 all-reduce.45
  2111.5 43.7 all-gather.22
  2165.4 58.4 all-reduce.47
where the time goes:
time: 2290 us; the launch traced here: 2270 us
  waiting for transfers between devices  1570 us (69%)
  blocking collectives  470 us (21%)
  matrix products  171 us (7%)
  other arithmetic  35.3 us (2%)
    psum x8, waiting for transfers between devices, kernel_terms(): lax.psum(jnp.stack(forward_list).astype(jnp.bfloat16), 'col')  733 us
    psum x15, blocking collectives, slab_total(): return lax.psum(value, 'col')  470 us
    psum x8, waiting for transfers between devices, on_device(): image = noise_var[None, :] * direction + lax.psum(terms, 'row')  468 us
    all_gather x8, waiting for transfers between devices, fetch_rows(): gathered = lax.all_gather(slab_bf, 'col', axis=1, tiled=True)  364 us
    dot_general x16, matrix products, kernel_terms(): lax.dot_general(slab_bf, blocks[k, 0], (((1,), (1,)), ((), ())), preferre...  91 us
    dot_general x16, matrix products, kernel_terms(): jnp.dot(fetched[k], blocks[k, 0], preferred_element_type=jnp.float32)  80 us
  transfers between devices with their start and end apart: 24, of which 24 were waited for; matrix products, arithmetic and copies ran while one was open for 0% of the time, Pallas kernels for 0%

commit v1 on v0

v1 whole, which is shorter than its diff:
```python
import jax
import jax.numpy as jnp
from jax import lax
from jax.sharding import PartitionSpec as P

ITERS = 8
PAD = 8


def all_reduce(x, axis, n):
    rows, width = x.shape
    w = width // n
    y = lax.all_to_all(x.reshape(rows, n, w), axis, 1, 1, tiled=True)
    part = jnp.sum(y, axis=1)
    z = lax.all_to_all(jnp.broadcast_to(part[:, None, :], (rows, n, w)), axis, 1, 1, tiled=True)
    return z.reshape(rows, width)


def pack(blocks, scalars):
    width = blocks[0].shape[1]
    tail = jnp.zeros((PAD, width), jnp.float32).at[0, : scalars.shape[0]].set(scalars)
    return jnp.concatenate(list(blocks) + [tail], axis=0)


def make_on_device(n_row, n_col):
    def on_device(rhs, noise_var, block_rows, kernel_blocks):
        blocks = kernel_blocks[0, 0]
        rows = block_rows[0]
        nb = rows.shape[0]
        vecs, width = rhs.shape
        col = lax.axis_index("col")
        first_row = lax.axis_index("row") == 0
        used = [col >= rows[k] for k in range(nb)]
        owner = [col == rows[k] for k in range(nb)]
        noise = noise_var[None, :]

        def fetch(res):
            sent = [jnp.where(owner[k], res, 0.0) for k in range(nb)]
            out = all_reduce(pack(sent, jnp.sum(res * res, axis=1)), "col", n_col)
            return [out[k * vecs:(k + 1) * vecs] for k in range(nb)], out[nb * vecs, :vecs]

        solution = jnp.zeros_like(rhs)
        residual = rhs
        direction = rhs
        dir_rows, norm_now = fetch(rhs)
        for step in range(ITERS):
            vb = direction.astype(jnp.bfloat16)
            forward = []
            mirrored = jnp.zeros((vecs, width), jnp.float32)
            for k in range(nb):
                f = lax.dot_general(vb, blocks[k, 0], (((1,), (1,)), ((), ())), preferred_element_type=jnp.float32)
                forward.append(jnp.where(used[k], f, 0.0))
                m = jnp.dot(dir_rows[k].astype(jnp.bfloat16), blocks[k, 0], preferred_element_type=jnp.float32)
                mirrored = mirrored + jnp.where(used[k], m, 0.0)
            part = jnp.sum(direction * mirrored, axis=1)
            part = part + jnp.where(first_row, jnp.sum(direction * (noise * direction), axis=1), 0.0)
            for k in range(nb):
                part = part + jnp.sum(dir_rows[k] * forward[k], axis=1)
            out = all_reduce(pack(forward, part), "col", n_col)
            terms = mirrored
            for k in range(nb):
                terms = terms + jnp.where(owner[k], out[k * vecs:(k + 1) * vecs], 0.0)
            out = all_reduce(pack([terms], out[nb * vecs, :vecs]), "row", n_row)
            image = noise * direction + out[:vecs]
            curvature = out[vecs, :vecs]
            alpha = norm_now / curvature
            solution = solution + alpha[:, None] * direction
            residual = residual - alpha[:, None] * image
            if step + 1 < ITERS:
                res_rows, norm_next = fetch(residual)
                beta = norm_next / norm_now
                direction = residual + beta[:, None] * direction
                dir_rows = [res_rows[k] + beta[:, None] * dir_rows[k] for k in range(nb)]
                norm_now = norm_next
        return (solution, residual)

    return on_device


def solution(mesh):
    return jax.shard_map(
        make_on_device(mesh.shape["row"], mesh.shape["col"]),
        mesh=mesh,
        in_specs=(
            P(None, "col"),
            P("col"),
            P("row", None),
            P("row", "col", None, None, None, None),
        ),
        out_specs=(P(None, "col"), P(None, "col")),
        check_vma=False,
    )
```

time: 2290 us -> 781 us (0.34)
  waiting for transfers between devices: 1570 us -> 14.2 us
  blocking collectives: 470 us -> 558 us
    psum x16 -> x0, waiting for transfers between devices: 1200 us -> none  [the longest x8 733 us: kernel_terms(): lax.psum(jnp.stack(forward_list).astype(jnp.bfloat16), 'col')]
    all_to_all x0 -> x46, blocking collectives: none -> 558 us  [the longest x24 315 us: all_reduce(): y = lax.all_to_all(x.reshape(rows, n, w), axis, 1, 1, tiled=True)]
    psum x15 -> x0, blocking collectives: 470 us -> none  [slab_total(): return lax.psum(value, 'col')]
    all_gather x8 -> x0, waiting for transfers between devices: 364 us -> none  [fetch_rows(): gathered = lax.all_gather(slab_bf, 'col', axis=1, tiled=True)]
  transfers between devices with their start and end apart: 24 -> 2, of which waited for: 24 -> 2; matrix products, arithmetic and copies ran while one was open for 0% -> 0% of each run, Pallas kernels for 0% -> 0%
where the time goes in v1:
time: 781 us; the launch traced here: 771 us
  blocking collectives  558 us (71%)
  matrix products  162 us (21%)
  other arithmetic  15.9 us (2%)
  waiting for transfers between devices  14.2 us (2%)
  starting transfers between devices  7.91 us (1%)
    all_to_all x24, blocking collectives, all_reduce(): y = lax.all_to_all(x.reshape(rows, n, w), axis, 1, 1, tiled=True)  315 us
    all_to_all x22, blocking collectives, all_reduce(): lax.all_to_all(jnp.broadcast_to(part[:, None, :], (rows, n, w)), axis, 1,...  243 us
    dot_general x16, matrix products, on_device(): lax.dot_general(vb, blocks[k, 0], (((1,), (1,)), ((), ())), preferred_ele...  88.8 us
    dot_general x16, matrix products, on_device(): jnp.dot(dir_rows[k].astype(jnp.bfloat16), blocks[k, 0], preferred_element...  73.3 us
  transfers between devices with their start and end apart: 2, of which 2 were waited for; matrix products, arithmetic and copies ran while one was open for 0% of the time, Pallas kernels for 0%

profile of v1, /device:TPU:1, one launch (start us, length us, event | category | flops | bytes accessed | tf_op | source)
XLA Modules:
  0.0 771.2 jit_solution(13552108823428423051)
XLA Ops:
  4.4 18.3 %all_to_all.240 = f32[56,16,128]{2,0,1:T(8,128)S(1)} all-to-all(f32[56,16,128]{2,0,1:T(8,128)S(1)} %copy_bitcast_fusion.31), channel_id=1, replica_groups=mesh['row'=8,'col'=16] {'col'}, dimensions={1} | all-to-all | bytes 917504 | tf_op jit(solution)/shard_map/all_to_all | solution.py:13
  51.4 11.2 %all_to_all.241 = f32[56,16,128]{2,0,1:T(8,128)S(1)} all-to-all(f32[56,16,128]{2,0,1:T(8,128)S(1)} %copy_bitcast_fusion.30), channel_id=1, replica_groups=mesh['row'=8,'col'=16] {'col'}, dimensions={1} | all-to-all | bytes 917504 | tf_op jit(solution)/shard_map/all_to_all | solution.py:13
  62.7 11.3 %all_to_all.242 = f32[56,16,128]{2,0,1:T(8,128)S(1)} all-to-all(f32[56,16,128]{2,0,1:T(8,128)S(1)} %broadcast_in_dim.128), channel_id=1, replica_groups=mesh['row'=8,'col'=16] {'col'}, dimensions={1} | all-to-all | bytes 917504 | tf_op jit(solution)/shard_map/all_to_all | solution.py:15
  74.1 16.1 %all_to_all.243 = f32[32,8,256]{2,0,1:T(8,128)S(1)} all-to-all(f32[32,8,256]{2,0,1:T(8,128)S(1)} %bitcast.778), channel_id=1, replica_groups=mesh['row'=8,'col'=16] {'row'}, dimensions={1} | all-to-all | bytes 524288 | tf_op jit(solution)/shard_map/all_to_all | solution.py:13
  102.2 12.2 %all_to_all.244 = f32[56,16,128]{2,0,1:T(8,128)S(1)} all-to-all(f32[56,16,128]{2,0,1:T(8,128)S(1)} %copy_bitcast_fusion.29), channel_id=1, replica_groups=mesh['row'=8,'col'=16] {'col'}, dimensions={1} | all-to-all | bytes 917504 | tf_op jit(solution)/shard_map/all_to_all | solution.py:13
  114.5 12.0 %all_to_all.245 = f32[56,16,128]{2,0,1:T(8,128)S(1)} all-to-all(f32[56,16,128]{2,0,1:T(8,128)S(1)} %broadcast_in_dim.131), channel_id=1, replica_groups=mesh['row'=8,'col'=16] {'col'}, dimensions={1} | all-to-all | bytes 917504 | tf_op jit(solution)/shard_map/all_to_all | solution.py:15
  147.5 11.5 %all_to_all.246 = f32[56,16,128]{2,0,1:T(8,128)S(1)} all-to-all(f32[56,16,128]{2,0,1:T(8,128)S(1)} %copy_bitcast_fusion.28), channel_id=1, replica_groups=mesh['row'=8,'col'=16] {'col'}, dimensions={1} | all-to-all | bytes 917504 | tf_op jit(solution)/shard_map/all_to_all | solution.py:13
  170.4 14.7 %all_to_all.248 = f32[32,8,256]{2,0,1:T(8,128)S(1)} all-to-all(f32[32,8,256]{2,0,1:T(8,128)S(1)} %bitcast.779), channel_id=1, replica_groups=mesh['row'=8,'col'=16] {'row'}, dimensions={1} | all-to-all | bytes 524288 | tf_op jit(solution)/shard_map/all_to_all | solution.py:13
  195.5 12.2 %all_to_all.250 = f32[56,16,128]{2,0,1:T(8,128)S(1)} all-to-all(f32[56,16,128]{2,0,1:T(8,128)S(1)} %copy_bitcast_fusion.27), channel_id=1, replica_groups=mesh['row'=8,'col'=16] {'col'}, dimensions={1} | all-to-all | bytes 917504 | tf_op jit(solution)/shard_map/all_to_all | solution.py:13
  207.8 12.0 %all_to_all.251 = f32[56,16,128]{2,0,1:T(8,128)S(1)} all-to-all(f32[56,16,128]{2,0,1:T(8,128)S(1)} %broadcast_in_dim.134), channel_id=1, replica_groups=mesh['row'=8,'col'=16] {'col'}, dimensions={1} | all-to-all | bytes 917504 | tf_op jit(solution)/shard_map/all_to_all | solution.py:15
  241.6 11.5 %all_to_all.252 = f32[56,16,128]{2,0,1:T(8,128)S(1)} all-to-all(f32[56,16,128]{2,0,1:T(8,128)S(1)} %copy_bitcast_fusion.26), channel_id=1, replica_groups=mesh['row'=8,'col'=16] {'col'}, dimensions={1} | all-to-all | bytes 917504 | tf_op jit(solution)/shard_map/all_to_all | solution.py:13
  264.5 14.7 %all_to_all.254 = f32[32,8,256]{2,0,1:T(8,128)S(1)} all-to-all(f32[32,8,256]{2,0,1:T(8,128)S(1)} %bitcast.780), channel_id=1, replica_groups=mesh['row'=8,'col'=16] {'row'}, dimensions={1} | all-to-all | bytes 524288 | tf_op jit(solution)/shard_map/all_to_all | solution.py:13
  290.2 12.2 %all_to_all.256 = f32[56,16,128]{2,0,1:T(8,128)S(1)} all-to-all(f32[56,16,128]{2,0,1:T(8,128)S(1)} %copy_bitcast_fusion.25), channel_id=1, replica_groups=mesh['row'=8,'col'=16] {'col'}, dimensions={1} | all-to-all | bytes 917504 | tf_op jit(solution)/shard_map/all_to_all | solution.py:13
  302.5 12.2 %all_to_all.257 = f32[56,16,128]{2,0,1:T(8,128)S(1)} all-to-all(f32[56,16,128]{2,0,1:T(8,128)S(1)} %broadcast_in_dim.137), channel_id=1, replica_groups=mesh['row'=8,'col'=16] {'col'}, dimensions={1} | all-to-all | bytes 917504 | tf_op jit(solution)/shard_map/all_to_all | solution.py:15
  337.2 11.5 %all_to_all.258 = f32[56,16,128]{2,0,1:T(8,128)S(1)} all-to-all(f32[56,16,128]{2,0,1:T(8,128)S(1)} %copy_bitcast_fusion.24), channel_id=1, replica_groups=mesh['row'=8,'col'=16] {'col'}, dimensions={1} | all-to-all | bytes 917504 | tf_op jit(solution)/shard_map/all_to_all | solution.py:13
  360.2 14.7 %all_to_all.260 = f32[32,8,256]{2,0,1:T(8,128)S(1)} all-to-all(f32[32,8,256]{2,0,1:T(8,128)S(1)} %bitcast.781), channel_id=1, replica_groups=mesh['row'=8,'col'=16] {'row'}, dimensions={1} | all-to-all | bytes 524288 | tf_op jit(solution)/shard_map/all_to_all | solution.py:13
  385.9 12.2 %all_to_all.262 = f32[56,16,128]{2,0,1:T(8,128)S(1)} all-to-all(f32[56,16,128]{2,0,1:T(8,128)S(1)} %copy_bitcast_fusion.23), channel_id=1, replica_groups=mesh['row'=8,'col'=16] {'col'}, dimensions={1} | all-to-all | bytes 917504 | tf_op jit(solution)/shard_map/all_to_all | solution.py:13
  398.2 11.9 %all_to_all.263 = f32[56,16,128]{2,0,1:T(8,128)S(1)} all-to-all(f32[56,16,128]{2,0,1:T(8,128)S(1)} %broadcast_in_dim.274), channel_id=1, replica_groups=mesh['row'=8,'col'=16] {'col'}, dimensions={1} | all-to-all | bytes 917504 | tf_op jit(solution)/shard_map/all_to_all | solution.py:15
  432.0 11.5 %all_to_all.264 = f32[56,16,128]{2,0,1:T(8,128)S(1)} all-to-all(f32[56,16,128]{2,0,1:T(8,128)S(1)} %copy_bitcast_fusion.22), channel_id=1, replica_groups=mesh['row'=8,'col'=16] {'col'}, dimensions={1} | all-to-all | bytes 917504 | tf_op jit(solution)/shard_map/all_to_all | solution.py:13
  454.9 14.7 %all_to_all.266 = f32[32,8,256]{2,0,1:T(8,128)S(1)} all-to-all(f32[32,8,256]{2,0,1:T(8,128)S(1)} %bitcast.782), channel_id=1, replica_groups=mesh['row'=8,'col'=16] {'row'}, dimensions={1} | all-to-all | bytes 524288 | tf_op jit(solution)/shard_map/all_to_all | solution.py:13
  480.6 12.4 %all_to_all.268 = f32[56,16,128]{2,0,1:T(8,128)S(1)} all-to-all(f32[56,16,128]{2,0,1:T(8,128)S(1)} %copy_bitcast_fusion.21), channel_id=1, replica_groups=mesh['row'=8,'col'=16] {'col'}, dimensions={1} | all-to-all | bytes 917504 | tf_op jit(solution)/shard_map/all_to_all | solution.py:13
  493.1 12.0 %all_to_all.269 = f32[56,16,128]{2,0,1:T(8,128)S(1)} all-to-all(f32[56,16,128]{2,0,1:T(8,128)S(1)} %broadcast_in_dim.277), channel_id=1, replica_groups=mesh['row'=8,'col'=16] {'col'}, dimensions={1} | all-to-all | bytes 917504 | tf_op jit(solution)/shard_map/all_to_all | solution.py:15
  528.3 11.5 %all_to_all.270 = f32[56,16,128]{2,0,1:T(8,128)S(1)} all-to-all(f32[56,16,128]{2,0,1:T(8,128)S(1)} %copy_bitcast_fusion.20), channel_id=1, replica_groups=mesh['row'=8,'col'=16] {'col'}, dimensions={1} | all-to-all | bytes 917504 | tf_op jit(solution)/shard_map/all_to_all | solution.py:13
  552.1 14.7 %all_to_all.272 = f32[32,8,256]{2,0,1:T(8,128)S(1)} all-to-all(f32[32,8,256]{2,0,1:T(8,128)S(1)} %bitcast.783), channel_id=1, replica_groups=mesh['row'=8,'col'=16] {'row'}, dimensions={1} | all-to-all | bytes 524288 | tf_op jit(solution)/shard_map/all_to_all | solution.py:13
  577.8 12.2 %all_to_all.274 = f32[56,16,128]{2,0,1:T(8,128)S(1)} all-to-all(f32[56,16,128]{2,0,1:T(8,128)S(1)} %copy_bitcast_fusion.19), channel_id=1, replica_groups=mesh['row'=8,'col'=16] {'col'}, dimensions={1} | all-to-all | bytes 917504 | tf_op jit(solution)/shard_map/all_to_all | solution.py:13
  590.1 12.0 %all_to_all.275 = f32[56,16,128]{2,0,1:T(8,128)S(1)} all-to-all(f32[56,16,128]{2,0,1:T(8,128)S(1)} %broadcast_in_dim.280), channel_id=1, replica_groups=mesh['row'=8,'col'=16] {'col'}, dimensions={1} | all-to-all | bytes 917504 | tf_op jit(solution)/shard_map/all_to_all | solution.py:15
  624.6 11.5 %all_to_all.276 = f32[56,16,128]{2,0,1:T(8,128)S(1)} all-to-all(f32[56,16,128]{2,0,1:T(8,128)S(1)} %copy_bitcast_fusion.18), channel_id=1, replica_groups=mesh['row'=8,'col'=16] {'col'}, dimensions={1} | all-to-all | bytes 917504 | tf_op jit(solution)/shard_map/all_to_all | solution.py:13
  648.5 14.7 %all_to_all.278 = f32[32,8,256]{2,0,1:T(8,128)S(1)} all-to-all(f32[32,8,256]{2,0,1:T(8,128)S(1)} %bitcast.784), channel_id=1, replica_groups=mesh['row'=8,'col'=16] {'row'}, dimensions={1} | all-to-all | bytes 524288 | tf_op jit(solution)/shard_map/all_to_all | solution.py:13
  674.2 12.4 %all_to_all.280 = f32[56,16,128]{2,0,1:T(8,128)S(1)} all-to-all(f32[56,16,128]{2,0,1:T(8,128)S(1)} %copy_bitcast_fusion.17), channel_id=1, replica_groups=mesh['row'=8,'col'=16] {'col'}, dimensions={1} | all-to-all | bytes 917504 | tf_op jit(solution)/shard_map/all_to_all | solution.py:13
  686.6 12.2 %all_to_all.281 = f32[56,16,128]{2,0,1:T(8,128)S(1)} all-to-all(f32[56,16,128]{2,0,1:T(8,128)S(1)} %broadcast_in_dim.283), channel_id=1, replica_groups=mesh['row'=8,'col'=16] {'col'}, dimensions={1} | all-to-all | bytes 917504 | tf_op jit(solution)/shard_map/all_to_all | solution.py:15
  721.3 11.5 %all_to_all.282 = f32[56,16,128]{2,0,1:T(8,128)S(1)} all-to-all(f32[56,16,128]{2,0,1:T(8,128)S(1)} %copy_bitcast_fusion.16), channel_id=1, replica_groups=mesh['row'=8,'col'=16] {'col'}, dimensions={1} | all-to-all | bytes 917504 | tf_op jit(solution)/shard_map/all_to_all | solution.py:13
  744.3 14.7 %all_to_all.284 = f32[32,8,256]{2,0,1:T(8,128)S(1)} all-to-all(f32[32,8,256]{2,0,1:T(8,128)S(1)} %bitcast.785), channel_id=1, replica_groups=mesh['row'=8,'col'=16] {'row'}, dimensions={1} | all-to-all | bytes 524288 | tf_op jit(solution)/shard_map/all_to_all | solution.py:13
  (279 shorter events, 355.8 us)
Async XLA Ops:
  0.6 47.0 %copy-start.1 = (f32[24,2048]{1,0:T(8,128)S(1)}, f32[24,2048]{1,0:T(8,128)}, u32[]{:S(2)}) copy-start(f32[24,2048]{1,0:T(8,128)} %param.52) | copy-start | bytes 589828
  0.6 49.4 %copy-start.2 = (f32[2048]{0:T(1024)S(1)}, f32[2048]{0:T(1024)}, u32[]{:S(2)}) copy-start(f32[2048]{0:T(1024)} %param.53) | copy-start | bytes 24580
  23.5 12.6 %all-to-all-start.1 = ((f32[56,16,128]{2,0,1:T(8,128)}), f32[56,16,128]{2,0,1:T(8,128)S(1)}, u32[]{:S(2)}, u32[]{:S(2)}) async-start(f32[56,16,128]{2,0,1:T(8,128)} %broadcast_in_dim.127), calls=%async_computation.1 | async-start | bytes 917504 | tf_op jit(solution)/shard_map/all_to_all | solution.py:15
  36.1 11.4 %copy-start = (bf16[1,1,2,1,2048,2048]{5,4,3,2,1,0:T(8,128)(2,1)S(1)}, bf16[1,1,2,1,2048,2048]{5,4,3,2,1,0:T(8,128)(2,1)}, u32[]{:S(2)}) copy-start(bf16[1,1,2,1,2048,2048]{5,4,3,2,1,0:T(8,128)(2,1)} %param.55) | copy-start | bytes 50331652
  91.0 10.8 %all-to-all-start.5 = ((f32[32,8,256]{2,0,1:T(8,128)}), f32[32,8,256]{2,0,1:T(8,128)S(1)}, u32[]{:S(2)}, u32[]{:S(2)}) async-start(f32[32,8,256]{2,0,1:T(8,128)} %broadcast_in_dim.130), calls=%async_computation.5 | async-start | bytes 524288 | tf_op jit(solution)/shard_map/all_to_all | solution.py:15
  219.8 0.8 copy-start.14
  314.8 0.8 copy-start.12
  337.2 88.9 %copy-start.7 = (f32[24,2048]{1,0:T(8,128)}, f32[24,2048]{1,0:T(8,128)S(1)}, u32[]{:S(2)}) copy-start(f32[24,2048]{1,0:T(8,128)S(1)} %get-tuple-element.449) | copy-start | bytes 589828
  410.1 16.0 %copy-start.15 = (f32[56,2048]{1,0:T(8,128)}, f32[56,2048]{1,0:T(8,128)S(1)}, u32[]{:S(2)}) copy-start(f32[56,2048]{1,0:T(8,128)S(1)} %copy_bitcast_fusion.7) | copy-start | bytes 1376260
  410.9 21.0 %copy-start.3 = (f32[16,3,8,128]{3,2,1,0:T(8,128)}, f32[16,3,8,128]{3,2,1,0:T(8,128)S(1)}, u32[]{:S(2)}) copy-start(f32[16,3,8,128]{3,2,1,0:T(8,128)S(1)} %get-tuple-element.395) | copy-start | bytes 589828
  411.0 21.0 %copy-start.5 = (f32[16,3,8,128]{3,2,1,0:T(8,128)}, f32[16,3,8,128]{3,2,1,0:T(8,128)S(1)}, u32[]{:S(2)}) copy-start(f32[16,3,8,128]{3,2,1,0:T(8,128)S(1)} %get-tuple-element.396) | copy-start | bytes 589828
  480.6 41.8 %copy-start.4 = (f32[16,3,8,128]{3,2,1,0:T(8,128)S(1)}, f32[16,3,8,128]{3,2,1,0:T(8,128)}, u32[]{:S(2)}) copy-start(f32[16,3,8,128]{3,2,1,0:T(8,128)} %copy-done.3) | copy-start | bytes 589828
  480.6 41.8 %copy-start.6 = (f32[16,3,8,128]{3,2,1,0:T(8,128)S(1)}, f32[16,3,8,128]{3,2,1,0:T(8,128)}, u32[]{:S(2)}) copy-start(f32[16,3,8,128]{3,2,1,0:T(8,128)} %copy-done.5) | copy-start | bytes 589828
  505.1 0.8 copy-start.13
  528.2 90.6 %copy-start.8 = (f32[24,2048]{1,0:T(8,128)}, f32[24,2048]{1,0:T(8,128)S(1)}, u32[]{:S(2)}) copy-start(f32[24,2048]{1,0:T(8,128)S(1)} %get-tuple-element.326) | copy-start | bytes 589828
  528.2 90.6 %copy-start.10 = (f32[24,2048]{1,0:T(8,128)}, f32[24,2048]{1,0:T(8,128)S(1)}, u32[]{:S(2)}) copy-start(f32[24,2048]{1,0:T(8,128)S(1)} %get-tuple-element.447) | copy-start | bytes 589828
  602.2 0.8 copy-start.16
  674.1 41.3 %copy-start.9 = (f32[24,2048]{1,0:T(8,128)S(1)}, f32[24,2048]{1,0:T(8,128)}, u32[]{:S(2)}) copy-start(f32[24,2048]{1,0:T(8,128)} %copy-done.8) | copy-start | bytes 589828
  686.6 28.9 %copy-start.11 = (f32[24,2048]{1,0:T(8,128)S(1)}, f32[24,2048]{1,0:T(8,128)}, u32[]{:S(2)}) copy-start(f32[24,2048]{1,0:T(8,128)} %copy-done.10) | copy-start | bytes 589828
  698.8 0.8 copy-start.17

commit v2 on v1

--- a/solution.py
+++ b/solution.py
@@ -1,6 +1,8 @@
 import jax
 import jax.numpy as jnp
 from jax import lax
+from jax.experimental import pallas as pl
+from jax.experimental.pallas import tpu as pltpu
 from jax.sharding import PartitionSpec as P
 
 ITERS = 8
@@ -16,6 +18,41 @@
     return z.reshape(rows, width)
 
 
+def products_kernel(vbc_ref, vbi_ref, k_ref, fwd_ref, m_ref):
+    @pl.when((pl.program_id(0) == 0) & (pl.program_id(1) == 0))
+    def _():
+        m_ref[...] = jnp.zeros_like(m_ref)
+
+    tile = k_ref[...]
+    fwd_ref[...] = lax.dot_general(
+        vbc_ref[...], tile, (((1,), (1,)), ((), ())), preferred_element_type=jnp.float32
+    )
+    m_ref[...] += jnp.dot(vbi_ref[...], tile, preferred_element_type=jnp.float32)
+
+
+def block_products(vbc, vbi, blocks, tile=512):
+    nb, _, order, _ = blocks.shape
+    vecs = vbc.shape[0]
+    return pl.pallas_call(
+        products_kernel,
+        grid=(nb, order // tile),
+        in_specs=[
+            pl.BlockSpec((vecs, order), lambda k, i: (0, 0)),
+            pl.BlockSpec((None, vecs, tile), lambda k, i: (k, 0, i)),
+            pl.BlockSpec((None, None, tile, order), lambda k, i: (k, 0, i, 0)),
+        ],
+        out_specs=[
+            pl.BlockSpec((None, vecs, tile), lambda k, i: (k, 0, i)),
+            pl.BlockSpec((vecs, order), lambda k, i: (0, 0)),
+        ],
+        out_shape=[
+            jax.ShapeDtypeStruct((nb, vecs, order), jnp.float32),
+            jax.ShapeDtypeStruct((vecs, order), jnp.float32),
+        ],
+        compiler_params=pltpu.CompilerParams(dimension_semantics=("arbitrary", "arbitrary")),
+    )(vbc, vbi, blocks)
+
+
 def pack(blocks, scalars):
     width = blocks[0].shape[1]
     tail = jnp.zeros((PAD, width), jnp.float32).at[0, : scalars.shape[0]].set(scalars)
@@ -25,6 +62,7 @@
 def make_on_device(n_row, n_col):
     def on_device(rhs, noise_var, block_rows, kernel_blocks):
         blocks = kernel_blocks[0, 0]
+        assert blocks.shape[1] == 1
         rows = block_rows[0]
         nb = rows.shape[0]
         vecs, width = rhs.shape
@@ -45,13 +83,9 @@
         dir_rows, norm_now = fetch(rhs)
         for step in range(ITERS):
             vb = direction.astype(jnp.bfloat16)
-            forward = []
-            mirrored = jnp.zeros((vecs, width), jnp.float32)
-            for k in range(nb):
-                f = lax.dot_general(vb, blocks[k, 0], (((1,), (1,)), ((), ())), preferred_element_type=jnp.float32)
-                forward.append(jnp.where(used[k], f, 0.0))
-                m = jnp.dot(dir_rows[k].astype(jnp.bfloat16), blocks[k, 0], preferred_element_type=jnp.float32)
-                mirrored = mirrored + jnp.where(used[k], m, 0.0)
+            vbi = jnp.stack([jnp.where(used[k], dir_rows[k], 0.0) for k in range(nb)]).astype(jnp.bfloat16)
+            fwd, mirrored = block_products(vb, vbi, blocks)
+            forward = [jnp.where(used[k], fwd[k], 0.0) for k in range(nb)]
             part = jnp.sum(direction * mirrored, axis=1)
             part = part + jnp.where(first_row, jnp.sum(direction * (noise * direction), axis=1), 0.0)
             for k in range(nb):

time: 781 us -> 767 us (0.982)
  matrix products: 162 us -> 0 us
  Pallas kernels: 0 us -> 103 us
  other arithmetic: 15.9 us -> 60.1 us
  local copies, waits for them, and re-layouts: 7.79 us -> 15.7 us
    dot_general x32 -> x0, matrix products: 162 us -> none  [the longest x16 88.8 us: on_device(): lax.dot_general(vb, blocks[k, 0], (((1,), (1,)), ((), ())), preferred_ele...]
    pallas_call x0 -> x8, Pallas kernels: none -> 103 us  [block_products(): pl.pallas_call(products_kernel, grid=(nb, order // tile), in_specs=[pl.Bl...]
    another operation x0 -> x16, other arithmetic: none -> 13.3 us
    reduce_sum x0 -> x16, other arithmetic: none -> 11.6 us  [the longest x8 8.58 us: on_device(): jnp.sum(direction * (noise * direction), axis=1)]
    slice x0 -> x40, local copies, waits for them, and re-layouts: none -> 9.62 us  [fetch(): out[k * vecs:(k + 1) * vecs]]
    select_n x0 -> x8, other arithmetic: none -> 8.64 us  [on_device(): forward = [jnp.where(used[k], fwd[k], 0.0) for k in range(nb)]]
where the time goes in v2:
time: 767 us; the launch traced here: 762 us
  blocking collectives  556 us (72%)
  Pallas kernels  103 us (13%)
  other arithmetic  60.1 us (8%)
  local copies, waits for them, and re-layouts  15.7 us (2%)
  waiting for transfers between devices  14.2 us (2%)
  starting transfers between devices  7.91 us (1%)
    all_to_all x24, blocking collectives, all_reduce(): y = lax.all_to_all(x.reshape(rows, n, w), axis, 1, 1, tiled=True)  315 us
    all_to_all x22, blocking collectives, all_reduce(): lax.all_to_all(jnp.broadcast_to(part[:, None, :], (rows, n, w)), axis, 1,...  242 us
    pallas_call x8, Pallas kernels, block_products(): pl.pallas_call(products_kernel, grid=(nb, order // tile), in_specs=[pl.Bl...  103 us
  transfers between devices with their start and end apart: 2, of which 2 were waited for; matrix products, arithmetic and copies ran while one was open for 0% of the time, Pallas kernels for 0%

profile of v2, /device:TPU:1, one launch (start us, length us, event | category | flops | bytes accessed | tf_op | source)
XLA Modules:
  0.0 762.1 jit_solution(6509465378351356158)
XLA Ops:
  5.1 18.3 %all_to_all.240 = f32[56,16,128]{2,0,1:T(8,128)S(1)} all-to-all(f32[56,16,128]{2,0,1:T(8,128)S(1)} %copy_bitcast_fusion.31), channel_id=1, replica_groups=mesh['row'=8,'col'=16] {'col'}, dimensions={1} | all-to-all | bytes 917504 | tf_op jit(solution)/shard_map/all_to_all | solution.py:15
  37.8 12.9 %shard_map.59 = (f32[2,24,2048]{2,1,0:T(8,128)}, f32[24,2048]{1,0:T(8,128)}) custom-call(bf16[24,2048]{1,0:T(8,128)(2,1)} %get-tuple-element.487.vbc_ref, bf16[2,24,2048]{2,1,0:T(8,128)(2,1)} %pad_maximum_fusion.vbi_ref, bf16[2,1,2048,2048]{3,2,1,0:T(8,128)(2,1)} %bitcast.465), custom_call_target="tpu_custom_call" | custom-call | tf_op jit(solution)/shard_map/pallas_call | solution.py:36
  76.9 16.1 %all_to_all.243 = f32[32,8,256]{2,0,1:T(8,128)S(1)} all-to-all(f32[32,8,256]{2,0,1:T(8,128)S(1)} %bitcast.489), channel_id=1, replica_groups=mesh['row'=8,'col'=16] {'row'}, dimensions={1} | all-to-all | bytes 524288 | tf_op jit(solution)/shard_map/all_to_all | solution.py:15
  105.0 12.2 %all_to_all.244 = f32[56,16,128]{2,0,1:T(8,128)S(1)} all-to-all(f32[56,16,128]{2,0,1:T(8,128)S(1)} %copy_bitcast_fusion.29), channel_id=1, replica_groups=mesh['row'=8,'col'=16] {'col'}, dimensions={1} | all-to-all | bytes 917504 | tf_op jit(solution)/shard_map/all_to_all | solution.py:15
  117.3 11.8 %all_to_all.245 = f32[56,16,128]{2,0,1:T(8,128)S(1)} all-to-all(f32[56,16,128]{2,0,1:T(8,128)S(1)} %broadcast_in_dim.134), channel_id=1, replica_groups=mesh['row'=8,'col'=16] {'col'}, dimensions={1} | all-to-all | bytes 917504 | tf_op jit(solution)/shard_map/all_to_all | solution.py:17
  131.0 12.9 %shard_map.60 = (f32[2,24,2048]{2,1,0:T(8,128)}, f32[24,2048]{1,0:T(8,128)}) custom-call(bf16[24,2048]{1,0:T(8,128)(2,1)} %get-tuple-element.396.vbc_ref, bf16[2,24,2048]{2,1,0:T(8,128)(2,1)} %pad_maximum_fusion.1.vbi_ref, bf16[2,1,2048,2048]{3,2,1,0:T(8,128)(2,1)} %bitcast.466), custom_call_target="tpu_custom_call" | custom-call | tf_op jit(solution)/shard_map/pallas_call | solution.py:36
  170.3 14.7 %all_to_all.248 = f32[32,8,256]{2,0,1:T(8,128)S(1)} all-to-all(f32[32,8,256]{2,0,1:T(8,128)S(1)} %bitcast.490), channel_id=1, replica_groups=mesh['row'=8,'col'=16] {'row'}, dimensions={1} | all-to-all | bytes 524288 | tf_op jit(solution)/shard_map/all_to_all | solution.py:15
  195.4 12.2 %all_to_all.250 = f32[56,16,128]{2,0,1:T(8,128)S(1)} all-to-all(f32[56,16,128]{2,0,1:T(8,128)S(1)} %copy_bitcast_fusion.27), channel_id=1, replica_groups=mesh['row'=8,'col'=16] {'col'}, dimensions={1} | all-to-all | bytes 917504 | tf_op jit(solution)/shard_map/all_to_all | solution.py:15
  207.7 11.8 %all_to_all.251 = f32[56,16,128]{2,0,1:T(8,128)S(1)} all-to-all(f32[56,16,128]{2,0,1:T(8,128)S(1)} %broadcast_in_dim.137), channel_id=1, replica_groups=mesh['row'=8,'col'=16] {'col'}, dimensions={1} | all-to-all | bytes 917504 | tf_op jit(solution)/shard_map/all_to_all | solution.py:17
  224.3 12.9 %shard_map.61 = (f32[2,24,2048]{2,1,0:T(8,128)}, f32[24,2048]{1,0:T(8,128)}) custom-call(bf16[24,2048]{1,0:T(8,128)(2,1)} %get-tuple-element.392.vbc_ref, bf16[2,24,2048]{2,1,0:T(8,128)(2,1)} %pad_maximum_fusion.2.vbi_ref, bf16[2,1,2048,2048]{3,2,1,0:T(8,128)(2,1)} %bitcast.467), custom_call_target="tpu_custom_call" | custom-call | tf_op jit(solution)/shard_map/pallas_call | solution.py:36
  263.7 14.7 %all_to_all.254 = f32[32,8,256]{2,0,1:T(8,128)S(1)} all-to-all(f32[32,8,256]{2,0,1:T(8,128)S(1)} %bitcast.491), channel_id=1, replica_groups=mesh['row'=8,'col'=16] {'row'}, dimensions={1} | all-to-all | bytes 524288 | tf_op jit(solution)/shard_map/all_to_all | solution.py:15
  289.9 12.2 %all_to_all.256 = f32[56,16,128]{2,0,1:T(8,128)S(1)} all-to-all(f32[56,16,128]{2,0,1:T(8,128)S(1)} %copy_bitcast_fusion.25), channel_id=1, replica_groups=mesh['row'=8,'col'=16] {'col'}, dimensions={1} | all-to-all | bytes 917504 | tf_op jit(solution)/shard_map/all_to_all | solution.py:15
  302.2 11.8 %all_to_all.257 = f32[56,16,128]{2,0,1:T(8,128)S(1)} all-to-all(f32[56,16,128]{2,0,1:T(8,128)S(1)} %broadcast_in_dim.274), channel_id=1, replica_groups=mesh['row'=8,'col'=16] {'col'}, dimensions={1} | all-to-all | bytes 917504 | tf_op jit(solution)/shard_map/all_to_all | solution.py:17
  317.4 13.0 %shard_map.62 = (f32[2,24,2048]{2,1,0:T(8,128)}, f32[24,2048]{1,0:T(8,128)}) custom-call(bf16[24,2048]{1,0:T(8,128)(2,1)} %get-tuple-element.380.vbc_ref, bf16[2,24,2048]{2,1,0:T(8,128)(2,1)} %pad_maximum_fusion.3.vbi_ref, bf16[2,1,2048,2048]{3,2,1,0:T(8,128)(2,1)} %bitcast.468), custom_call_target="tpu_custom_call" | custom-call | tf_op jit(solution)/shard_map/pallas_call | solution.py:36
  332.9 11.5 %all_to_all.258 = f32[56,16,128]{2,0,1:T(8,128)S(1)} all-to-all(f32[56,16,128]{2,0,1:T(8,128)S(1)} %copy_bitcast_fusion.24), channel_id=1, replica_groups=mesh['row'=8,'col'=16] {'col'}, dimensions={1} | all-to-all | bytes 917504 | tf_op jit(solution)/shard_map/all_to_all | solution.py:15
  356.8 14.7 %all_to_all.260 = f32[32,8,256]{2,0,1:T(8,128)S(1)} all-to-all(f32[32,8,256]{2,0,1:T(8,128)S(1)} %bitcast.492), channel_id=1, replica_groups=mesh['row'=8,'col'=16] {'row'}, dimensions={1} | all-to-all | bytes 524288 | tf_op jit(solution)/shard_map/all_to_all | solution.py:15
  382.2 12.2 %all_to_all.262 = f32[56,16,128]{2,0,1:T(8,128)S(1)} all-to-all(f32[56,16,128]{2,0,1:T(8,128)S(1)} %copy_bitcast_fusion.23), channel_id=1, replica_groups=mesh['row'=8,'col'=16] {'col'}, dimensions={1} | all-to-all | bytes 917504 | tf_op jit(solution)/shard_map/all_to_all | solution.py:15
  394.5 11.8 %all_to_all.263 = f32[56,16,128]{2,0,1:T(8,128)S(1)} all-to-all(f32[56,16,128]{2,0,1:T(8,128)S(1)} %broadcast_in_dim.277), channel_id=1, replica_groups=mesh['row'=8,'col'=16] {'col'}, dimensions={1} | all-to-all | bytes 917504 | tf_op jit(solution)/shard_map/all_to_all | solution.py:17
  411.3 12.9 %shard_map.63 = (f32[2,24,2048]{2,1,0:T(8,128)}, f32[24,2048]{1,0:T(8,128)}) custom-call(bf16[24,2048]{1,0:T(8,128)(2,1)} %get-tuple-element.376.vbc_ref, bf16[2,24,2048]{2,1,0:T(8,128)(2,1)} %pad_maximum_fusion.4.vbi_ref, bf16[2,1,2048,2048]{3,2,1,0:T(8,128)(2,1)} %bitcast.469), custom_call_target="tpu_custom_call" | custom-call | tf_op jit(solution)/shard_map/pallas_call | solution.py:36
  450.7 14.7 %all_to_all.266 = f32[32,8,256]{2,0,1:T(8,128)S(1)} all-to-all(f32[32,8,256]{2,0,1:T(8,128)S(1)} %bitcast.493), channel_id=1, replica_groups=mesh['row'=8,'col'=16] {'row'}, dimensions={1} | all-to-all | bytes 524288 | tf_op jit(solution)/shard_map/all_to_all | solution.py:15
  476.4 12.2 %all_to_all.268 = f32[56,16,128]{2,0,1:T(8,128)S(1)} all-to-all(f32[56,16,128]{2,0,1:T(8,128)S(1)} %copy_bitcast_fusion.21), channel_id=1, replica_groups=mesh['row'=8,'col'=16] {'col'}, dimensions={1} | all-to-all | bytes 917504 | tf_op jit(solution)/shard_map/all_to_all | solution.py:15
  488.7 11.8 %all_to_all.269 = f32[56,16,128]{2,0,1:T(8,128)S(1)} all-to-all(f32[56,16,128]{2,0,1:T(8,128)S(1)} %broadcast_in_dim.280), channel_id=1, replica_groups=mesh['row'=8,'col'=16] {'col'}, dimensions={1} | all-to-all | bytes 917504 | tf_op jit(solution)/shard_map/all_to_all | solution.py:17
  503.0 12.9 %shard_map.64 = (f32[2,24,2048]{2,1,0:T(8,128)}, f32[24,2048]{1,0:T(8,128)}) custom-call(bf16[24,2048]{1,0:T(8,128)(2,1)} %get-tuple-element.364.vbc_ref, bf16[2,24,2048]{2,1,0:T(8,128)(2,1)} %pad_maximum_fusion.5.vbi_ref, bf16[2,1,2048,2048]{3,2,1,0:T(8,128)(2,1)} %bitcast.470), custom_call_target="tpu_custom_call" | custom-call | tf_op jit(solution)/shard_map/pallas_call | solution.py:36
  542.3 14.7 %all_to_all.272 = f32[32,8,256]{2,0,1:T(8,128)S(1)} all-to-all(f32[32,8,256]{2,0,1:T(8,128)S(1)} %bitcast.494), channel_id=1, replica_groups=mesh['row'=8,'col'=16] {'row'}, dimensions={1} | all-to-all | bytes 524288 | tf_op jit(solution)/shard_map/all_to_all | solution.py:15
  568.0 12.2 %all_to_all.274 = f32[56,16,128]{2,0,1:T(8,128)S(1)} all-to-all(f32[56,16,128]{2,0,1:T(8,128)S(1)} %copy_bitcast_fusion.19), channel_id=1, replica_groups=mesh['row'=8,'col'=16] {'col'}, dimensions={1} | all-to-all | bytes 917504 | tf_op jit(solution)/shard_map/all_to_all | solution.py:15
  580.3 11.8 %all_to_all.275 = f32[56,16,128]{2,0,1:T(8,128)S(1)} all-to-all(f32[56,16,128]{2,0,1:T(8,128)S(1)} %broadcast_in_dim.283), channel_id=1, replica_groups=mesh['row'=8,'col'=16] {'col'}, dimensions={1} | all-to-all | bytes 917504 | tf_op jit(solution)/shard_map/all_to_all | solution.py:17
  602.7 12.9 %shard_map.65 = (f32[2,24,2048]{2,1,0:T(8,128)}, f32[24,2048]{1,0:T(8,128)}) custom-call(bf16[24,2048]{1,0:T(8,128)(2,1)} %get-tuple-element.360.vbc_ref, bf16[2,24,2048]{2,1,0:T(8,128)(2,1)} %pad_maximum_fusion.6.vbi_ref, bf16[2,1,2048,2048]{3,2,1,0:T(8,128)(2,1)} %bitcast.471), custom_call_target="tpu_custom_call" | custom-call | tf_op jit(solution)/shard_map/pallas_call | solution.py:36
  642.9 14.8 %all_to_all.278 = f32[32,8,256]{2,0,1:T(8,128)S(1)} all-to-all(f32[32,8,256]{2,0,1:T(8,128)S(1)} %bitcast.495), channel_id=1, replica_groups=mesh['row'=8,'col'=16] {'row'}, dimensions={1} | all-to-all | bytes 524288 | tf_op jit(solution)/shard_map/all_to_all | solution.py:15
  668.7 12.2 %all_to_all.280 = f32[56,16,128]{2,0,1:T(8,128)S(1)} all-to-all(f32[56,16,128]{2,0,1:T(8,128)S(1)} %copy_bitcast_fusion.17), channel_id=1, replica_groups=mesh['row'=8,'col'=16] {'col'}, dimensions={1} | all-to-all | bytes 917504 | tf_op jit(solution)/shard_map/all_to_all | solution.py:15
  681.0 11.8 %all_to_all.281 = f32[56,16,128]{2,0,1:T(8,128)S(1)} all-to-all(f32[56,16,128]{2,0,1:T(8,128)S(1)} %broadcast_in_dim.286), channel_id=1, replica_groups=mesh['row'=8,'col'=16] {'col'}, dimensions={1} | all-to-all | bytes 917504 | tf_op jit(solution)/shard_map/all_to_all | solution.py:17
  696.3 12.9 %shard_map.66 = (f32[2,24,2048]{2,1,0:T(8,128)}, f32[24,2048]{1,0:T(8,128)}) custom-call(bf16[24,2048]{1,0:T(8,128)(2,1)} %get-tuple-element.348.vbc_ref, bf16[2,24,2048]{2,1,0:T(8,128)(2,1)} %pad_maximum_fusion.7.vbi_ref, bf16[2,1,2048,2048]{3,2,1,0:T(8,128)(2,1)} %bitcast.472), custom_call_target="tpu_custom_call" | custom-call | tf_op jit(solution)/shard_map/pallas_call | solution.py:36
  735.7 14.7 %all_to_all.284 = f32[32,8,256]{2,0,1:T(8,128)S(1)} all-to-all(f32[32,8,256]{2,0,1:T(8,128)S(1)} %bitcast.496), channel_id=1, replica_groups=mesh['row'=8,'col'=16] {'row'}, dimensions={1} | all-to-all | bytes 524288 | tf_op jit(solution)/shard_map/all_to_all | solution.py:15
  (353 shorter events, 337.0 us)
Async XLA Ops:
  0.6 51.3 %copy-start = (f32[24,2048]{1,0:T(8,128)S(1)}, f32[24,2048]{1,0:T(8,128)}, u32[]{:S(2)}) copy-start(f32[24,2048]{1,0:T(8,128)} %param.52) | copy-start | bytes 589828
  0.6 51.3 %copy-start.1 = (f32[2048]{0:T(1024)S(1)}, f32[2048]{0:T(1024)}, u32[]{:S(2)}) copy-start(f32[2048]{0:T(1024)} %param.53) | copy-start | bytes 24580
  24.3 12.6 %all-to-all-start.1 = ((f32[56,16,128]{2,0,1:T(8,128)}), f32[56,16,128]{2,0,1:T(8,128)S(1)}, u32[]{:S(2)}, u32[]{:S(2)}) async-start(f32[56,16,128]{2,0,1:T(8,128)} %broadcast_in_dim.129), calls=%async_computation.1 | async-start | bytes 917504 | tf_op jit(solution)/shard_map/all_to_all | solution.py:17
  93.8 10.8 %all-to-all-start.5 = ((f32[32,8,256]{2,0,1:T(8,128)}), f32[32,8,256]{2,0,1:T(8,128)S(1)}, u32[]{:S(2)}, u32[]{:S(2)}) async-start(f32[32,8,256]{2,0,1:T(8,128)} %broadcast_in_dim.133), calls=%async_computation.5 | async-start | bytes 524288 | tf_op jit(solution)/shard_map/all_to_all | solution.py:17
  129.1 65.9 %copy-start.12 = (f32[56,2048]{1,0:T(8,128)}, f32[56,2048]{1,0:T(8,128)S(1)}, u32[]{:S(2)}) copy-start(f32[56,2048]{1,0:T(8,128)S(1)} %copy_bitcast_fusion.13) | copy-start | bytes 1376260
  195.1 26.7 %copy-start.14 = (f32[24]{0:T(128)}, f32[24]{0:T(128)S(1)}, u32[]{:S(2)}) copy-start(f32[24]{0:T(128)S(1)} %fusion.129) | copy-start | bytes 292
  219.5 1.4 copy-start.9
  223.6 92.0 %copy-start.3 = (f32[1,24,2048]{2,1,0:T(8,128)}, f32[1,24,2048]{2,1,0:T(8,128)S(1)}, u32[]{:S(2)}) copy-start(f32[1,24,2048]{2,1,0:T(8,128)S(1)} %get-tuple-element.389) | copy-start | bytes 589828
  289.1 0.5 copy-start.16
  314.0 67.5 %copy-start.10 = (f32[56,2048]{1,0:T(8,128)}, f32[56,2048]{1,0:T(8,128)S(1)}, u32[]{:S(2)}) copy-start(f32[56,2048]{1,0:T(8,128)S(1)} %copy_bitcast_fusion.9) | copy-start | bytes 1376260
  317.4 91.9 %copy-start.4 = (f32[1,24,2048]{2,1,0:T(8,128)S(1)}, f32[1,24,2048]{2,1,0:T(8,128)}, u32[]{:S(2)}) copy-start(f32[1,24,2048]{2,1,0:T(8,128)} %copy-done.3) | copy-start | bytes 589828
  381.5 0.5 copy-start.18
  406.3 1.4 copy-start.7
  410.6 91.6 %copy-start.2 = (f32[1,24,2048]{2,1,0:T(8,128)}, f32[1,24,2048]{2,1,0:T(8,128)S(1)}, u32[]{:S(2)}) copy-start(f32[1,24,2048]{2,1,0:T(8,128)S(1)} %get-tuple-element.493) | copy-start | bytes 589828
  500.5 1.5 copy-start.11
  592.1 0.8 copy-start.8
  642.8 68.7 %copy-start.5 = (f32[24,16,128]{2,0,1:T(8,128)S(1)}, f32[24,16,128]{2,0,1:T(8,128)}, u32[]{:S(2)}) copy-start(f32[24,16,128]{2,0,1:T(8,128)} %get-tuple-element.353) | copy-start | bytes 589828
  642.8 68.7 %copy-start.6 = (f32[24,16,128]{2,0,1:T(8,128)S(1)}, f32[24,16,128]{2,0,1:T(8,128)}, u32[]{:S(2)}) copy-start(f32[24,16,128]{2,0,1:T(8,128)} %get-tuple-element.403) | copy-start | bytes 589828
  692.8 1.4 copy-start.13
  694.3 66.8 %copy-start.15 = (f32[24]{0:T(128)S(1)}, f32[24]{0:T(128)}, u32[]{:S(2)}) copy-start(f32[24]{0:T(128)} %copy-done.14) | copy-start | bytes 292
  694.3 66.8 %copy-start.17 = (f32[24]{0:T(128)S(1)}, f32[24]{0:T(128)}, u32[]{:S(2)}) copy-start(f32[24]{0:T(128)} %copy-done.16) | copy-start | bytes 292
  694.3 66.8 %copy-start.19 = (f32[24]{0:T(128)S(1)}, f32[24]{0:T(128)}, u32[]{:S(2)}) copy-start(f32[24]{0:T(128)} %copy-done.18) | copy-start | bytes 292

commit v3 on v2

--- a/solution.py
+++ b/solution.py
@@ -6,7 +6,7 @@
 from jax.sharding import PartitionSpec as P
 
 ITERS = 8
-PAD = 8
+PAD = 1
 
 
 def all_reduce(x, axis, n):

time: 767 us -> 802 us (1.046)
  other arithmetic: 60.1 us -> 75.8 us
  local copies, waits for them, and re-layouts: 15.7 us -> 25.6 us
    another operation x8 -> x33, other arithmetic: 7.62 us -> 23.4 us
where the time goes in v3:
time: 802 us; the launch traced here: 789 us
  blocking collectives  557 us (69%)
  Pallas kernels  103 us (13%)
  other arithmetic  75.8 us (9%)
  local copies, waits for them, and re-layouts  25.6 us (3%)
  waiting for transfers between devices  14 us (2%)
    all_to_all x24, blocking collectives, all_reduce(): y = lax.all_to_all(x.reshape(rows, n, w), axis, 1, 1, tiled=True)  314 us
    all_to_all x22, blocking collectives, all_reduce(): lax.all_to_all(jnp.broadcast_to(part[:, None, :], (rows, n, w)), axis, 1,...  242 us
    pallas_call x8, Pallas kernels, block_products(): pl.pallas_call(products_kernel, grid=(nb, order // tile), in_specs=[pl.Bl...  103 us
    another operation x33, other arithmetic  23.4 us
  transfers between devices with their start and end apart: 2, of which 2 were waited for; matrix products, arithmetic and copies ran while one was open for 0% of the time, Pallas kernels for 0%

profile of v3, /device:TPU:1, one launch (start us, length us, event | category | flops | bytes accessed | tf_op | source)
XLA Modules:
  0.0 789.3 jit_solution(522694198401091208)
XLA Ops:
  6.7 18.3 %all_to_all.240 = f32[49,16,128]{2,0,1:T(8,128)S(1)} all-to-all(f32[49,16,128]{2,0,1:T(8,128)S(1)} %copy.94), channel_id=1, replica_groups=mesh['row'=8,'col'=16] {'col'}, dimensions={1} | all-to-all | bytes 802816 | tf_op jit(solution)/shard_map/all_to_all | solution.py:15
  39.4 12.9 %shard_map.59 = (f32[2,24,2048]{2,1,0:T(8,128)}, f32[24,2048]{1,0:T(8,128)}) custom-call(bf16[24,2048]{1,0:T(8,128)(2,1)} %get-tuple-element.487.vbc_ref, bf16[2,24,2048]{2,1,0:T(8,128)(2,1)} %pad_maximum_fusion.vbi_ref, bf16[2,1,2048,2048]{3,2,1,0:T(8,128)(2,1)} %bitcast.409), custom_call_target="tpu_custom_call" | custom-call | tf_op jit(solution)/shard_map/pallas_call | solution.py:36
  80.5 16.1 %all_to_all.243 = f32[25,8,256]{2,0,1:T(8,128)S(1)} all-to-all(f32[25,8,256]{2,0,1:T(8,128)S(1)} %copy.104), channel_id=1, replica_groups=mesh['row'=8,'col'=16] {'row'}, dimensions={1} | all-to-all | bytes 409600 | tf_op jit(solution)/shard_map/all_to_all | solution.py:15
  109.7 12.2 %all_to_all.244 = f32[49,16,128]{2,0,1:T(8,128)S(1)} all-to-all(f32[49,16,128]{2,0,1:T(8,128)S(1)} %copy.107), channel_id=1, replica_groups=mesh['row'=8,'col'=16] {'col'}, dimensions={1} | all-to-all | bytes 802816 | tf_op jit(solution)/shard_map/all_to_all | solution.py:15
  122.0 11.8 %all_to_all.245 = f32[49,16,128]{2,0,1:T(8,128)S(1)} all-to-all(f32[49,16,128]{2,0,1:T(8,128)S(1)} %broadcast_in_dim.134), channel_id=1, replica_groups=mesh['row'=8,'col'=16] {'col'}, dimensions={1} | all-to-all | bytes 802816 | tf_op jit(solution)/shard_map/all_to_all | solution.py:17
  135.9 12.9 %shard_map.60 = (f32[2,24,2048]{2,1,0:T(8,128)}, f32[24,2048]{1,0:T(8,128)}) custom-call(bf16[24,2048]{1,0:T(8,128)(2,1)} %get-tuple-element.396.vbc_ref, bf16[2,24,2048]{2,1,0:T(8,128)(2,1)} %pad_maximum_fusion.1.vbi_ref, bf16[2,1,2048,2048]{3,2,1,0:T(8,128)(2,1)} %bitcast.410), custom_call_target="tpu_custom_call" | custom-call | tf_op jit(solution)/shard_map/pallas_call | solution.py:36
  177.2 14.7 %all_to_all.248 = f32[25,8,256]{2,0,1:T(8,128)S(1)} all-to-all(f32[25,8,256]{2,0,1:T(8,128)S(1)} %copy.117), channel_id=1, replica_groups=mesh['row'=8,'col'=16] {'row'}, dimensions={1} | all-to-all | bytes 409600 | tf_op jit(solution)/shard_map/all_to_all | solution.py:15
  203.3 12.2 %all_to_all.250 = f32[49,16,128]{2,0,1:T(8,128)S(1)} all-to-all(f32[49,16,128]{2,0,1:T(8,128)S(1)} %copy.120), channel_id=1, replica_groups=mesh['row'=8,'col'=16] {'col'}, dimensions={1} | all-to-all | bytes 802816 | tf_op jit(solution)/shard_map/all_to_all | solution.py:15
  215.6 11.9 %all_to_all.251 = f32[49,16,128]{2,0,1:T(8,128)S(1)} all-to-all(f32[49,16,128]{2,0,1:T(8,128)S(1)} %broadcast_in_dim.137), channel_id=1, replica_groups=mesh['row'=8,'col'=16] {'col'}, dimensions={1} | all-to-all | bytes 802816 | tf_op jit(solution)/shard_map/all_to_all | solution.py:17
  232.7 12.9 %shard_map.61 = (f32[2,24,2048]{2,1,0:T(8,128)}, f32[24,2048]{1,0:T(8,128)}) custom-call(bf16[24,2048]{1,0:T(8,128)(2,1)} %get-tuple-element.392.vbc_ref, bf16[2,24,2048]{2,1,0:T(8,128)(2,1)} %pad_maximum_fusion.2.vbi_ref, bf16[2,1,2048,2048]{3,2,1,0:T(8,128)(2,1)} %bitcast.411), custom_call_target="tpu_custom_call" | custom-call | tf_op jit(solution)/shard_map/pallas_call | solution.py:36
  249.1 11.5 %all_to_all.252 = f32[49,16,128]{2,0,1:T(8,128)S(1)} all-to-all(f32[49,16,128]{2,0,1:T(8,128)S(1)} %copy.126), channel_id=1, replica_groups=mesh['row'=8,'col'=16] {'col'}, dimensions={1} | all-to-all | bytes 802816 | tf_op jit(solution)/shard_map/all_to_all | solution.py:15
  274.0 14.7 %all_to_all.254 = f32[25,8,256]{2,0,1:T(8,128)S(1)} all-to-all(f32[25,8,256]{2,0,1:T(8,128)S(1)} %copy.130), channel_id=1, replica_groups=mesh['row'=8,'col'=16] {'row'}, dimensions={1} | all-to-all | bytes 409600 | tf_op jit(solution)/shard_map/all_to_all | solution.py:15
  300.8 12.2 %all_to_all.256 = f32[49,16,128]{2,0,1:T(8,128)S(1)} all-to-all(f32[49,16,128]{2,0,1:T(8,128)S(1)} %copy.133), channel_id=1, replica_groups=mesh['row'=8,'col'=16] {'col'}, dimensions={1} | all-to-all | bytes 802816 | tf_op jit(solution)/shard_map/all_to_all | solution.py:15
  313.1 11.8 %all_to_all.257 = f32[49,16,128]{2,0,1:T(8,128)S(1)} all-to-all(f32[49,16,128]{2,0,1:T(8,128)S(1)} %broadcast_in_dim.274), channel_id=1, replica_groups=mesh['row'=8,'col'=16] {'col'}, dimensions={1} | all-to-all | bytes 802816 | tf_op jit(solution)/shard_map/all_to_all | solution.py:17
  328.6 12.9 %shard_map.62 = (f32[2,24,2048]{2,1,0:T(8,128)}, f32[24,2048]{1,0:T(8,128)}) custom-call(bf16[24,2048]{1,0:T(8,128)(2,1)} %get-tuple-element.380.vbc_ref, bf16[2,24,2048]{2,1,0:T(8,128)(2,1)} %pad_maximum_fusion.3.vbi_ref, bf16[2,1,2048,2048]{3,2,1,0:T(8,128)(2,1)} %bitcast.412), custom_call_target="tpu_custom_call" | custom-call | tf_op jit(solution)/shard_map/pallas_call | solution.py:36
  369.9 14.7 %all_to_all.260 = f32[25,8,256]{2,0,1:T(8,128)S(1)} all-to-all(f32[25,8,256]{2,0,1:T(8,128)S(1)} %copy.143), channel_id=1, replica_groups=mesh['row'=8,'col'=16] {'row'}, dimensions={1} | all-to-all | bytes 409600 | tf_op jit(solution)/shard_map/all_to_all | solution.py:15
  396.4 12.2 %all_to_all.262 = f32[49,16,128]{2,0,1:T(8,128)S(1)} all-to-all(f32[49,16,128]{2,0,1:T(8,128)S(1)} %copy.146), channel_id=1, replica_groups=mesh['row'=8,'col'=16] {'col'}, dimensions={1} | all-to-all | bytes 802816 | tf_op jit(solution)/shard_map/all_to_all | solution.py:15
  408.7 12.0 %all_to_all.263 = f32[49,16,128]{2,0,1:T(8,128)S(1)} all-to-all(f32[49,16,128]{2,0,1:T(8,128)S(1)} %broadcast_in_dim.277), channel_id=1, replica_groups=mesh['row'=8,'col'=16] {'col'}, dimensions={1} | all-to-all | bytes 802816 | tf_op jit(solution)/shard_map/all_to_all | solution.py:17
  426.0 12.9 %shard_map.63 = (f32[2,24,2048]{2,1,0:T(8,128)}, f32[24,2048]{1,0:T(8,128)}) custom-call(bf16[24,2048]{1,0:T(8,128)(2,1)} %get-tuple-element.376.vbc_ref, bf16[2,24,2048]{2,1,0:T(8,128)(2,1)} %pad_maximum_fusion.4.vbi_ref, bf16[2,1,2048,2048]{3,2,1,0:T(8,128)(2,1)} %bitcast.413), custom_call_target="tpu_custom_call" | custom-call | tf_op jit(solution)/shard_map/pallas_call | solution.py:36
  467.3 14.7 %all_to_all.266 = f32[25,8,256]{2,0,1:T(8,128)S(1)} all-to-all(f32[25,8,256]{2,0,1:T(8,128)S(1)} %copy.156), channel_id=1, replica_groups=mesh['row'=8,'col'=16] {'row'}, dimensions={1} | all-to-all | bytes 409600 | tf_op jit(solution)/shard_map/all_to_all | solution.py:15
  494.1 12.2 %all_to_all.268 = f32[49,16,128]{2,0,1:T(8,128)S(1)} all-to-all(f32[49,16,128]{2,0,1:T(8,128)S(1)} %copy.159), channel_id=1, replica_groups=mesh['row'=8,'col'=16] {'col'}, dimensions={1} | all-to-all | bytes 802816 | tf_op jit(solution)/shard_map/all_to_all | solution.py:15
  506.4 11.8 %all_to_all.269 = f32[49,16,128]{2,0,1:T(8,128)S(1)} all-to-all(f32[49,16,128]{2,0,1:T(8,128)S(1)} %broadcast_in_dim.280), channel_id=1, replica_groups=mesh['row'=8,'col'=16] {'col'}, dimensions={1} | all-to-all | bytes 802816 | tf_op jit(solution)/shard_map/all_to_all | solution.py:17
  520.9 12.9 %shard_map.64 = (f32[2,24,2048]{2,1,0:T(8,128)}, f32[24,2048]{1,0:T(8,128)}) custom-call(bf16[24,2048]{1,0:T(8,128)(2,1)} %get-tuple-element.364.vbc_ref, bf16[2,24,2048]{2,1,0:T(8,128)(2,1)} %pad_maximum_fusion.5.vbi_ref, bf16[2,1,2048,2048]{3,2,1,0:T(8,128)(2,1)} %bitcast.414), custom_call_target="tpu_custom_call" | custom-call | tf_op jit(solution)/shard_map/pallas_call | solution.py:36
  562.2 14.7 %all_to_all.272 = f32[25,8,256]{2,0,1:T(8,128)S(1)} all-to-all(f32[25,8,256]{2,0,1:T(8,128)S(1)} %copy.169), channel_id=1, replica_groups=mesh['row'=8,'col'=16] {'row'}, dimensions={1} | all-to-all | bytes 409600 | tf_op jit(solution)/shard_map/all_to_all | solution.py:15
  589.0 12.2 %all_to_all.274 = f32[49,16,128]{2,0,1:T(8,128)S(1)} all-to-all(f32[49,16,128]{2,0,1:T(8,128)S(1)} %copy.172), channel_id=1, replica_groups=mesh['row'=8,'col'=16] {'col'}, dimensions={1} | all-to-all | bytes 802816 | tf_op jit(solution)/shard_map/all_to_all | solution.py:15
  601.3 12.0 %all_to_all.275 = f32[49,16,128]{2,0,1:T(8,128)S(1)} all-to-all(f32[49,16,128]{2,0,1:T(8,128)S(1)} %broadcast_in_dim.283), channel_id=1, replica_groups=mesh['row'=8,'col'=16] {'col'}, dimensions={1} | all-to-all | bytes 802816 | tf_op jit(solution)/shard_map/all_to_all | solution.py:17
  624.2 12.9 %shard_map.65 = (f32[2,24,2048]{2,1,0:T(8,128)}, f32[24,2048]{1,0:T(8,128)}) custom-call(bf16[24,2048]{1,0:T(8,128)(2,1)} %get-tuple-element.360.vbc_ref, bf16[2,24,2048]{2,1,0:T(8,128)(2,1)} %pad_maximum_fusion.6.vbi_ref, bf16[2,1,2048,2048]{3,2,1,0:T(8,128)(2,1)} %bitcast.415), custom_call_target="tpu_custom_call" | custom-call | tf_op jit(solution)/shard_map/pallas_call | solution.py:36
  666.2 14.7 %all_to_all.278 = f32[25,8,256]{2,0,1:T(8,128)S(1)} all-to-all(f32[25,8,256]{2,0,1:T(8,128)S(1)} %copy.182), channel_id=1, replica_groups=mesh['row'=8,'col'=16] {'row'}, dimensions={1} | all-to-all | bytes 409600 | tf_op jit(solution)/shard_map/all_to_all | solution.py:15
  693.1 12.2 %all_to_all.280 = f32[49,16,128]{2,0,1:T(8,128)S(1)} all-to-all(f32[49,16,128]{2,0,1:T(8,128)S(1)} %copy.185), channel_id=1, replica_groups=mesh['row'=8,'col'=16] {'col'}, dimensions={1} | all-to-all | bytes 802816 | tf_op jit(solution)/shard_map/all_to_all | solution.py:15
  705.4 11.8 %all_to_all.281 = f32[49,16,128]{2,0,1:T(8,128)S(1)} all-to-all(f32[49,16,128]{2,0,1:T(8,128)S(1)} %broadcast_in_dim.286), channel_id=1, replica_groups=mesh['row'=8,'col'=16] {'col'}, dimensions={1} | all-to-all | bytes 802816 | tf_op jit(solution)/shard_map/all_to_all | solution.py:17
  721.0 12.9 %shard_map.66 = (f32[2,24,2048]{2,1,0:T(8,128)}, f32[24,2048]{1,0:T(8,128)}) custom-call(bf16[24,2048]{1,0:T(8,128)(2,1)} %get-tuple-element.348.vbc_ref, bf16[2,24,2048]{2,1,0:T(8,128)(2,1)} %pad_maximum_fusion.7.vbi_ref, bf16[2,1,2048,2048]{3,2,1,0:T(8,128)(2,1)} %bitcast.416), custom_call_target="tpu_custom_call" | custom-call | tf_op jit(solution)/shard_map/pallas_call | solution.py:36
  762.3 14.7 %all_to_all.284 = f32[25,8,256]{2,0,1:T(8,128)S(1)} all-to-all(f32[25,8,256]{2,0,1:T(8,128)S(1)} %copy.195), channel_id=1, replica_groups=mesh['row'=8,'col'=16] {'row'}, dimensions={1} | all-to-all | bytes 409600 | tf_op jit(solution)/shard_map/all_to_all | solution.py:15
  (474 shorter events, 362.4 us)
Async XLA Ops:
  0.6 52.9 %copy-start = (f32[24,2048]{1,0:T(8,128)S(1)}, f32[24,2048]{1,0:T(8,128)}, u32[]{:S(2)}) copy-start(f32[24,2048]{1,0:T(8,128)} %param.52) | copy-start | bytes 589828
  0.6 52.9 %copy-start.1 = (f32[2048]{0:T(1024)S(1)}, f32[2048]{0:T(1024)}, u32[]{:S(2)}) copy-start(f32[2048]{0:T(1024)} %param.53) | copy-start | bytes 24580
  25.9 12.6 %all-to-all-start.1 = ((f32[49,16,128]{2,0,1:T(8,128)}), f32[49,16,128]{2,0,1:T(8,128)S(1)}, u32[]{:S(2)}, u32[]{:S(2)}) async-start(f32[49,16,128]{2,0,1:T(8,128)} %broadcast_in_dim.129), calls=%async_computation.1 | async-start | bytes 917504 | tf_op jit(solution)/shard_map/all_to_all | solution.py:17
  97.3 10.8 %all-to-all-start.5 = ((f32[25,8,256]{2,0,1:T(8,128)}), f32[25,8,256]{2,0,1:T(8,128)S(1)}, u32[]{:S(2)}, u32[]{:S(2)}) async-start(f32[25,8,256]{2,0,1:T(8,128)} %broadcast_in_dim.133), calls=%async_computation.5 | async-start | bytes 524288 | tf_op jit(solution)/shard_map/all_to_all | solution.py:17
  134.0 68.1 %copy-start.12 = (f32[7,8,16,128]{3,1,2,0:T(8,128)}, f32[7,8,16,128]{3,1,2,0:T(8,128)S(1)}, u32[]{:S(2)}) copy-start(f32[7,8,16,128]{3,1,2,0:T(8,128)S(1)} %copy.231) | copy-start | bytes 1376260
  202.1 28.0 %copy-start.14 = (f32[24]{0:T(128)}, f32[24]{0:T(128)S(1)}, u32[]{:S(2)}) copy-start(f32[24]{0:T(128)S(1)} %fusion.129) | copy-start | bytes 292
  227.8 1.4 copy-start.9
  231.9 94.9 %copy-start.3 = (f32[1,24,2048]{2,1,0:T(8,128)}, f32[1,24,2048]{2,1,0:T(8,128)S(1)}, u32[]{:S(2)}) copy-start(f32[1,24,2048]{2,1,0:T(8,128)S(1)} %get-tuple-element.389) | copy-start | bytes 589828
  299.6 1.2 copy-start.16
  325.2 69.7 %copy-start.10 = (f32[7,8,16,128]{3,1,2,0:T(8,128)}, f32[7,8,16,128]{3,1,2,0:T(8,128)S(1)}, u32[]{:S(2)}) copy-start(f32[7,8,16,128]{3,1,2,0:T(8,128)S(1)} %copy.247) | copy-start | bytes 1376260
  341.5 82.5 %copy-start.4 = (f32[1,24,2048]{2,1,0:T(8,128)S(1)}, f32[1,24,2048]{2,1,0:T(8,128)}, u32[]{:S(2)}) copy-start(f32[1,24,2048]{2,1,0:T(8,128)} %copy-done.3) | copy-start | bytes 589828
  394.8 0.5 copy-start.18
  421.0 1.4 copy-start.7
  425.2 94.9 %copy-start.2 = (f32[1,24,2048]{2,1,0:T(8,128)}, f32[1,24,2048]{2,1,0:T(8,128)S(1)}, u32[]{:S(2)}) copy-start(f32[1,24,2048]{2,1,0:T(8,128)S(1)} %get-tuple-element.493) | copy-start | bytes 589828
  518.5 1.5 copy-start.11
  613.6 0.8 copy-start.8
  692.0 44.2 %copy-start.5 = (f32[24,16,128]{2,0,1:T(8,128)S(1)}, f32[24,16,128]{2,0,1:T(8,128)}, u32[]{:S(2)}) copy-start(f32[24,16,128]{2,0,1:T(8,128)} %get-tuple-element.353) | copy-start | bytes 589828
  692.0 44.1 %copy-start.6 = (f32[24,16,128]{2,0,1:T(8,128)S(1)}, f32[24,16,128]{2,0,1:T(8,128)}, u32[]{:S(2)}) copy-start(f32[24,16,128]{2,0,1:T(8,128)} %get-tuple-element.403) | copy-start | bytes 589828
  717.5 1.4 copy-start.13
  721.0 66.9 %copy-start.15 = (f32[24]{0:T(128)S(1)}, f32[24]{0:T(128)}, u32[]{:S(2)}) copy-start(f32[24]{0:T(128)} %copy-done.14) | copy-start | bytes 292
  721.0 66.9 %copy-start.17 = (f32[24]{0:T(128)S(1)}, f32[24]{0:T(128)}, u32[]{:S(2)}) copy-start(f32[24]{0:T(128)} %copy-done.16) | copy-start | bytes 292
  721.0 66.9 %copy-start.19 = (f32[24]{0:T(128)S(1)}, f32[24]{0:T(128)}, u32[]{:S(2)}) copy-start(f32[24]{0:T(128)} %copy-done.18) | copy-start | bytes 292

commit v4 on v2

--- a/solution.py
+++ b/solution.py
@@ -9,48 +9,65 @@
 PAD = 8
 
 
-def all_reduce(x, axis, n):
+def all_reduce(x, axis, n, late=None):
     rows, width = x.shape
     w = width // n
     y = lax.all_to_all(x.reshape(rows, n, w), axis, 1, 1, tiled=True)
     part = jnp.sum(y, axis=1)
-    z = lax.all_to_all(jnp.broadcast_to(part[:, None, :], (rows, n, w)), axis, 1, 1, tiled=True)
-    return z.reshape(rows, width)
+    if late is not None:
+        extra = jnp.zeros((PAD, w), jnp.float32).at[0, : late.shape[0]].set(late)
+        part = jnp.concatenate([part, extra], axis=0)
+    z = lax.all_to_all(jnp.broadcast_to(part[:, None, :], part.shape[:1] + (n, w)), axis, 1, 1, tiled=True)
+    if late is None:
+        return z.reshape(rows, width), None
+    lates = z[rows, :, : late.shape[0]]
+    return z[:rows].reshape(rows, width), jnp.sum(lates, axis=0)
 
 
-def products_kernel(vbc_ref, vbi_ref, k_ref, fwd_ref, m_ref):
+def forward_kernel(vbc_ref, k_ref, fwd_ref):
+    fwd_ref[...] = lax.dot_general(
+        vbc_ref[...], k_ref[...], (((1,), (1,)), ((), ())), preferred_element_type=jnp.float32
+    )
+
+
+def mirrored_kernel(vbi_ref, k_ref, m_ref):
     @pl.when((pl.program_id(0) == 0) & (pl.program_id(1) == 0))
     def _():
         m_ref[...] = jnp.zeros_like(m_ref)
 
-    tile = k_ref[...]
-    fwd_ref[...] = lax.dot_general(
-        vbc_ref[...], tile, (((1,), (1,)), ((), ())), preferred_element_type=jnp.float32
-    )
-    m_ref[...] += jnp.dot(vbi_ref[...], tile, preferred_element_type=jnp.float32)
+    m_ref[...] += jnp.dot(vbi_ref[...], k_ref[...], preferred_element_type=jnp.float32)
 
 
-def block_products(vbc, vbi, blocks, tile=512):
+def forward_products(vbc, blocks, tile=512):
     nb, _, order, _ = blocks.shape
     vecs = vbc.shape[0]
     return pl.pallas_call(
-        products_kernel,
+        forward_kernel,
         grid=(nb, order // tile),
         in_specs=[
             pl.BlockSpec((vecs, order), lambda k, i: (0, 0)),
+            pl.BlockSpec((None, None, tile, order), lambda k, i: (k, 0, i, 0)),
+        ],
+        out_specs=pl.BlockSpec((None, vecs, tile), lambda k, i: (k, 0, i)),
+        out_shape=jax.ShapeDtypeStruct((nb, vecs, order), jnp.float32),
+        compiler_params=pltpu.CompilerParams(dimension_semantics=("arbitrary", "arbitrary")),
+    )(vbc, blocks)
+
+
+def mirrored_products(vbi, blocks, tile=512):
+    nb, _, order, _ = blocks.shape
+    vecs = vbi.shape[1]
+    return pl.pallas_call(
+        mirrored_kernel,
+        grid=(nb, order // tile),
+        in_specs=[
             pl.BlockSpec((None, vecs, tile), lambda k, i: (k, 0, i)),
             pl.BlockSpec((None, None, tile, order), lambda k, i: (k, 0, i, 0)),
         ],
-        out_specs=[
-            pl.BlockSpec((None, vecs, tile), lambda k, i: (k, 0, i)),
-            pl.BlockSpec((vecs, order), lambda k, i: (0, 0)),
-        ],
-        out_shape=[
-            jax.ShapeDtypeStruct((nb, vecs, order), jnp.float32),
-            jax.ShapeDtypeStruct((vecs, order), jnp.float32),
-        ],
+        out_specs=pl.BlockSpec((vecs, order), lambda k, i: (0, 0)),
+        out_shape=jax.ShapeDtypeStruct((vecs, order), jnp.float32),
         compiler_params=pltpu.CompilerParams(dimension_semantics=("arbitrary", "arbitrary")),
-    )(vbc, vbi, blocks)
+    )(vbi, blocks)
 
 
 def pack(blocks, scalars):
@@ -74,7 +91,7 @@
 
         def fetch(res):
             sent = [jnp.where(owner[k], res, 0.0) for k in range(nb)]
-            out = all_reduce(pack(sent, jnp.sum(res * res, axis=1)), "col", n_col)
+            out, _ = all_reduce(pack(sent, jnp.sum(res * res, axis=1)), "col", n_col)
             return [out[k * vecs:(k + 1) * vecs] for k in range(nb)], out[nb * vecs, :vecs]
 
         solution = jnp.zeros_like(rhs)
@@ -83,18 +100,18 @@
         dir_rows, norm_now = fetch(rhs)
         for step in range(ITERS):
             vb = direction.astype(jnp.bfloat16)
-            vbi = jnp.stack([jnp.where(used[k], dir_rows[k], 0.0) for k in range(nb)]).astype(jnp.bfloat16)
-            fwd, mirrored = block_products(vb, vbi, blocks)
+            fwd = forward_products(vb, blocks)
             forward = [jnp.where(used[k], fwd[k], 0.0) for k in range(nb)]
-            part = jnp.sum(direction * mirrored, axis=1)
-            part = part + jnp.where(first_row, jnp.sum(direction * (noise * direction), axis=1), 0.0)
+            part = jnp.where(first_row, jnp.sum(direction * (noise * direction), axis=1), 0.0)
             for k in range(nb):
                 part = part + jnp.sum(dir_rows[k] * forward[k], axis=1)
-            out = all_reduce(pack(forward, part), "col", n_col)
+            vbi = jnp.stack([jnp.where(used[k], dir_rows[k], 0.0) for k in range(nb)]).astype(jnp.bfloat16)
+            mirrored = mirrored_products(vbi, blocks)
+            out, late = all_reduce(pack(forward, part), "col", n_col, late=jnp.sum(direction * mirrored, axis=1))
             terms = mirrored
             for k in range(nb):
                 terms = terms + jnp.where(owner[k], out[k * vecs:(k + 1) * vecs], 0.0)
-            out = all_reduce(pack([terms], out[nb * vecs, :vecs]), "row", n_row)
+            out, _ = all_reduce(pack([terms], out[nb * vecs, :vecs] + late), "row", n_row)
             image = noise * direction + out[:vecs]
             curvature = out[vecs, :vecs]
             alpha = norm_now / curvature

time: 767 us -> 832 us (1.085)
  Pallas kernels: 103 us -> 170 us
  blocking collectives: 556 us -> 541 us
  starting transfers between devices: 7.91 us -> 19.6 us
    pallas_call x8 -> x16, Pallas kernels: 103 us -> 170 us  [the longest x8 89.2 us: forward_products(): pl.pallas_call(forward_kernel, grid=(nb, order // tile), in_specs=[pl.Blo...]
    all_to_all x24 -> x23, blocking collectives: 315 us -> 296 us  [all_reduce(): y = lax.all_to_all(x.reshape(rows, n, w), axis, 1, 1, tiled=True)]
    all_to_all x2 -> x3, starting transfers between devices: 7.91 us -> 19.6 us  [the longest x2 11 us: all_reduce(): lax.all_to_all(jnp.broadcast_to(part[:, None, :], part.shape[:1] + (n, w)...]
  transfers between devices with their start and end apart: 2 -> 3, of which waited for: 2 -> 2; matrix products, arithmetic and copies ran while one was open for 0% -> 0% of each run, Pallas kernels for 0% -> 1%
where the time goes in v4:
time: 832 us; the launch traced here: 827 us
  blocking collectives  541 us (65%)
  Pallas kernels  170 us (20%)
  other arithmetic  62.7 us (8%)
  starting transfers between devices  19.6 us (2%)
  waiting for transfers between devices  14.6 us (2%)
  local copies, waits for them, and re-layouts  14 us (2%)
    all_to_all x23, blocking collectives, all_reduce(): y = lax.all_to_all(x.reshape(rows, n, w), axis, 1, 1, tiled=True)  296 us
    all_to_all x22, blocking collectives, all_reduce(): lax.all_to_all(jnp.broadcast_to(part[:, None, :], part.shape[:1] + (n, w)...  245 us
    pallas_call x8, Pallas kernels, forward_products(): pl.pallas_call(forward_kernel, grid=(nb, order // tile), in_specs=[pl.Blo...  89.2 us
    pallas_call x8, Pallas kernels, mirrored_products(): pl.pallas_call(mirrored_kernel, grid=(nb, order // tile), in_specs=[pl.Bl...  81 us
  transfers between devices with their start and end apart: 3, of which 2 were waited for; matrix products, arithmetic and copies ran while one was open for 0% of the time, Pallas kernels for 1%

profile of v4, /device:TPU:1, one launch (start us, length us, event | category | flops | bytes accessed | tf_op | source)
XLA Modules:
  0.0 827.4 jit_solution(9518369558497813204)
XLA Ops:
  56.3 11.8 %all_to_all.240 = f32[56,16,128]{2,0,1:T(8,128)S(1)} all-to-all(f32[56,16,128]{2,0,1:T(8,128)S(1)} %copy_bitcast_fusion.30), channel_id=1, replica_groups=mesh['row'=8,'col'=16] {'col'}, dimensions={1} | all-to-all | bytes 917504 | tf_op jit(solution)/shard_map/all_to_all | solution.py:15
  68.2 11.8 %all_to_all.241 = f32[64,16,128]{2,0,1:T(8,128)S(1)} all-to-all(f32[64,16,128]{2,0,1:T(8,128)S(1)} %broadcast_in_dim.131), channel_id=1, replica_groups=mesh['row'=8,'col'=16] {'col'}, dimensions={1} | all-to-all | bytes 1048576 | tf_op jit(solution)/shard_map/all_to_all | solution.py:20
  81.2 15.2 %all_to_all.242 = f32[32,8,256]{2,0,1:T(8,128)S(1)} all-to-all(f32[32,8,256]{2,0,1:T(8,128)S(1)} %bitcast.521), channel_id=1, replica_groups=mesh['row'=8,'col'=16] {'row'}, dimensions={1} | all-to-all | bytes 524288 | tf_op jit(solution)/shard_map/all_to_all | solution.py:15
  108.7 12.2 %all_to_all.243 = f32[56,16,128]{2,0,1:T(8,128)S(1)} all-to-all(f32[56,16,128]{2,0,1:T(8,128)S(1)} %copy_bitcast_fusion.29), channel_id=1, replica_groups=mesh['row'=8,'col'=16] {'col'}, dimensions={1} | all-to-all | bytes 917504 | tf_op jit(solution)/shard_map/all_to_all | solution.py:15
  121.0 11.8 %all_to_all.244 = f32[56,16,128]{2,0,1:T(8,128)S(1)} all-to-all(f32[56,16,128]{2,0,1:T(8,128)S(1)} %broadcast_in_dim.134), channel_id=1, replica_groups=mesh['row'=8,'col'=16] {'col'}, dimensions={1} | all-to-all | bytes 917504 | tf_op jit(solution)/shard_map/all_to_all | solution.py:20
  170.8 11.6 %all_to_all.246 = f32[64,16,128]{2,0,1:T(8,128)S(1)} all-to-all(f32[64,16,128]{2,0,1:T(8,128)S(1)} %broadcast_in_dim.135), channel_id=1, replica_groups=mesh['row'=8,'col'=16] {'col'}, dimensions={1} | all-to-all | bytes 1048576 | tf_op jit(solution)/shard_map/all_to_all | solution.py:20
  183.5 14.7 %all_to_all.247 = f32[32,8,256]{2,0,1:T(8,128)S(1)} all-to-all(f32[32,8,256]{2,0,1:T(8,128)S(1)} %bitcast.522), channel_id=1, replica_groups=mesh['row'=8,'col'=16] {'row'}, dimensions={1} | all-to-all | bytes 524288 | tf_op jit(solution)/shard_map/all_to_all | solution.py:15
  209.2 12.2 %all_to_all.249 = f32[56,16,128]{2,0,1:T(8,128)S(1)} all-to-all(f32[56,16,128]{2,0,1:T(8,128)S(1)} %copy_bitcast_fusion.27), channel_id=1, replica_groups=mesh['row'=8,'col'=16] {'col'}, dimensions={1} | all-to-all | bytes 917504 | tf_op jit(solution)/shard_map/all_to_all | solution.py:15
  221.5 11.8 %all_to_all.250 = f32[56,16,128]{2,0,1:T(8,128)S(1)} all-to-all(f32[56,16,128]{2,0,1:T(8,128)S(1)} %broadcast_in_dim.137), channel_id=1, replica_groups=mesh['row'=8,'col'=16] {'col'}, dimensions={1} | all-to-all | bytes 917504 | tf_op jit(solution)/shard_map/all_to_all | solution.py:20
  275.0 11.6 %all_to_all.252 = f32[64,16,128]{2,0,1:T(8,128)S(1)} all-to-all(f32[64,16,128]{2,0,1:T(8,128)S(1)} %broadcast_in_dim.272), channel_id=1, replica_groups=mesh['row'=8,'col'=16] {'col'}, dimensions={1} | all-to-all | bytes 1048576 | tf_op jit(solution)/shard_map/all_to_all | solution.py:20
  287.8 14.7 %all_to_all.253 = f32[32,8,256]{2,0,1:T(8,128)S(1)} all-to-all(f32[32,8,256]{2,0,1:T(8,128)S(1)} %bitcast.523), channel_id=1, replica_groups=mesh['row'=8,'col'=16] {'row'}, dimensions={1} | all-to-all | bytes 524288 | tf_op jit(solution)/shard_map/all_to_all | solution.py:15
  313.4 12.2 %all_to_all.255 = f32[56,16,128]{2,0,1:T(8,128)S(1)} all-to-all(f32[56,16,128]{2,0,1:T(8,128)S(1)} %copy_bitcast_fusion.25), channel_id=1, replica_groups=mesh['row'=8,'col'=16] {'col'}, dimensions={1} | all-to-all | bytes 917504 | tf_op jit(solution)/shard_map/all_to_all | solution.py:15
  325.7 11.8 %all_to_all.256 = f32[56,16,128]{2,0,1:T(8,128)S(1)} all-to-all(f32[56,16,128]{2,0,1:T(8,128)S(1)} %broadcast_in_dim.274), channel_id=1, replica_groups=mesh['row'=8,'col'=16] {'col'}, dimensions={1} | all-to-all | bytes 917504 | tf_op jit(solution)/shard_map/all_to_all | solution.py:20
  376.2 11.8 %all_to_all.258 = f32[64,16,128]{2,0,1:T(8,128)S(1)} all-to-all(f32[64,16,128]{2,0,1:T(8,128)S(1)} %broadcast_in_dim.275), channel_id=1, replica_groups=mesh['row'=8,'col'=16] {'col'}, dimensions={1} | all-to-all | bytes 1048576 | tf_op jit(solution)/shard_map/all_to_all | solution.py:20
  389.1 14.7 %all_to_all.259 = f32[32,8,256]{2,0,1:T(8,128)S(1)} all-to-all(f32[32,8,256]{2,0,1:T(8,128)S(1)} %bitcast.524), channel_id=1, replica_groups=mesh['row'=8,'col'=16] {'row'}, dimensions={1} | all-to-all | bytes 524288 | tf_op jit(solution)/shard_map/all_to_all | solution.py:15
  414.8 12.2 %all_to_all.261 = f32[56,16,128]{2,0,1:T(8,128)S(1)} all-to-all(f32[56,16,128]{2,0,1:T(8,128)S(1)} %copy_bitcast_fusion.23), channel_id=1, replica_groups=mesh['row'=8,'col'=16] {'col'}, dimensions={1} | all-to-all | bytes 917504 | tf_op jit(solution)/shard_map/all_to_all | solution.py:15
  427.1 11.8 %all_to_all.262 = f32[56,16,128]{2,0,1:T(8,128)S(1)} all-to-all(f32[56,16,128]{2,0,1:T(8,128)S(1)} %broadcast_in_dim.277), channel_id=1, replica_groups=mesh['row'=8,'col'=16] {'col'}, dimensions={1} | all-to-all | bytes 917504 | tf_op jit(solution)/shard_map/all_to_all | solution.py:20
  468.5 11.5 %all_to_all.263 = f32[56,16,128]{2,0,1:T(8,128)S(1)} all-to-all(f32[56,16,128]{2,0,1:T(8,128)S(1)} %copy_bitcast_fusion.22), channel_id=1, replica_groups=mesh['row'=8,'col'=16] {'col'}, dimensions={1} | all-to-all | bytes 917504 | tf_op jit(solution)/shard_map/all_to_all | solution.py:15
  480.0 11.8 %all_to_all.264 = f32[64,16,128]{2,0,1:T(8,128)S(1)} all-to-all(f32[64,16,128]{2,0,1:T(8,128)S(1)} %broadcast_in_dim.278), channel_id=1, replica_groups=mesh['row'=8,'col'=16] {'col'}, dimensions={1} | all-to-all | bytes 1048576 | tf_op jit(solution)/shard_map/all_to_all | solution.py:20
  492.9 14.7 %all_to_all.265 = f32[32,8,256]{2,0,1:T(8,128)S(1)} all-to-all(f32[32,8,256]{2,0,1:T(8,128)S(1)} %bitcast.525), channel_id=1, replica_groups=mesh['row'=8,'col'=16] {'row'}, dimensions={1} | all-to-all | bytes 524288 | tf_op jit(solution)/shard_map/all_to_all | solution.py:15
  518.8 12.2 %all_to_all.267 = f32[56,16,128]{2,0,1:T(8,128)S(1)} all-to-all(f32[56,16,128]{2,0,1:T(8,128)S(1)} %copy_bitcast_fusion.21), channel_id=1, replica_groups=mesh['row'=8,'col'=16] {'col'}, dimensions={1} | all-to-all | bytes 917504 | tf_op jit(solution)/shard_map/all_to_all | solution.py:15
  531.2 11.8 %all_to_all.268 = f32[56,16,128]{2,0,1:T(8,128)S(1)} all-to-all(f32[56,16,128]{2,0,1:T(8,128)S(1)} %broadcast_in_dim.280), channel_id=1, replica_groups=mesh['row'=8,'col'=16] {'col'}, dimensions={1} | all-to-all | bytes 917504 | tf_op jit(solution)/shard_map/all_to_all | solution.py:20
  581.6 11.8 %all_to_all.270 = f32[64,16,128]{2,0,1:T(8,128)S(1)} all-to-all(f32[64,16,128]{2,0,1:T(8,128)S(1)} %broadcast_in_dim.281), channel_id=1, replica_groups=mesh['row'=8,'col'=16] {'col'}, dimensions={1} | all-to-all | bytes 1048576 | tf_op jit(solution)/shard_map/all_to_all | solution.py:20
  594.5 14.8 %all_to_all.271 = f32[32,8,256]{2,0,1:T(8,128)S(1)} all-to-all(f32[32,8,256]{2,0,1:T(8,128)S(1)} %bitcast.526), channel_id=1, replica_groups=mesh['row'=8,'col'=16] {'row'}, dimensions={1} | all-to-all | bytes 524288 | tf_op jit(solution)/shard_map/all_to_all | solution.py:15
  620.6 12.2 %all_to_all.273 = f32[56,16,128]{2,0,1:T(8,128)S(1)} all-to-all(f32[56,16,128]{2,0,1:T(8,128)S(1)} %copy_bitcast_fusion.19), channel_id=1, replica_groups=mesh['row'=8,'col'=16] {'col'}, dimensions={1} | all-to-all | bytes 917504 | tf_op jit(solution)/shard_map/all_to_all | solution.py:15
  632.9 11.8 %all_to_all.274 = f32[56,16,128]{2,0,1:T(8,128)S(1)} all-to-all(f32[56,16,128]{2,0,1:T(8,128)S(1)} %broadcast_in_dim.283), channel_id=1, replica_groups=mesh['row'=8,'col'=16] {'col'}, dimensions={1} | all-to-all | bytes 917504 | tf_op jit(solution)/shard_map/all_to_all | solution.py:20
  686.7 11.8 %all_to_all.276 = f32[64,16,128]{2,0,1:T(8,128)S(1)} all-to-all(f32[64,16,128]{2,0,1:T(8,128)S(1)} %broadcast_in_dim.284), channel_id=1, replica_groups=mesh['row'=8,'col'=16] {'col'}, dimensions={1} | all-to-all | bytes 1048576 | tf_op jit(solution)/shard_map/all_to_all | solution.py:20
  699.6 14.7 %all_to_all.277 = f32[32,8,256]{2,0,1:T(8,128)S(1)} all-to-all(f32[32,8,256]{2,0,1:T(8,128)S(1)} %bitcast.527), channel_id=1, replica_groups=mesh['row'=8,'col'=16] {'row'}, dimensions={1} | all-to-all | bytes 524288 | tf_op jit(solution)/shard_map/all_to_all | solution.py:15
  725.3 12.2 %all_to_all.279 = f32[56,16,128]{2,0,1:T(8,128)S(1)} all-to-all(f32[56,16,128]{2,0,1:T(8,128)S(1)} %copy_bitcast_fusion.17), channel_id=1, replica_groups=mesh['row'=8,'col'=16] {'col'}, dimensions={1} | all-to-all | bytes 917504 | tf_op jit(solution)/shard_map/all_to_all | solution.py:15
  737.6 11.8 %all_to_all.280 = f32[56,16,128]{2,0,1:T(8,128)S(1)} all-to-all(f32[56,16,128]{2,0,1:T(8,128)S(1)} %broadcast_in_dim.286), channel_id=1, replica_groups=mesh['row'=8,'col'=16] {'col'}, dimensions={1} | all-to-all | bytes 917504 | tf_op jit(solution)/shard_map/all_to_all | solution.py:20
  788.2 11.6 %all_to_all.282 = f32[64,16,128]{2,0,1:T(8,128)S(1)} all-to-all(f32[64,16,128]{2,0,1:T(8,128)S(1)} %broadcast_in_dim.287), channel_id=1, replica_groups=mesh['row'=8,'col'=16] {'col'}, dimensions={1} | all-to-all | bytes 1048576 | tf_op jit(solution)/shard_map/all_to_all | solution.py:20
  801.0 14.7 %all_to_all.283 = f32[32,8,256]{2,0,1:T(8,128)S(1)} all-to-all(f32[32,8,256]{2,0,1:T(8,128)S(1)} %bitcast.528), channel_id=1, replica_groups=mesh['row'=8,'col'=16] {'row'}, dimensions={1} | all-to-all | bytes 524288 | tf_op jit(solution)/shard_map/all_to_all | solution.py:15
  (400 shorter events, 419.3 us)
Async XLA Ops:
  5.9 21.2 %all-to-all-start = ((f32[56,16,128]{2,0,1:T(8,128)}), f32[56,16,128]{2,0,1:T(8,128)S(1)}, u32[]{:S(2)}, u32[]{:S(2)}) async-start(f32[56,16,128]{2,0,1:T(8,128)} %copy_bitcast_fusion.31), calls=%async_computation | async-start | bytes 917504 | tf_op jit(solution)/shard_map/all_to_all | solution.py:15
  15.8 39.4 %copy-start = (f32[24,2048]{1,0:T(8,128)S(1)}, f32[24,2048]{1,0:T(8,128)}, u32[]{:S(2)}) copy-start(f32[24,2048]{1,0:T(8,128)} %param.68) | copy-start | bytes 589828
  15.8 39.4 %copy-start.1 = (f32[2048]{0:T(1024)S(1)}, f32[2048]{0:T(1024)}, u32[]{:S(2)}) copy-start(f32[2048]{0:T(1024)} %param.69) | copy-start | bytes 24580
  27.9 16.0 %all-to-all-start.1 = ((f32[56,16,128]{2,0,1:T(8,128)}), f32[56,16,128]{2,0,1:T(8,128)S(1)}, u32[]{:S(2)}, u32[]{:S(2)}) async-start(f32[56,16,128]{2,0,1:T(8,128)} %broadcast_in_dim.129), calls=%async_computation.1 | async-start | bytes 917504 | tf_op jit(solution)/shard_map/all_to_all | solution.py:20
  97.1 10.8 %all-to-all-start.5 = ((f32[32,8,256]{2,0,1:T(8,128)}), f32[32,8,256]{2,0,1:T(8,128)S(1)}, u32[]{:S(2)}, u32[]{:S(2)}) async-start(f32[32,8,256]{2,0,1:T(8,128)} %broadcast_in_dim.133), calls=%async_computation.5 | async-start | bytes 524288 | tf_op jit(solution)/shard_map/all_to_all | solution.py:20
  132.8 0.8 copy-start.21
  208.9 26.6 %copy-start.25 = (f32[24]{0:T(128)}, f32[24]{0:T(128)S(1)}, u32[]{:S(2)}) copy-start(f32[24]{0:T(128)S(1)} %fusion.121) | copy-start | bytes 292
  250.0 102.0 %copy-start.7 = (f32[24,16,128]{2,0,1:T(8,128)}, f32[24,16,128]{2,0,1:T(8,128)S(1)}, u32[]{:S(2)}) copy-start(f32[24,16,128]{2,0,1:T(8,128)S(1)} %get-tuple-element.449) | copy-start | bytes 589828
  250.0 102.0 %copy-start.9 = (f32[24,16,128]{2,0,1:T(8,128)}, f32[24,16,128]{2,0,1:T(8,128)S(1)}, u32[]{:S(2)}) copy-start(f32[24,16,128]{2,0,1:T(8,128)S(1)} %get-tuple-element.465) | copy-start | bytes 589828
  250.1 13.3 %copy-start.33 = (f32[24]{0:T(128)S(1)}, f32[24]{0:T(128)}, u32[]{:S(2)}) copy-start(f32[24]{0:T(128)} %get-tuple-element.448) | copy-start | bytes 292
  250.1 13.3 %copy-start.34 = (f32[24]{0:T(128)S(1)}, f32[24]{0:T(128)}, u32[]{:S(2)}) copy-start(f32[24]{0:T(128)} %get-tuple-element.464) | copy-start | bytes 292
  250.1 13.3 %copy-start.14 = (f32[24,2048]{1,0:T(8,128)S(1)}, f32[24,2048]{1,0:T(8,128)}, u32[]{:S(2)}) copy-start(f32[24,2048]{1,0:T(8,128)} %get-tuple-element.525) | copy-start | bytes 589828
  337.5 0.8 copy-start.19
  376.2 78.0 %copy-start.8 = (f32[24,16,128]{2,0,1:T(8,128)S(1)}, f32[24,16,128]{2,0,1:T(8,128)}, u32[]{:S(2)}) copy-start(f32[24,16,128]{2,0,1:T(8,128)} %copy-done.7) | copy-start | bytes 589828
  414.5 24.4 %copy-start.27 = (f32[24]{0:T(128)}, f32[24]{0:T(128)S(1)}, u32[]{:S(2)}) copy-start(f32[24]{0:T(128)S(1)} %fusion.123) | copy-start | bytes 292
  456.1 101.4 %copy-start.4 = (f32[24,16,128]{2,0,1:T(8,128)}, f32[24,16,128]{2,0,1:T(8,128)S(1)}, u32[]{:S(2)}) copy-start(f32[24,16,128]{2,0,1:T(8,128)S(1)} %get-tuple-element.433) | copy-start | bytes 589828
  456.1 12.3 %copy-start.10 = (f32[24,2048]{1,0:T(8,128)S(1)}, f32[24,2048]{1,0:T(8,128)}, u32[]{:S(2)}) copy-start(f32[24,2048]{1,0:T(8,128)} %get-tuple-element.514) | copy-start | bytes 589828
  456.1 12.3 %copy-start.11 = (f32[24,2048]{1,0:T(8,128)S(1)}, f32[24,2048]{1,0:T(8,128)}, u32[]{:S(2)}) copy-start(f32[24,2048]{1,0:T(8,128)} %get-tuple-element.517) | copy-start | bytes 589828
  456.4 101.5 %copy-start.2 = (f32[1,24,2048]{2,1,0:T(8,128)}, f32[1,24,2048]{2,1,0:T(8,128)S(1)}, u32[]{:S(2)}) copy-start(f32[1,24,2048]{2,1,0:T(8,128)S(1)} %get-tuple-element.557) | copy-start | bytes 589828
  480.0 77.5 %copy-start.6 = (f32[24,16,128]{2,0,1:T(8,128)S(1)}, f32[24,16,128]{2,0,1:T(8,128)}, u32[]{:S(2)}) copy-start(f32[24,16,128]{2,0,1:T(8,128)} %get-tuple-element.469) | copy-start | bytes 589828
  543.0 0.8 copy-start.20
  581.6 78.3 %copy-start.5 = (f32[24,16,128]{2,0,1:T(8,128)S(1)}, f32[24,16,128]{2,0,1:T(8,128)}, u32[]{:S(2)}) copy-start(f32[24,16,128]{2,0,1:T(8,128)} %copy-done.4) | copy-start | bytes 589828
  594.5 68.5 %copy-start.3 = (f32[1,24,2048]{2,1,0:T(8,128)S(1)}, f32[1,24,2048]{2,1,0:T(8,128)}, u32[]{:S(2)}) copy-start(f32[1,24,2048]{2,1,0:T(8,128)} %copy-done.2) | copy-start | bytes 589828
  661.9 13.2 %copy-start.12 = (f32[24,2048]{1,0:T(8,128)S(1)}, f32[24,2048]{1,0:T(8,128)}, u32[]{:S(2)}) copy-start(f32[24,2048]{1,0:T(8,128)} %get-tuple-element.506) | copy-start | bytes 589828
  663.1 11.9 %copy-start.13 = (f32[24,2048]{1,0:T(8,128)S(1)}, f32[24,2048]{1,0:T(8,128)}, u32[]{:S(2)}) copy-start(f32[24,2048]{1,0:T(8,128)} %get-tuple-element.509) | copy-start | bytes 589828
  686.7 76.5 %copy-start.15 = (f32[24,16,128]{2,0,1:T(8,128)S(1)}, f32[24,16,128]{2,0,1:T(8,128)}, u32[]{:S(2)}) copy-start(f32[24,16,128]{2,0,1:T(8,128)} %get-tuple-element.417) | copy-start | bytes 589828
  749.4 1.4 copy-start.22
  763.0 63.4 %copy-start.24 = (f32[24]{0:T(128)S(1)}, f32[24]{0:T(128)}, u32[]{:S(2)}) copy-start(f32[24]{0:T(128)} %copy-done.23) | copy-start | bytes 292
  763.0 63.3 %copy-start.26 = (f32[24]{0:T(128)S(1)}, f32[24]{0:T(128)}, u32[]{:S(2)}) copy-start(f32[24]{0:T(128)} %copy-done.25) | copy-start | bytes 292
  763.0 63.3 %copy-start.28 = (f32[24]{0:T(128)S(1)}, f32[24]{0:T(128)}, u32[]{:S(2)}) copy-start(f32[24]{0:T(128)} %copy-done.27) | copy-start | bytes 292
  763.0 63.3 %copy-start.30 = (f32[24]{0:T(128)S(1)}, f32[24]{0:T(128)}, u32[]{:S(2)}) copy-start(f32[24]{0:T(128)} %copy-done.29) | copy-start | bytes 292
  763.1 63.3 %copy-start.32 = (f32[24]{0:T(128)S(1)}, f32[24]{0:T(128)}, u32[]{:S(2)}) copy-start(f32[24]{0:T(128)} %copy-done.31) | copy-start | bytes 292
  (6 other events, 3.9 us)

commit v5 on v2

v5 whole, which is shorter than its diff:
```python
import jax
import jax.numpy as jnp
from jax import lax
from jax.experimental import pallas as pl
from jax.experimental.pallas import tpu as pltpu
from jax.sharding import PartitionSpec as P

ITERS = 8
PAD = 8


def all_reduce(x, axis, n):
    rows, width = x.shape
    w = width // n
    y = lax.all_to_all(x.reshape(rows, n, w), axis, 1, 1, tiled=True)
    part = jnp.sum(y, axis=1)
    z = lax.all_to_all(jnp.broadcast_to(part[:, None, :], (rows, n, w)), axis, 1, 1, tiled=True)
    return z.reshape(rows, width)


def products_kernel(flags_ref, d_ref, di_ref, k_ref, fwd_ref, m_ref, p_ref):
    k = pl.program_id(0)
    i = pl.program_id(1)

    @pl.when((k == 0) & (i == 0))
    def _():
        m_ref[...] = jnp.zeros_like(m_ref)
        p_ref[...] = jnp.zeros_like(p_ref)

    used = flags_ref[k] != 0
    tile = k_ref[...]
    f = lax.dot_general(
        d_ref[...].astype(jnp.bfloat16), tile, (((1,), (1,)), ((), ())), preferred_element_type=jnp.float32
    )
    f = jnp.where(used, f, 0.0)
    fwd_ref[...] = f
    di = di_ref[...]
    acc = p_ref[...]
    for j in range(f.shape[1] // 128):
        acc = acc + di[:, j * 128:(j + 1) * 128] * f[:, j * 128:(j + 1) * 128]
    p_ref[...] = acc
    vbi = jnp.where(used, di, 0.0).astype(jnp.bfloat16)
    m_ref[...] += jnp.dot(vbi, tile, preferred_element_type=jnp.float32)

    @pl.when((k == pl.num_programs(0) - 1) & (i == pl.num_programs(1) - 1))
    def _():
        acc = p_ref[...]
        for j in range(m_ref.shape[1] // 128):
            acc = acc + d_ref[:, j * 128:(j + 1) * 128] * m_ref[:, j * 128:(j + 1) * 128]
        p_ref[...] = acc


def block_products(flags, d, di, blocks, tile=512):
    nb, _, order, _ = blocks.shape
    vecs = d.shape[0]
    grid_spec = pltpu.PrefetchScalarGridSpec(
        num_scalar_prefetch=1,
        grid=(nb, order // tile),
        in_specs=[
            pl.BlockSpec((vecs, order), lambda k, i, f: (0, 0)),
            pl.BlockSpec((None, vecs, tile), lambda k, i, f: (k, 0, i)),
            pl.BlockSpec((None, None, tile, order), lambda k, i, f: (k, 0, i, 0)),
        ],
        out_specs=[
            pl.BlockSpec((None, vecs, tile), lambda k, i, f: (k, 0, i)),
            pl.BlockSpec((vecs, order), lambda k, i, f: (0, 0)),
            pl.BlockSpec((vecs, 128), lambda k, i, f: (0, 0)),
        ],
    )
    return pl.pallas_call(
        products_kernel,
        grid_spec=grid_spec,
        out_shape=[
            jax.ShapeDtypeStruct((nb, vecs, order), jnp.float32),
            jax.ShapeDtypeStruct((vecs, order), jnp.float32),
            jax.ShapeDtypeStruct((vecs, 128), jnp.float32),
        ],
        compiler_params=pltpu.CompilerParams(dimension_semantics=("arbitrary", "arbitrary")),
    )(flags, d, di, blocks)


def pack(blocks, scalars):
    width = blocks[0].shape[1]
    tail = jnp.zeros((PAD, width), jnp.float32).at[0, : scalars.shape[0]].set(scalars)
    return jnp.concatenate(list(blocks) + [tail], axis=0)


def make_on_device(n_row, n_col):
    def on_device(rhs, noise_var, block_rows, kernel_blocks):
        blocks = kernel_blocks[0, 0]
        assert blocks.shape[1] == 1
        rows = block_rows[0]
        nb = rows.shape[0]
        vecs, width = rhs.shape
        col = lax.axis_index("col")
        first_row = lax.axis_index("row") == 0
        flags = (col >= rows).astype(jnp.int32)
        owner = [col == rows[k] for k in range(nb)]
        noise = noise_var[None, :]

        def fetch(res):
            sent = [jnp.where(owner[k], res, 0.0) for k in range(nb)]
            out = all_reduce(pack(sent, jnp.sum(res * res, axis=1)), "col", n_col)
            return out[: nb * vecs].reshape(nb, vecs, width), out[nb * vecs, :vecs]

        solution = jnp.zeros_like(rhs)
        residual = rhs
        direction = rhs
        dir_rows, norm_now = fetch(rhs)
        for step in range(ITERS):
            fwd, mirrored, lanes = block_products(flags, direction, dir_rows, blocks)
            forward = [fwd[k] for k in range(nb)]
            part = jnp.sum(lanes, axis=1)
            part = part + jnp.where(first_row, jnp.sum(direction * (noise * direction), axis=1), 0.0)
            out = all_reduce(pack(forward, part), "col", n_col)
            terms = mirrored
            for k in range(nb):
                terms = terms + jnp.where(owner[k], out[k * vecs:(k + 1) * vecs], 0.0)
            out = all_reduce(pack([terms], out[nb * vecs, :vecs]), "row", n_row)
            image = noise * direction + out[:vecs]
            curvature = out[vecs, :vecs]
            alpha = norm_now / curvature
            solution = solution + alpha[:, None] * direction
            residual = residual - alpha[:, None] * image
            if step + 1 < ITERS:
                res_rows, norm_next = fetch(residual)
                beta = norm_next / norm_now
                direction = residual + beta[:, None] * direction
                dir_rows = res_rows + beta[None, :, None] * dir_rows
                norm_now = norm_next
        return (solution, residual)

    return on_device


def solution(mesh):
    return jax.shard_map(
        make_on_device(mesh.shape["row"], mesh.shape["col"]),
        mesh=mesh,
        in_specs=(
            P(None, "col"),
            P("col"),
            P("row", None),
            P("row", "col", None, None, None, None),
        ),
        out_specs=(P(None, "col"), P(None, "col")),
        check_vma=False,
    )
```

time: 767 us -> 750 us (0.978)
  other arithmetic: 60.1 us -> 34.5 us
  Pallas kernels: 103 us -> 111 us
    another operation x16 -> x0, other arithmetic: 13.3 us -> none
    select_n x8 -> x0, other arithmetic: 8.64 us -> none  [on_device(): forward = [jnp.where(used[k], fwd[k], 0.0) for k in range(nb)]]
    unnamed x64 -> x82, local copies, waits for them, and re-layouts: 1.69 us -> 10.3 us
    slice x40 -> x16, local copies, waits for them, and re-layouts: 9.62 us -> 1.25 us  [fetch(): return (out[:nb * vecs].reshape(nb, vecs, width), out[nb * vecs, :vecs])]
where the time goes in v5:
time: 750 us; the launch traced here: 745 us
  blocking collectives  556 us (74%)
  Pallas kernels  111 us (15%)
  other arithmetic  34.5 us (5%)
  local copies, waits for them, and re-layouts  18.3 us (2%)
  waiting for transfers between devices  14.2 us (2%)
  starting transfers between devices  7.91 us (1%)
    all_to_all x24, blocking collectives, all_reduce(): y = lax.all_to_all(x.reshape(rows, n, w), axis, 1, 1, tiled=True)  314 us
    all_to_all x22, blocking collectives, all_reduce(): lax.all_to_all(jnp.broadcast_to(part[:, None, :], (rows, n, w)), axis, 1,...  242 us
    pallas_call x8, Pallas kernels, block_products(): pl.pallas_call(products_kernel, grid_spec=grid_spec, out_shape=[jax.Shape...  111 us
  transfers between devices with their start and end apart: 2, of which 2 were waited for; matrix products, arithmetic and copies ran while one was open for 0% of the time, Pallas kernels for 0%

profile of v5, /device:TPU:1, one launch (start us, length us, event | category | flops | bytes accessed | tf_op | source)
XLA Modules:
  0.0 745.3 jit_solution(8663971591250416970)
XLA Ops:
  4.4 18.3 %all_to_all.240 = f32[56,16,128]{2,0,1:T(8,128)S(1)} all-to-all(f32[56,16,128]{2,0,1:T(8,128)S(1)} %copy_bitcast_fusion.23), channel_id=1, replica_groups=mesh['row'=8,'col'=16] {'col'}, dimensions={1} | all-to-all | bytes 917504 | tf_op jit(solution)/shard_map/all_to_all | solution.py:15
  37.1 13.9 %shard_map.59 = (f32[2,24,2048]{2,1,0:T(8,128)}, f32[24,2048]{1,0:T(8,128)}, f32[24,128]{1,0:T(8,128)}) custom-call(s32[2]{0:T(128)} %fusion.64.flags_ref, f32[24,2048]{1,0:T(8,128)} %d_ref.1, f32[2,24,2048]{2,1,0:T(8,128)} %reshape.1249.di_ref, bf16[2,1,2048,2048]{3,2,1,0:T(8,128)(2,1)} %bitcast.411), custom_call_target="tpu_custom_call" | custom-call | tf_op jit(solution)/shard_map/pallas_call | solution.py:70
  76.8 16.1 %all_to_all.243 = f32[32,8,256]{2,0,1:T(8,128)S(1)} all-to-all(f32[32,8,256]{2,0,1:T(8,128)S(1)} %bitcast.435), channel_id=1, replica_groups=mesh['row'=8,'col'=16] {'row'}, dimensions={1} | all-to-all | bytes 524288 | tf_op jit(solution)/shard_map/all_to_all | solution.py:15
  104.9 12.2 %all_to_all.244 = f32[56,16,128]{2,0,1:T(8,128)S(1)} all-to-all(f32[56,16,128]{2,0,1:T(8,128)S(1)} %copy_bitcast_fusion.22), channel_id=1, replica_groups=mesh['row'=8,'col'=16] {'col'}, dimensions={1} | all-to-all | bytes 917504 | tf_op jit(solution)/shard_map/all_to_all | solution.py:15
  117.2 11.8 %all_to_all.245 = f32[56,16,128]{2,0,1:T(8,128)S(1)} all-to-all(f32[56,16,128]{2,0,1:T(8,128)S(1)} %broadcast_in_dim.99), channel_id=1, replica_groups=mesh['row'=8,'col'=16] {'col'}, dimensions={1} | all-to-all | bytes 917504 | tf_op jit(solution)/shard_map/all_to_all | solution.py:17
  131.0 13.9 %shard_map.60 = (f32[2,24,2048]{2,1,0:T(8,128)}, f32[24,2048]{1,0:T(8,128)}, f32[24,128]{1,0:T(8,128)}) custom-call(s32[2]{0:T(128)} %fusion.64.flags_ref, f32[24,2048]{1,0:T(8,128)} %get-tuple-element.365.d_ref, f32[2,24,2048]{2,1,0:T(8,128)} %multiply_add_fusion.6.di_ref, bf16[2,1,2048,2048]{3,2,1,0:T(8,128)(2,1)} %bitcast.412), custom_call_target="tpu_custom_call" | custom-call | tf_op jit(solution)/shard_map/pallas_call | solution.py:70
  170.9 14.7 %all_to_all.248 = f32[32,8,256]{2,0,1:T(8,128)S(1)} all-to-all(f32[32,8,256]{2,0,1:T(8,128)S(1)} %bitcast.436), channel_id=1, replica_groups=mesh['row'=8,'col'=16] {'row'}, dimensions={1} | all-to-all | bytes 524288 | tf_op jit(solution)/shard_map/all_to_all | solution.py:15
  195.9 12.2 %all_to_all.250 = f32[56,16,128]{2,0,1:T(8,128)S(1)} all-to-all(f32[56,16,128]{2,0,1:T(8,128)S(1)} %copy_bitcast_fusion.21), channel_id=1, replica_groups=mesh['row'=8,'col'=16] {'col'}, dimensions={1} | all-to-all | bytes 917504 | tf_op jit(solution)/shard_map/all_to_all | solution.py:15
  208.2 11.8 %all_to_all.251 = f32[56,16,128]{2,0,1:T(8,128)S(1)} all-to-all(f32[56,16,128]{2,0,1:T(8,128)S(1)} %broadcast_in_dim.102), channel_id=1, replica_groups=mesh['row'=8,'col'=16] {'col'}, dimensions={1} | all-to-all | bytes 917504 | tf_op jit(solution)/shard_map/all_to_all | solution.py:17
  222.1 13.9 %shard_map.61 = (f32[2,24,2048]{2,1,0:T(8,128)}, f32[24,2048]{1,0:T(8,128)}, f32[24,128]{1,0:T(8,128)}) custom-call(s32[2]{0:T(128)} %fusion.64.flags_ref, f32[24,2048]{1,0:T(8,128)} %get-tuple-element.361.d_ref, f32[2,24,2048]{2,1,0:T(8,128)} %multiply_add_fusion.5.di_ref, bf16[2,1,2048,2048]{3,2,1,0:T(8,128)(2,1)} %bitcast.413), custom_call_target="tpu_custom_call" | custom-call | tf_op jit(solution)/shard_map/pallas_call | solution.py:70
  261.9 14.7 %all_to_all.254 = f32[32,8,256]{2,0,1:T(8,128)S(1)} all-to-all(f32[32,8,256]{2,0,1:T(8,128)S(1)} %bitcast.437), channel_id=1, replica_groups=mesh['row'=8,'col'=16] {'row'}, dimensions={1} | all-to-all | bytes 524288 | tf_op jit(solution)/shard_map/all_to_all | solution.py:15
  287.2 12.2 %all_to_all.256 = f32[56,16,128]{2,0,1:T(8,128)S(1)} all-to-all(f32[56,16,128]{2,0,1:T(8,128)S(1)} %copy_bitcast_fusion.20), channel_id=1, replica_groups=mesh['row'=8,'col'=16] {'col'}, dimensions={1} | all-to-all | bytes 917504 | tf_op jit(solution)/shard_map/all_to_all | solution.py:15
  299.5 11.8 %all_to_all.257 = f32[56,16,128]{2,0,1:T(8,128)S(1)} all-to-all(f32[56,16,128]{2,0,1:T(8,128)S(1)} %broadcast_in_dim.105), channel_id=1, replica_groups=mesh['row'=8,'col'=16] {'col'}, dimensions={1} | all-to-all | bytes 917504 | tf_op jit(solution)/shard_map/all_to_all | solution.py:17
  313.3 13.9 %shard_map.62 = (f32[2,24,2048]{2,1,0:T(8,128)}, f32[24,2048]{1,0:T(8,128)}, f32[24,128]{1,0:T(8,128)}) custom-call(s32[2]{0:T(128)} %fusion.64.flags_ref, f32[24,2048]{1,0:T(8,128)} %get-tuple-element.357.d_ref, f32[2,24,2048]{2,1,0:T(8,128)} %multiply_add_fusion.4.di_ref, bf16[2,1,2048,2048]{3,2,1,0:T(8,128)(2,1)} %bitcast.414), custom_call_target="tpu_custom_call" | custom-call | tf_op jit(solution)/shard_map/pallas_call | solution.py:70
  353.2 14.7 %all_to_all.260 = f32[32,8,256]{2,0,1:T(8,128)S(1)} all-to-all(f32[32,8,256]{2,0,1:T(8,128)S(1)} %bitcast.438), channel_id=1, replica_groups=mesh['row'=8,'col'=16] {'row'}, dimensions={1} | all-to-all | bytes 524288 | tf_op jit(solution)/shard_map/all_to_all | solution.py:15
  378.3 12.2 %all_to_all.262 = f32[56,16,128]{2,0,1:T(8,128)S(1)} all-to-all(f32[56,16,128]{2,0,1:T(8,128)S(1)} %copy_bitcast_fusion.19), channel_id=1, replica_groups=mesh['row'=8,'col'=16] {'col'}, dimensions={1} | all-to-all | bytes 917504 | tf_op jit(solution)/shard_map/all_to_all | solution.py:15
  390.6 11.8 %all_to_all.263 = f32[56,16,128]{2,0,1:T(8,128)S(1)} all-to-all(f32[56,16,128]{2,0,1:T(8,128)S(1)} %broadcast_in_dim.108), channel_id=1, replica_groups=mesh['row'=8,'col'=16] {'col'}, dimensions={1} | all-to-all | bytes 917504 | tf_op jit(solution)/shard_map/all_to_all | solution.py:17
  404.4 13.9 %shard_map.63 = (f32[2,24,2048]{2,1,0:T(8,128)}, f32[24,2048]{1,0:T(8,128)}, f32[24,128]{1,0:T(8,128)}) custom-call(s32[2]{0:T(128)} %fusion.64.flags_ref, f32[24,2048]{1,0:T(8,128)} %get-tuple-element.353.d_ref, f32[2,24,2048]{2,1,0:T(8,128)} %multiply_add_fusion.3.di_ref, bf16[2,1,2048,2048]{3,2,1,0:T(8,128)(2,1)} %bitcast.415), custom_call_target="tpu_custom_call" | custom-call | tf_op jit(solution)/shard_map/pallas_call | solution.py:70
  420.4 11.5 %all_to_all.264 = f32[56,16,128]{2,0,1:T(8,128)S(1)} all-to-all(f32[56,16,128]{2,0,1:T(8,128)S(1)} %pad_maximum_fusion.4), channel_id=1, replica_groups=mesh['row'=8,'col'=16] {'col'}, dimensions={1} | all-to-all | bytes 917504 | tf_op jit(solution)/shard_map/all_to_all | solution.py:15
  444.3 14.7 %all_to_all.266 = f32[32,8,256]{2,0,1:T(8,128)S(1)} all-to-all(f32[32,8,256]{2,0,1:T(8,128)S(1)} %bitcast.439), channel_id=1, replica_groups=mesh['row'=8,'col'=16] {'row'}, dimensions={1} | all-to-all | bytes 524288 | tf_op jit(solution)/shard_map/all_to_all | solution.py:15
  469.7 12.2 %all_to_all.268 = f32[56,16,128]{2,0,1:T(8,128)S(1)} all-to-all(f32[56,16,128]{2,0,1:T(8,128)S(1)} %copy_bitcast_fusion.18), channel_id=1, replica_groups=mesh['row'=8,'col'=16] {'col'}, dimensions={1} | all-to-all | bytes 917504 | tf_op jit(solution)/shard_map/all_to_all | solution.py:15
  482.0 11.8 %all_to_all.269 = f32[56,16,128]{2,0,1:T(8,128)S(1)} all-to-all(f32[56,16,128]{2,0,1:T(8,128)S(1)} %broadcast_in_dim.111), channel_id=1, replica_groups=mesh['row'=8,'col'=16] {'col'}, dimensions={1} | all-to-all | bytes 917504 | tf_op jit(solution)/shard_map/all_to_all | solution.py:17
  495.9 13.9 %shard_map.64 = (f32[2,24,2048]{2,1,0:T(8,128)}, f32[24,2048]{1,0:T(8,128)}, f32[24,128]{1,0:T(8,128)}) custom-call(s32[2]{0:T(128)} %fusion.64.flags_ref, f32[24,2048]{1,0:T(8,128)} %get-tuple-element.349.d_ref, f32[2,24,2048]{2,1,0:T(8,128)} %multiply_add_fusion.2.di_ref, bf16[2,1,2048,2048]{3,2,1,0:T(8,128)(2,1)} %bitcast.416), custom_call_target="tpu_custom_call" | custom-call | tf_op jit(solution)/shard_map/pallas_call | solution.py:70
  535.8 14.7 %all_to_all.272 = f32[32,8,256]{2,0,1:T(8,128)S(1)} all-to-all(f32[32,8,256]{2,0,1:T(8,128)S(1)} %bitcast.440), channel_id=1, replica_groups=mesh['row'=8,'col'=16] {'row'}, dimensions={1} | all-to-all | bytes 524288 | tf_op jit(solution)/shard_map/all_to_all | solution.py:15
  561.2 12.2 %all_to_all.274 = f32[56,16,128]{2,0,1:T(8,128)S(1)} all-to-all(f32[56,16,128]{2,0,1:T(8,128)S(1)} %copy_bitcast_fusion.17), channel_id=1, replica_groups=mesh['row'=8,'col'=16] {'col'}, dimensions={1} | all-to-all | bytes 917504 | tf_op jit(solution)/shard_map/all_to_all | solution.py:15
  573.5 11.8 %all_to_all.275 = f32[56,16,128]{2,0,1:T(8,128)S(1)} all-to-all(f32[56,16,128]{2,0,1:T(8,128)S(1)} %broadcast_in_dim.114), channel_id=1, replica_groups=mesh['row'=8,'col'=16] {'col'}, dimensions={1} | all-to-all | bytes 917504 | tf_op jit(solution)/shard_map/all_to_all | solution.py:17
  587.4 13.9 %shard_map.65 = (f32[2,24,2048]{2,1,0:T(8,128)}, f32[24,2048]{1,0:T(8,128)}, f32[24,128]{1,0:T(8,128)}) custom-call(s32[2]{0:T(128)} %fusion.64.flags_ref, f32[24,2048]{1,0:T(8,128)} %get-tuple-element.345.d_ref, f32[2,24,2048]{2,1,0:T(8,128)} %multiply_add_fusion.1.di_ref, bf16[2,1,2048,2048]{3,2,1,0:T(8,128)(2,1)} %bitcast.417), custom_call_target="tpu_custom_call" | custom-call | tf_op jit(solution)/shard_map/pallas_call | solution.py:70
  627.3 14.7 %all_to_all.278 = f32[32,8,256]{2,0,1:T(8,128)S(1)} all-to-all(f32[32,8,256]{2,0,1:T(8,128)S(1)} %bitcast.441), channel_id=1, replica_groups=mesh['row'=8,'col'=16] {'row'}, dimensions={1} | all-to-all | bytes 524288 | tf_op jit(solution)/shard_map/all_to_all | solution.py:15
  653.0 12.2 %all_to_all.280 = f32[56,16,128]{2,0,1:T(8,128)S(1)} all-to-all(f32[56,16,128]{2,0,1:T(8,128)S(1)} %copy_bitcast_fusion.16), channel_id=1, replica_groups=mesh['row'=8,'col'=16] {'col'}, dimensions={1} | all-to-all | bytes 917504 | tf_op jit(solution)/shard_map/all_to_all | solution.py:15
  665.3 11.8 %all_to_all.281 = f32[56,16,128]{2,0,1:T(8,128)S(1)} all-to-all(f32[56,16,128]{2,0,1:T(8,128)S(1)} %broadcast_in_dim.117), channel_id=1, replica_groups=mesh['row'=8,'col'=16] {'col'}, dimensions={1} | all-to-all | bytes 917504 | tf_op jit(solution)/shard_map/all_to_all | solution.py:17
  679.8 13.7 %shard_map.66 = (f32[2,24,2048]{2,1,0:T(8,128)}, f32[24,2048]{1,0:T(8,128)}, f32[24,128]{1,0:T(8,128)}) custom-call(s32[2]{0:T(128)} %fusion.64.flags_ref, f32[24,2048]{1,0:T(8,128)} %get-tuple-element.341.d_ref, f32[2,24,2048]{2,1,0:T(8,128)} %multiply_add_fusion.di_ref, bf16[2,1,2048,2048]{3,2,1,0:T(8,128)(2,1)} %bitcast.418), custom_call_target="tpu_custom_call" | custom-call | tf_op jit(solution)/shard_map/pallas_call | solution.py:70
  719.6 14.7 %all_to_all.284 = f32[32,8,256]{2,0,1:T(8,128)S(1)} all-to-all(f32[32,8,256]{2,0,1:T(8,128)S(1)} %bitcast.442), channel_id=1, replica_groups=mesh['row'=8,'col'=16] {'row'}, dimensions={1} | all-to-all | bytes 524288 | tf_op jit(solution)/shard_map/all_to_all | solution.py:15
  (355 shorter events, 314.0 us)
Async XLA Ops:
  23.5 12.6 %all-to-all-start.1 = ((f32[56,16,128]{2,0,1:T(8,128)}), f32[56,16,128]{2,0,1:T(8,128)S(1)}, u32[]{:S(2)}, u32[]{:S(2)}) async-start(f32[56,16,128]{2,0,1:T(8,128)} %broadcast_in_dim.95), calls=%async_computation.1 | async-start | bytes 917504 | tf_op jit(solution)/shard_map/all_to_all | solution.py:17
  27.1 77.5 %copy-start = (f32[24,2048]{1,0:T(8,128)S(1)}, f32[24,2048]{1,0:T(8,128)}, u32[]{:S(2)}) copy-start(f32[24,2048]{1,0:T(8,128)} %d_ref.1) | copy-start | bytes 589828
  27.1 77.5 %copy-start.14 = (f32[2048]{0:T(1024)S(1)}, f32[2048]{0:T(1024)}, u32[]{:S(2)}) copy-start(f32[2048]{0:T(1024)} %param.53) | copy-start | bytes 24580
  37.1 93.1 %copy-start.7 = (f32[2,24,2048]{2,1,0:T(8,128)S(1)}, f32[2,24,2048]{2,1,0:T(8,128)}, u32[]{:S(2)}) copy-start(f32[2,24,2048]{2,1,0:T(8,128)} %reshape.1249.di_ref) | copy-start | bytes 1179652
  93.7 10.8 %all-to-all-start.5 = ((f32[32,8,256]{2,0,1:T(8,128)}), f32[32,8,256]{2,0,1:T(8,128)S(1)}, u32[]{:S(2)}, u32[]{:S(2)}) async-start(f32[32,8,256]{2,0,1:T(8,128)} %broadcast_in_dim.98), calls=%async_computation.5 | async-start | bytes 524288 | tf_op jit(solution)/shard_map/all_to_all | solution.py:17
  129.9 65.7 %copy-start.1 = (f32[24,2048]{1,0:T(8,128)S(1)}, f32[24,2048]{1,0:T(8,128)}, u32[]{:S(2)}) copy-start(f32[24,2048]{1,0:T(8,128)} %get-tuple-element.365.d_ref) | copy-start | bytes 589828
  131.0 90.2 %copy-start.8 = (f32[2,24,2048]{2,1,0:T(8,128)S(1)}, f32[2,24,2048]{2,1,0:T(8,128)}, u32[]{:S(2)}) copy-start(f32[2,24,2048]{2,1,0:T(8,128)} %multiply_add_fusion.6.di_ref) | copy-start | bytes 1179652
  220.9 65.7 %copy-start.2 = (f32[24,2048]{1,0:T(8,128)S(1)}, f32[24,2048]{1,0:T(8,128)}, u32[]{:S(2)}) copy-start(f32[24,2048]{1,0:T(8,128)} %get-tuple-element.361.d_ref) | copy-start | bytes 589828
  222.1 90.4 %copy-start.9 = (f32[2,24,2048]{2,1,0:T(8,128)S(1)}, f32[2,24,2048]{2,1,0:T(8,128)}, u32[]{:S(2)}) copy-start(f32[2,24,2048]{2,1,0:T(8,128)} %multiply_add_fusion.5.di_ref) | copy-start | bytes 1179652
  286.7 0.5 copy-start.17
  312.2 65.7 %copy-start.3 = (f32[24,2048]{1,0:T(8,128)S(1)}, f32[24,2048]{1,0:T(8,128)}, u32[]{:S(2)}) copy-start(f32[24,2048]{1,0:T(8,128)} %get-tuple-element.357.d_ref) | copy-start | bytes 589828
  313.3 90.2 %copy-start.10 = (f32[2,24,2048]{2,1,0:T(8,128)S(1)}, f32[2,24,2048]{2,1,0:T(8,128)}, u32[]{:S(2)}) copy-start(f32[2,24,2048]{2,1,0:T(8,128)} %multiply_add_fusion.4.di_ref) | copy-start | bytes 1179652
  378.0 24.4 %copy-start.19 = (f32[24]{0:T(128)}, f32[24]{0:T(128)S(1)}, u32[]{:S(2)}) copy-start(f32[24]{0:T(128)S(1)} %fusion.68) | copy-start | bytes 292
  403.3 65.7 %copy-start.4 = (f32[24,2048]{1,0:T(8,128)S(1)}, f32[24,2048]{1,0:T(8,128)}, u32[]{:S(2)}) copy-start(f32[24,2048]{1,0:T(8,128)} %get-tuple-element.353.d_ref) | copy-start | bytes 589828
  404.4 90.6 %copy-start.11 = (f32[2,24,2048]{2,1,0:T(8,128)S(1)}, f32[2,24,2048]{2,1,0:T(8,128)}, u32[]{:S(2)}) copy-start(f32[2,24,2048]{2,1,0:T(8,128)} %multiply_add_fusion.3.di_ref) | copy-start | bytes 1179652
  469.0 0.5 copy-start.21
  494.7 65.8 %copy-start.5 = (f32[24,2048]{1,0:T(8,128)S(1)}, f32[24,2048]{1,0:T(8,128)}, u32[]{:S(2)}) copy-start(f32[24,2048]{1,0:T(8,128)} %get-tuple-element.349.d_ref) | copy-start | bytes 589828
  495.9 90.6 %copy-start.12 = (f32[2,24,2048]{2,1,0:T(8,128)S(1)}, f32[2,24,2048]{2,1,0:T(8,128)}, u32[]{:S(2)}) copy-start(f32[2,24,2048]{2,1,0:T(8,128)} %multiply_add_fusion.2.di_ref) | copy-start | bytes 1179652
  560.5 0.5 copy-start.23
  585.3 0.9 copy-start.16
  586.3 66.4 %copy-start.6 = (f32[24,2048]{1,0:T(8,128)S(1)}, f32[24,2048]{1,0:T(8,128)}, u32[]{:S(2)}) copy-start(f32[24,2048]{1,0:T(8,128)} %get-tuple-element.345.d_ref) | copy-start | bytes 589828
  587.4 91.6 %copy-start.13 = (f32[2,24,2048]{2,1,0:T(8,128)S(1)}, f32[2,24,2048]{2,1,0:T(8,128)}, u32[]{:S(2)}) copy-start(f32[2,24,2048]{2,1,0:T(8,128)} %multiply_add_fusion.1.di_ref) | copy-start | bytes 1179652
  678.6 65.6 %copy-start.15 = (f32[24,2048]{1,0:T(8,128)S(1)}, f32[24,2048]{1,0:T(8,128)}, u32[]{:S(2)}) copy-start(f32[24,2048]{1,0:T(8,128)} %get-tuple-element.341.d_ref) | copy-start | bytes 589828
  678.7 65.6 %copy-start.18 = (f32[24]{0:T(128)S(1)}, f32[24]{0:T(128)}, u32[]{:S(2)}) copy-start(f32[24]{0:T(128)} %copy-done.17) | copy-start | bytes 292
  678.7 65.6 %copy-start.20 = (f32[24]{0:T(128)S(1)}, f32[24]{0:T(128)}, u32[]{:S(2)}) copy-start(f32[24]{0:T(128)} %copy-done.19) | copy-start | bytes 292
  678.7 65.6 %copy-start.22 = (f32[24]{0:T(128)S(1)}, f32[24]{0:T(128)}, u32[]{:S(2)}) copy-start(f32[24]{0:T(128)} %copy-done.21) | copy-start | bytes 292
  678.7 65.6 %copy-start.24 = (f32[24]{0:T(128)S(1)}, f32[24]{0:T(128)}, u32[]{:S(2)}) copy-start(f32[24]{0:T(128)} %copy-done.23) | copy-start | bytes 292

commit v6 on v5

--- a/solution.py
+++ b/solution.py
@@ -99,9 +99,18 @@
         noise = noise_var[None, :]
 
         def fetch(res):
-            sent = [jnp.where(owner[k], res, 0.0) for k in range(nb)]
-            out = all_reduce(pack(sent, jnp.sum(res * res, axis=1)), "col", n_col)
-            return out[: nb * vecs].reshape(nb, vecs, width), out[nb * vecs, :vecs]
+            w = width // n_col
+            tail = jnp.zeros((PAD, n_col, w), jnp.float32).at[0, :, :vecs].set(
+                jnp.broadcast_to(jnp.sum(res * res, axis=1), (n_col, vecs))
+            )
+            x = jnp.concatenate([res.reshape(vecs, n_col, w), tail], axis=0)
+            y = lax.all_to_all(x, "col", 1, 1, tiled=True)
+            norm = jnp.sum(y[vecs, :, :vecs], axis=0)
+            kept = jnp.concatenate(
+                [lax.dynamic_index_in_dim(y[:vecs], rows[k], axis=1, keepdims=False) for k in range(nb)], axis=0
+            )
+            z = lax.all_to_all(jnp.broadcast_to(kept[:, None, :], (nb * vecs, n_col, w)), "col", 1, 1, tiled=True)
+            return z.reshape(nb, vecs, width), norm
 
         solution = jnp.zeros_like(rhs)
         residual = rhs

time: 750 us -> 733 us (0.977)
  blocking collectives: 556 us -> 433 us
  waiting for transfers between devices: 14.2 us -> 74.7 us
  starting transfers between devices: 7.91 us -> 45.5 us
    all_to_all x24 -> x16, blocking collectives: 314 us -> 212 us  [all_reduce(): y = lax.all_to_all(x.reshape(rows, n, w), axis, 1, 1, tiled=True)]
    all_to_all x22 -> x14, blocking collectives: 242 us -> 148 us  [all_reduce(): lax.all_to_all(jnp.broadcast_to(part[:, None, :], (rows, n, w)), axis, 1,...]
    all_to_all x0 -> x7, blocking collectives: none -> 72.4 us  [fetch(): y = lax.all_to_all(x, 'col', 1, 1, tiled=True)]
    all_to_all x0 -> x9, waiting for transfers between devices: none -> 60.7 us  [the longest x8 58.1 us: fetch(): lax.all_to_all(jnp.broadcast_to(kept[:, None, :], (nb * vecs, n_col, w)),...]
    all_to_all x0 -> x9, starting transfers between devices: none -> 37.6 us  [the longest x8 29 us: fetch(): lax.all_to_all(jnp.broadcast_to(kept[:, None, :], (nb * vecs, n_col, w)),...]
  transfers between devices with their start and end apart: 2 -> 11, of which waited for: 2 -> 11; matrix products, arithmetic and copies ran while one was open for 0% -> 1% of each run, Pallas kernels for 0% -> 0%
where the time goes in v6:
time: 733 us; the launch traced here: 728 us
  blocking collectives  433 us (59%)
  Pallas kernels  111 us (15%)
  waiting for transfers between devices  74.7 us (10%)
  starting transfers between devices  45.5 us (6%)
  other arithmetic  32.9 us (4%)
  local copies, waits for them, and re-layouts  24.8 us (3%)
    all_to_all x16, blocking collectives, all_reduce(): y = lax.all_to_all(x.reshape(rows, n, w), axis, 1, 1, tiled=True)  212 us
    all_to_all x14, blocking collectives, all_reduce(): lax.all_to_all(jnp.broadcast_to(part[:, None, :], (rows, n, w)), axis, 1,...  148 us
    pallas_call x8, Pallas kernels, block_products(): pl.pallas_call(products_kernel, grid_spec=grid_spec, out_shape=[jax.Shape...  111 us
    all_to_all x7, blocking collectives, fetch(): y = lax.all_to_all(x, 'col', 1, 1, tiled=True)  72.4 us
    all_to_all x8, waiting for transfers between devices, fetch(): lax.all_to_all(jnp.broadcast_to(kept[:, None, :], (nb * vecs, n_col, w)),...  58.1 us
    all_to_all x8, starting transfers between devices, fetch(): lax.all_to_all(jnp.broadcast_to(kept[:, None, :], (nb * vecs, n_col, w)),...  29 us
  transfers between devices with their start and end apart: 11, of which 11 were waited for; matrix products, arithmetic and copies ran while one was open for 1% of the time, Pallas kernels for 0%

profile of v6, /device:TPU:1, one launch (start us, length us, event | category | flops | bytes accessed | tf_op | source)
XLA Modules:
  0.0 728.4 jit_solution(8853074489217663868)
XLA Ops:
  33.8 13.9 %shard_map.59 = (f32[2,24,2048]{2,1,0:T(8,128)}, f32[24,2048]{1,0:T(8,128)}, f32[24,128]{1,0:T(8,128)}) custom-call(s32[2]{0:T(128)} %fusion.56.flags_ref, f32[24,2048]{1,0:T(8,128)} %d_ref.1, f32[2,24,2048]{2,1,0:T(8,128)} %reshape.1204.di_ref, bf16[2,1,2048,2048]{3,2,1,0:T(8,128)(2,1)} %bitcast.402), custom_call_target="tpu_custom_call" | custom-call | tf_op jit(solution)/shard_map/pallas_call | solution.py:70
  49.8 11.2 %all_to_all.240 = f32[56,16,128]{2,0,1:T(8,128)S(1)} all-to-all(f32[56,16,128]{2,0,1:T(8,128)S(1)} %pad_maximum_fusion), channel_id=1, replica_groups=mesh['row'=8,'col'=16] {'col'}, dimensions={1} | all-to-all | bytes 917504 | tf_op jit(solution)/shard_map/all_to_all | solution.py:15
  75.2 15.7 %all_to_all.241 = f32[32,8,256]{2,0,1:T(8,128)S(1)} all-to-all(f32[32,8,256]{2,0,1:T(8,128)S(1)} %bitcast.427), channel_id=1, replica_groups=mesh['row'=8,'col'=16] {'row'}, dimensions={1} | all-to-all | bytes 524288 | tf_op jit(solution)/shard_map/all_to_all | solution.py:15
  126.9 13.9 %shard_map.60 = (f32[2,24,2048]{2,1,0:T(8,128)}, f32[24,2048]{1,0:T(8,128)}, f32[24,128]{1,0:T(8,128)}) custom-call(s32[2]{0:T(128)} %fusion.56.flags_ref, f32[24,2048]{1,0:T(8,128)} %get-tuple-element.365.d_ref, f32[2,24,2048]{2,1,0:T(8,128)} %multiply_add_fusion.6.di_ref, bf16[2,1,2048,2048]{3,2,1,0:T(8,128)(2,1)} %bitcast.403), custom_call_target="tpu_custom_call" | custom-call | tf_op jit(solution)/shard_map/pallas_call | solution.py:70
  142.9 11.5 %all_to_all.243 = f32[56,16,128]{2,0,1:T(8,128)S(1)} all-to-all(f32[56,16,128]{2,0,1:T(8,128)S(1)} %pad_maximum_fusion.1), channel_id=1, replica_groups=mesh['row'=8,'col'=16] {'col'}, dimensions={1} | all-to-all | bytes 917504 | tf_op jit(solution)/shard_map/all_to_all | solution.py:15
  154.5 11.2 %all_to_all.244 = f32[56,16,128]{2,0,1:T(8,128)S(1)} all-to-all(f32[56,16,128]{2,0,1:T(8,128)S(1)} %broadcast_in_dim.81), channel_id=1, replica_groups=mesh['row'=8,'col'=16] {'col'}, dimensions={1} | all-to-all | bytes 917504 | tf_op jit(solution)/shard_map/all_to_all | solution.py:17
  166.8 15.0 %all_to_all.245 = f32[32,8,256]{2,0,1:T(8,128)S(1)} all-to-all(f32[32,8,256]{2,0,1:T(8,128)S(1)} %bitcast.428), channel_id=1, replica_groups=mesh['row'=8,'col'=16] {'row'}, dimensions={1} | all-to-all | bytes 524288 | tf_op jit(solution)/shard_map/all_to_all | solution.py:15
  216.1 13.9 %shard_map.61 = (f32[2,24,2048]{2,1,0:T(8,128)}, f32[24,2048]{1,0:T(8,128)}, f32[24,128]{1,0:T(8,128)}) custom-call(s32[2]{0:T(128)} %fusion.56.flags_ref, f32[24,2048]{1,0:T(8,128)} %get-tuple-element.361.d_ref, f32[2,24,2048]{2,1,0:T(8,128)} %multiply_add_fusion.5.di_ref, bf16[2,1,2048,2048]{3,2,1,0:T(8,128)(2,1)} %bitcast.404), custom_call_target="tpu_custom_call" | custom-call | tf_op jit(solution)/shard_map/pallas_call | solution.py:70
  232.2 11.5 %all_to_all.248 = f32[56,16,128]{2,0,1:T(8,128)S(1)} all-to-all(f32[56,16,128]{2,0,1:T(8,128)S(1)} %pad_maximum_fusion.2), channel_id=1, replica_groups=mesh['row'=8,'col'=16] {'col'}, dimensions={1} | all-to-all | bytes 917504 | tf_op jit(solution)/shard_map/all_to_all | solution.py:15
  243.7 11.2 %all_to_all.249 = f32[56,16,128]{2,0,1:T(8,128)S(1)} all-to-all(f32[56,16,128]{2,0,1:T(8,128)S(1)} %broadcast_in_dim.84), channel_id=1, replica_groups=mesh['row'=8,'col'=16] {'col'}, dimensions={1} | all-to-all | bytes 917504 | tf_op jit(solution)/shard_map/all_to_all | solution.py:17
  256.0 15.0 %all_to_all.250 = f32[32,8,256]{2,0,1:T(8,128)S(1)} all-to-all(f32[32,8,256]{2,0,1:T(8,128)S(1)} %bitcast.429), channel_id=1, replica_groups=mesh['row'=8,'col'=16] {'row'}, dimensions={1} | all-to-all | bytes 524288 | tf_op jit(solution)/shard_map/all_to_all | solution.py:15
  281.3 10.3 %all_to_all.252 = f32[32,16,128]{2,0,1:T(8,128)S(1)} all-to-all(f32[32,16,128]{2,0,1:T(8,128)S(1)} %pad_maximum_fusion.11), channel_id=1, replica_groups=mesh['row'=8,'col'=16] {'col'}, dimensions={1} | all-to-all | bytes 524288 | tf_op jit(solution)/shard_map/all_to_all | solution.py:107
  305.4 13.9 %shard_map.62 = (f32[2,24,2048]{2,1,0:T(8,128)}, f32[24,2048]{1,0:T(8,128)}, f32[24,128]{1,0:T(8,128)}) custom-call(s32[2]{0:T(128)} %fusion.56.flags_ref, f32[24,2048]{1,0:T(8,128)} %get-tuple-element.357.d_ref, f32[2,24,2048]{2,1,0:T(8,128)} %multiply_add_fusion.4.di_ref, bf16[2,1,2048,2048]{3,2,1,0:T(8,128)(2,1)} %bitcast.405), custom_call_target="tpu_custom_call" | custom-call | tf_op jit(solution)/shard_map/pallas_call | solution.py:70
  321.4 11.5 %all_to_all.253 = f32[56,16,128]{2,0,1:T(8,128)S(1)} all-to-all(f32[56,16,128]{2,0,1:T(8,128)S(1)} %pad_maximum_fusion.3), channel_id=1, replica_groups=mesh['row'=8,'col'=16] {'col'}, dimensions={1} | all-to-all | bytes 917504 | tf_op jit(solution)/shard_map/all_to_all | solution.py:15
  332.9 11.2 %all_to_all.254 = f32[56,16,128]{2,0,1:T(8,128)S(1)} all-to-all(f32[56,16,128]{2,0,1:T(8,128)S(1)} %broadcast_in_dim.87), channel_id=1, replica_groups=mesh['row'=8,'col'=16] {'col'}, dimensions={1} | all-to-all | bytes 917504 | tf_op jit(solution)/shard_map/all_to_all | solution.py:17
  345.3 15.0 %all_to_all.255 = f32[32,8,256]{2,0,1:T(8,128)S(1)} all-to-all(f32[32,8,256]{2,0,1:T(8,128)S(1)} %bitcast.430), channel_id=1, replica_groups=mesh['row'=8,'col'=16] {'row'}, dimensions={1} | all-to-all | bytes 524288 | tf_op jit(solution)/shard_map/all_to_all | solution.py:15
  394.6 13.9 %shard_map.63 = (f32[2,24,2048]{2,1,0:T(8,128)}, f32[24,2048]{1,0:T(8,128)}, f32[24,128]{1,0:T(8,128)}) custom-call(s32[2]{0:T(128)} %fusion.56.flags_ref, f32[24,2048]{1,0:T(8,128)} %get-tuple-element.353.d_ref, f32[2,24,2048]{2,1,0:T(8,128)} %multiply_add_fusion.3.di_ref, bf16[2,1,2048,2048]{3,2,1,0:T(8,128)(2,1)} %bitcast.406), custom_call_target="tpu_custom_call" | custom-call | tf_op jit(solution)/shard_map/pallas_call | solution.py:70
  410.6 11.5 %all_to_all.258 = f32[56,16,128]{2,0,1:T(8,128)S(1)} all-to-all(f32[56,16,128]{2,0,1:T(8,128)S(1)} %pad_maximum_fusion.4), channel_id=1, replica_groups=mesh['row'=8,'col'=16] {'col'}, dimensions={1} | all-to-all | bytes 917504 | tf_op jit(solution)/shard_map/all_to_all | solution.py:15
  422.2 11.2 %all_to_all.259 = f32[56,16,128]{2,0,1:T(8,128)S(1)} all-to-all(f32[56,16,128]{2,0,1:T(8,128)S(1)} %broadcast_in_dim.90), channel_id=1, replica_groups=mesh['row'=8,'col'=16] {'col'}, dimensions={1} | all-to-all | bytes 917504 | tf_op jit(solution)/shard_map/all_to_all | solution.py:17
  434.5 15.0 %all_to_all.260 = f32[32,8,256]{2,0,1:T(8,128)S(1)} all-to-all(f32[32,8,256]{2,0,1:T(8,128)S(1)} %bitcast.431), channel_id=1, replica_groups=mesh['row'=8,'col'=16] {'row'}, dimensions={1} | all-to-all | bytes 524288 | tf_op jit(solution)/shard_map/all_to_all | solution.py:15
  483.9 13.9 %shard_map.64 = (f32[2,24,2048]{2,1,0:T(8,128)}, f32[24,2048]{1,0:T(8,128)}, f32[24,128]{1,0:T(8,128)}) custom-call(s32[2]{0:T(128)} %fusion.56.flags_ref, f32[24,2048]{1,0:T(8,128)} %get-tuple-element.349.d_ref, f32[2,24,2048]{2,1,0:T(8,128)} %multiply_add_fusion.2.di_ref, bf16[2,1,2048,2048]{3,2,1,0:T(8,128)(2,1)} %bitcast.407), custom_call_target="tpu_custom_call" | custom-call | tf_op jit(solution)/shard_map/pallas_call | solution.py:70
  499.9 11.5 %all_to_all.263 = f32[56,16,128]{2,0,1:T(8,128)S(1)} all-to-all(f32[56,16,128]{2,0,1:T(8,128)S(1)} %pad_maximum_fusion.5), channel_id=1, replica_groups=mesh['row'=8,'col'=16] {'col'}, dimensions={1} | all-to-all | bytes 917504 | tf_op jit(solution)/shard_map/all_to_all | solution.py:15
  511.4 11.2 %all_to_all.264 = f32[56,16,128]{2,0,1:T(8,128)S(1)} all-to-all(f32[56,16,128]{2,0,1:T(8,128)S(1)} %broadcast_in_dim.93), channel_id=1, replica_groups=mesh['row'=8,'col'=16] {'col'}, dimensions={1} | all-to-all | bytes 917504 | tf_op jit(solution)/shard_map/all_to_all | solution.py:17
  523.8 15.0 %all_to_all.265 = f32[32,8,256]{2,0,1:T(8,128)S(1)} all-to-all(f32[32,8,256]{2,0,1:T(8,128)S(1)} %bitcast.432), channel_id=1, replica_groups=mesh['row'=8,'col'=16] {'row'}, dimensions={1} | all-to-all | bytes 524288 | tf_op jit(solution)/shard_map/all_to_all | solution.py:15
  573.1 13.9 %shard_map.65 = (f32[2,24,2048]{2,1,0:T(8,128)}, f32[24,2048]{1,0:T(8,128)}, f32[24,128]{1,0:T(8,128)}) custom-call(s32[2]{0:T(128)} %fusion.56.flags_ref, f32[24,2048]{1,0:T(8,128)} %get-tuple-element.345.d_ref, f32[2,24,2048]{2,1,0:T(8,128)} %multiply_add_fusion.1.di_ref, bf16[2,1,2048,2048]{3,2,1,0:T(8,128)(2,1)} %bitcast.408), custom_call_target="tpu_custom_call" | custom-call | tf_op jit(solution)/shard_map/pallas_call | solution.py:70
  589.2 11.7 %all_to_all.268 = f32[56,16,128]{2,0,1:T(8,128)S(1)} all-to-all(f32[56,16,128]{2,0,1:T(8,128)S(1)} %pad_maximum_fusion.6), channel_id=1, replica_groups=mesh['row'=8,'col'=16] {'col'}, dimensions={1} | all-to-all | bytes 917504 | tf_op jit(solution)/shard_map/all_to_all | solution.py:15
  600.9 11.2 %all_to_all.269 = f32[56,16,128]{2,0,1:T(8,128)S(1)} all-to-all(f32[56,16,128]{2,0,1:T(8,128)S(1)} %broadcast_in_dim.96), channel_id=1, replica_groups=mesh['row'=8,'col'=16] {'col'}, dimensions={1} | all-to-all | bytes 917504 | tf_op jit(solution)/shard_map/all_to_all | solution.py:17
  613.2 15.0 %all_to_all.270 = f32[32,8,256]{2,0,1:T(8,128)S(1)} all-to-all(f32[32,8,256]{2,0,1:T(8,128)S(1)} %bitcast.433), channel_id=1, replica_groups=mesh['row'=8,'col'=16] {'row'}, dimensions={1} | all-to-all | bytes 524288 | tf_op jit(solution)/shard_map/all_to_all | solution.py:15
  662.6 13.7 %shard_map.66 = (f32[2,24,2048]{2,1,0:T(8,128)}, f32[24,2048]{1,0:T(8,128)}, f32[24,128]{1,0:T(8,128)}) custom-call(s32[2]{0:T(128)} %fusion.56.flags_ref, f32[24,2048]{1,0:T(8,128)} %get-tuple-element.341.d_ref, f32[2,24,2048]{2,1,0:T(8,128)} %multiply_add_fusion.di_ref, bf16[2,1,2048,2048]{3,2,1,0:T(8,128)(2,1)} %bitcast.409), custom_call_target="tpu_custom_call" | custom-call | tf_op jit(solution)/shard_map/pallas_call | solution.py:70
  678.5 11.5 %all_to_all.273 = f32[56,16,128]{2,0,1:T(8,128)S(1)} all-to-all(f32[56,16,128]{2,0,1:T(8,128)S(1)} %pad_maximum_fusion.7), channel_id=1, replica_groups=mesh['row'=8,'col'=16] {'col'}, dimensions={1} | all-to-all | bytes 917504 | tf_op jit(solution)/shard_map/all_to_all | solution.py:15
  690.0 11.2 %all_to_all.274 = f32[56,16,128]{2,0,1:T(8,128)S(1)} all-to-all(f32[56,16,128]{2,0,1:T(8,128)S(1)} %broadcast_in_dim.99), channel_id=1, replica_groups=mesh['row'=8,'col'=16] {'col'}, dimensions={1} | all-to-all | bytes 917504 | tf_op jit(solution)/shard_map/all_to_all | solution.py:17
  702.3 15.0 %all_to_all.275 = f32[32,8,256]{2,0,1:T(8,128)S(1)} all-to-all(f32[32,8,256]{2,0,1:T(8,128)S(1)} %bitcast.434), channel_id=1, replica_groups=mesh['row'=8,'col'=16] {'row'}, dimensions={1} | all-to-all | bytes 524288 | tf_op jit(solution)/shard_map/all_to_all | solution.py:15
  (372 shorter events, 309.3 us)
Async XLA Ops:
  3.5 16.1 %all-to-all-start = ((f32[32,16,128]{2,0,1:T(8,128)}), f32[32,16,128]{2,0,1:T(8,128)S(1)}, u32[]{:S(2)}, u32[]{:S(2)}) async-start(f32[32,16,128]{2,0,1:T(8,128)} %copy.85), calls=%async_computation | async-start | bytes 524288 | tf_op jit(solution)/shard_map/all_to_all | solution.py:107
  12.1 90.5 %copy-start = (f32[24,2048]{1,0:T(8,128)S(1)}, f32[24,2048]{1,0:T(8,128)}, u32[]{:S(2)}) copy-start(f32[24,2048]{1,0:T(8,128)} %d_ref.1) | copy-start | bytes 589828
  12.1 90.5 %copy-start.14 = (f32[2048]{0:T(1024)S(1)}, f32[2048]{0:T(1024)}, u32[]{:S(2)}) copy-start(f32[2048]{0:T(1024)} %param.53) | copy-start | bytes 24580
  20.5 12.4 %all-to-all-start.1 = ((f32[48,16,128]{2,0,1:T(8,128)}), f32[48,16,128]{2,0,1:T(8,128)S(1)}, u32[]{:S(2)}, u32[]{:S(2)}) async-start(f32[48,16,128]{2,0,1:T(8,128)} %broadcast_in_dim.76), calls=%async_computation.1 | async-start | bytes 786432 | tf_op jit(solution)/shard_map/all_to_all | solution.py:112
  33.8 92.2 %copy-start.7 = (f32[2,24,2048]{2,1,0:T(8,128)S(1)}, f32[2,24,2048]{2,1,0:T(8,128)}, u32[]{:S(2)}) copy-start(f32[2,24,2048]{2,1,0:T(8,128)} %reshape.1204.di_ref) | copy-start | bytes 1179652
  61.9 12.2 %all-to-all-start.3 = ((f32[56,16,128]{2,0,1:T(8,128)}), f32[56,16,128]{2,0,1:T(8,128)S(1)}, u32[]{:S(2)}, u32[]{:S(2)}) async-start(f32[56,16,128]{2,0,1:T(8,128)} %broadcast_in_dim.77), calls=%async_computation.3 | async-start | bytes 917504 | tf_op jit(solution)/shard_map/all_to_all | solution.py:17
  91.6 10.8 %all-to-all-start.5 = ((f32[32,8,256]{2,0,1:T(8,128)}), f32[32,8,256]{2,0,1:T(8,128)S(1)}, u32[]{:S(2)}, u32[]{:S(2)}) async-start(f32[32,8,256]{2,0,1:T(8,128)} %broadcast_in_dim.79), calls=%async_computation.5 | async-start | bytes 524288 | tf_op jit(solution)/shard_map/all_to_all | solution.py:17
  114.0 11.8 %all-to-all-start.7 = ((f32[48,16,128]{2,0,1:T(8,128)}), f32[48,16,128]{2,0,1:T(8,128)S(1)}, u32[]{:S(2)}, u32[]{:S(2)}) async-start(f32[48,16,128]{2,0,1:T(8,128)} %broadcast_in_dim.80), calls=%async_computation.7 | async-start | bytes 786432 | tf_op jit(solution)/shard_map/all_to_all | solution.py:112
  118.5 73.3 %copy-start.1 = (f32[24,2048]{1,0:T(8,128)S(1)}, f32[24,2048]{1,0:T(8,128)}, u32[]{:S(2)}) copy-start(f32[24,2048]{1,0:T(8,128)} %get-tuple-element.365.d_ref) | copy-start | bytes 589828
  126.9 88.4 %copy-start.9 = (f32[2,24,2048]{2,1,0:T(8,128)S(1)}, f32[2,24,2048]{2,1,0:T(8,128)}, u32[]{:S(2)}) copy-start(f32[2,24,2048]{2,1,0:T(8,128)} %multiply_add_fusion.6.di_ref) | copy-start | bytes 1179652
  203.3 11.8 %all-to-all-start.13 = ((f32[48,16,128]{2,0,1:T(8,128)}), f32[48,16,128]{2,0,1:T(8,128)S(1)}, u32[]{:S(2)}, u32[]{:S(2)}) async-start(f32[48,16,128]{2,0,1:T(8,128)} %broadcast_in_dim.83), calls=%async_computation.13 | async-start | bytes 786432 | tf_op jit(solution)/shard_map/all_to_all | solution.py:112
  207.8 73.3 %copy-start.2 = (f32[24,2048]{1,0:T(8,128)S(1)}, f32[24,2048]{1,0:T(8,128)}, u32[]{:S(2)}) copy-start(f32[24,2048]{1,0:T(8,128)} %get-tuple-element.361.d_ref) | copy-start | bytes 589828
  216.1 88.4 %copy-start.10 = (f32[2,24,2048]{2,1,0:T(8,128)S(1)}, f32[2,24,2048]{2,1,0:T(8,128)}, u32[]{:S(2)}) copy-start(f32[2,24,2048]{2,1,0:T(8,128)} %multiply_add_fusion.5.di_ref) | copy-start | bytes 1179652
  292.5 11.8 %all-to-all-start.19 = ((f32[48,16,128]{2,0,1:T(8,128)}), f32[48,16,128]{2,0,1:T(8,128)S(1)}, u32[]{:S(2)}, u32[]{:S(2)}) async-start(f32[48,16,128]{2,0,1:T(8,128)} %broadcast_in_dim.86), calls=%async_computation.19 | async-start | bytes 786432 | tf_op jit(solution)/shard_map/all_to_all | solution.py:112
  297.2 73.1 %copy-start.3 = (f32[24,2048]{1,0:T(8,128)S(1)}, f32[24,2048]{1,0:T(8,128)}, u32[]{:S(2)}) copy-start(f32[24,2048]{1,0:T(8,128)} %get-tuple-element.357.d_ref) | copy-start | bytes 589828
  305.4 88.4 %copy-start.11 = (f32[2,24,2048]{2,1,0:T(8,128)S(1)}, f32[2,24,2048]{2,1,0:T(8,128)}, u32[]{:S(2)}) copy-start(f32[2,24,2048]{2,1,0:T(8,128)} %multiply_add_fusion.4.di_ref) | copy-start | bytes 1179652
  381.8 11.8 %all-to-all-start.25 = ((f32[48,16,128]{2,0,1:T(8,128)}), f32[48,16,128]{2,0,1:T(8,128)S(1)}, u32[]{:S(2)}, u32[]{:S(2)}) async-start(f32[48,16,128]{2,0,1:T(8,128)} %broadcast_in_dim.89), calls=%async_computation.25 | async-start | bytes 786432 | tf_op jit(solution)/shard_map/all_to_all | solution.py:112
  386.2 73.3 %copy-start.4 = (f32[24,2048]{1,0:T(8,128)S(1)}, f32[24,2048]{1,0:T(8,128)}, u32[]{:S(2)}) copy-start(f32[24,2048]{1,0:T(8,128)} %get-tuple-element.353.d_ref) | copy-start | bytes 589828
  394.6 88.4 %copy-start.12 = (f32[2,24,2048]{2,1,0:T(8,128)S(1)}, f32[2,24,2048]{2,1,0:T(8,128)}, u32[]{:S(2)}) copy-start(f32[2,24,2048]{2,1,0:T(8,128)} %multiply_add_fusion.3.di_ref) | copy-start | bytes 1179652
  471.0 11.8 %all-to-all-start.31 = ((f32[48,16,128]{2,0,1:T(8,128)}), f32[48,16,128]{2,0,1:T(8,128)S(1)}, u32[]{:S(2)}, u32[]{:S(2)}) async-start(f32[48,16,128]{2,0,1:T(8,128)} %broadcast_in_dim.92), calls=%async_computation.31 | async-start | bytes 786432 | tf_op jit(solution)/shard_map/all_to_all | solution.py:112
  475.5 73.3 %copy-start.5 = (f32[24,2048]{1,0:T(8,128)S(1)}, f32[24,2048]{1,0:T(8,128)}, u32[]{:S(2)}) copy-start(f32[24,2048]{1,0:T(8,128)} %get-tuple-element.349.d_ref) | copy-start | bytes 589828
  483.9 88.4 %copy-start.13 = (f32[2,24,2048]{2,1,0:T(8,128)S(1)}, f32[2,24,2048]{2,1,0:T(8,128)}, u32[]{:S(2)}) copy-start(f32[2,24,2048]{2,1,0:T(8,128)} %multiply_add_fusion.2.di_ref) | copy-start | bytes 1179652
  560.3 11.8 %all-to-all-start.37 = ((f32[48,16,128]{2,0,1:T(8,128)}), f32[48,16,128]{2,0,1:T(8,128)S(1)}, u32[]{:S(2)}, u32[]{:S(2)}) async-start(f32[48,16,128]{2,0,1:T(8,128)} %broadcast_in_dim.95), calls=%async_computation.37 | async-start | bytes 786432 | tf_op jit(solution)/shard_map/all_to_all | solution.py:112
  564.8 73.5 %copy-start.6 = (f32[24,2048]{1,0:T(8,128)S(1)}, f32[24,2048]{1,0:T(8,128)}, u32[]{:S(2)}) copy-start(f32[24,2048]{1,0:T(8,128)} %get-tuple-element.345.d_ref) | copy-start | bytes 589828
  573.1 88.6 %copy-start.8 = (f32[2,24,2048]{2,1,0:T(8,128)S(1)}, f32[2,24,2048]{2,1,0:T(8,128)}, u32[]{:S(2)}) copy-start(f32[2,24,2048]{2,1,0:T(8,128)} %multiply_add_fusion.1.di_ref) | copy-start | bytes 1179652
  649.7 11.8 %all-to-all-start.43 = ((f32[48,16,128]{2,0,1:T(8,128)}), f32[48,16,128]{2,0,1:T(8,128)S(1)}, u32[]{:S(2)}, u32[]{:S(2)}) async-start(f32[48,16,128]{2,0,1:T(8,128)} %broadcast_in_dim.98), calls=%async_computation.43 | async-start | bytes 786432 | tf_op jit(solution)/shard_map/all_to_all | solution.py:112
  654.2 73.2 %copy-start.15 = (f32[24,2048]{1,0:T(8,128)S(1)}, f32[24,2048]{1,0:T(8,128)}, u32[]{:S(2)}) copy-start(f32[24,2048]{1,0:T(8,128)} %get-tuple-element.341.d_ref) | copy-start | bytes 589828

commit v7 on v6

--- a/solution.py
+++ b/solution.py
@@ -79,6 +79,12 @@
     )(flags, d, di, blocks)
 
 
+def scalar_tail(scalars, n, w):
+    return jnp.zeros((PAD, n, w), jnp.float32).at[0, :, : scalars.shape[0]].set(
+        jnp.broadcast_to(scalars, (n, scalars.shape[0]))
+    )
+
+
 def pack(blocks, scalars):
     width = blocks[0].shape[1]
     tail = jnp.zeros((PAD, width), jnp.float32).at[0, : scalars.shape[0]].set(scalars)
@@ -95,15 +101,11 @@
         col = lax.axis_index("col")
         first_row = lax.axis_index("row") == 0
         flags = (col >= rows).astype(jnp.int32)
-        owner = [col == rows[k] for k in range(nb)]
         noise = noise_var[None, :]
 
         def fetch(res):
             w = width // n_col
-            tail = jnp.zeros((PAD, n_col, w), jnp.float32).at[0, :, :vecs].set(
-                jnp.broadcast_to(jnp.sum(res * res, axis=1), (n_col, vecs))
-            )
-            x = jnp.concatenate([res.reshape(vecs, n_col, w), tail], axis=0)
+            x = jnp.concatenate([res.reshape(vecs, n_col, w), scalar_tail(jnp.sum(res * res, axis=1), n_col, w)], axis=0)
             y = lax.all_to_all(x, "col", 1, 1, tiled=True)
             norm = jnp.sum(y[vecs, :, :vecs], axis=0)
             kept = jnp.concatenate(
@@ -121,13 +123,24 @@
             forward = [fwd[k] for k in range(nb)]
             part = jnp.sum(lanes, axis=1)
             part = part + jnp.where(first_row, jnp.sum(direction * (noise * direction), axis=1), 0.0)
-            out = all_reduce(pack(forward, part), "col", n_col)
-            terms = mirrored
+            w = width // n_col
+            x = jnp.concatenate([fwd.reshape(nb * vecs, n_col, w), scalar_tail(part, n_col, w)], axis=0)
+            s = jnp.sum(lax.all_to_all(x, "col", 1, 1, tiled=True), axis=1)
+            chunks = s[: nb * vecs].reshape(nb, vecs, w)
+            dest = jnp.arange(n_col, dtype=jnp.int32)[None, :, None]
+            send = jnp.zeros((vecs, n_col, w), jnp.float32)
             for k in range(nb):
-                terms = terms + jnp.where(owner[k], out[k * vecs:(k + 1) * vecs], 0.0)
-            out = all_reduce(pack([terms], out[nb * vecs, :vecs]), "row", n_row)
-            image = noise * direction + out[:vecs]
-            curvature = out[vecs, :vecs]
+                send = jnp.where(dest == rows[k], chunks[k][:, None, :], send)
+            owned = lax.all_to_all(send, "col", 1, 1, tiled=True).reshape(vecs, width)
+            terms = mirrored + owned
+            w = width // n_row
+            x = jnp.concatenate([terms.reshape(vecs, n_row, w), scalar_tail(s[nb * vecs, :vecs], n_row, w)], axis=0)
+            s = jnp.sum(lax.all_to_all(x, "row", 1, 1, tiled=True), axis=1)
+            curvature = s[vecs, :vecs]
+            kernel_part = lax.all_to_all(
+                jnp.broadcast_to(s[:vecs][:, None, :], (vecs, n_row, w)), "row", 1, 1, tiled=True
+            ).reshape(vecs, width)
+            image = noise * direction + kernel_part
             alpha = norm_now / curvature
             solution = solution + alpha[:, None] * direction
             residual = residual - alpha[:, None] * image

time: 733 us -> 739 us (level)
  blocking collectives: 433 us -> 254 us
  waiting for transfers between devices: 74.7 us -> 179 us
  starting transfers between devices: 45.5 us -> 113 us
  other arithmetic: 32.9 us -> 41.4 us
    all_to_all x30 -> x14, blocking collectives: 360 us -> 182 us  [the longest x7 101 us: on_device(): s = jnp.sum(lax.all_to_all(x, 'row', 1, 1, tiled=True), axis=1)]
    all_to_all x2 -> x18, waiting for transfers between devices: 13.9 us -> 118 us  [the longest x8 57 us: on_device(): owned = lax.all_to_all(send, 'col', 1, 1, tiled=True).reshape(vecs, width)]
    all_to_all x2 -> x18, starting transfers between devices: 7.91 us -> 75.9 us  [the longest x8 34.7 us: on_device(): lax.all_to_all(jnp.broadcast_to(s[:vecs][:, None, :], (vecs, n_row, w)),...]
  transfers between devices with their start and end apart: 11 -> 27, of which waited for: 11 -> 27; matrix products, arithmetic and copies ran while one was open for 1% -> 1% of each run, Pallas kernels for 0% -> 0%
where the time goes in v7:
time: 739 us; the launch traced here: 733 us
  blocking collectives  254 us (34%)
  waiting for transfers between devices  179 us (24%)
  starting transfers between devices  113 us (15%)
  Pallas kernels  111 us (15%)
  other arithmetic  41.4 us (6%)
  local copies, waits for them, and re-layouts  27.6 us (4%)
    pallas_call x8, Pallas kernels, block_products(): pl.pallas_call(products_kernel, grid_spec=grid_spec, out_shape=[jax.Shape...  111 us
    all_to_all x7, blocking collectives, on_device(): s = jnp.sum(lax.all_to_all(x, 'row', 1, 1, tiled=True), axis=1)  101 us
    all_to_all x7, blocking collectives, on_device(): s = jnp.sum(lax.all_to_all(x, 'col', 1, 1, tiled=True), axis=1)  80.3 us
    all_to_all x7, blocking collectives, fetch(): y = lax.all_to_all(x, 'col', 1, 1, tiled=True)  72.7 us
    all_to_all x8, waiting for transfers between devices, fetch(): lax.all_to_all(jnp.broadcast_to(kept[:, None, :], (nb * vecs, n_col, w)),...  58.7 us
    all_to_all x8, waiting for transfers between devices, on_device(): owned = lax.all_to_all(send, 'col', 1, 1, tiled=True).reshape(vecs, width)  57 us
    all_to_all x8, waiting for transfers between devices, on_device(): lax.all_to_all(jnp.broadcast_to(s[:vecs][:, None, :], (vecs, n_row, w)),...  47 us
    all_to_all x8, starting transfers between devices, on_device(): lax.all_to_all(jnp.broadcast_to(s[:vecs][:, None, :], (vecs, n_row, w)),...  34.7 us
  transfers between devices with their start and end apart: 27, of which 27 were waited for; matrix products, arithmetic and copies ran while one was open for 1% of the time, Pallas kernels for 0%

profile of v7, /device:TPU:1, one launch (start us, length us, event | category | flops | bytes accessed | tf_op | source)
XLA Modules:
  0.0 732.6 jit_solution(14390169442438794854)
XLA Ops:
  3.6 8.6 %all-to-all-start = ((f32[32,16,128]{2,0,1:T(8,128)}), f32[32,16,128]{2,0,1:T(8,128)S(1)}, u32[]{:S(2)}, u32[]{:S(2)}) async-start(f32[32,16,128]{2,0,1:T(8,128)} %copy.53), calls=%async_computation | async-start | bytes 524288 | tf_op jit(solution)/shard_map/all_to_all | solution.py:109
  33.9 13.9 %shard_map.59 = (f32[2,24,2048]{2,1,0:T(8,128)}, f32[24,2048]{1,0:T(8,128)}, f32[24,128]{1,0:T(8,128)}) custom-call(s32[2]{0:T(128)} %fusion.40.flags_ref, f32[24,2048]{1,0:T(8,128)} %d_ref.1, f32[2,24,2048]{2,1,0:T(8,128)} %reshape.1332.di_ref, bf16[2,1,2048,2048]{3,2,1,0:T(8,128)(2,1)} %bitcast.242), custom_call_target="tpu_custom_call" | custom-call | tf_op jit(solution)/shard_map/pallas_call | solution.py:70
  75.9 9.2 %all-to-all-start.4 = ((f32[32,8,256]{2,0,1:T(8,128)}), f32[32,8,256]{2,0,1:T(8,128)S(1)}, u32[]{:S(2)}, u32[]{:S(2)}) async-start(f32[32,8,256]{2,0,1:T(8,128)} %pad_maximum_fusion.9), calls=%async_computation.4 | async-start | bytes 524288 | tf_op jit(solution)/shard_map/all_to_all | solution.py:138
  102.9 10.4 %all_to_all.240 = f32[32,16,128]{2,0,1:T(8,128)S(1)} all-to-all(f32[32,16,128]{2,0,1:T(8,128)S(1)} %pad_maximum_fusion.10), channel_id=1, replica_groups=mesh['row'=8,'col'=16] {'col'}, dimensions={1} | all-to-all | bytes 524288 | tf_op jit(solution)/shard_map/all_to_all | solution.py:109
  127.0 13.9 %shard_map.60 = (f32[2,24,2048]{2,1,0:T(8,128)}, f32[24,2048]{1,0:T(8,128)}, f32[24,128]{1,0:T(8,128)}) custom-call(s32[2]{0:T(128)} %fusion.40.flags_ref, f32[24,2048]{1,0:T(8,128)} %get-tuple-element.365.d_ref, f32[2,24,2048]{2,1,0:T(8,128)} %multiply_add_fusion.6.di_ref, bf16[2,1,2048,2048]{3,2,1,0:T(8,128)(2,1)} %bitcast.243), custom_call_target="tpu_custom_call" | custom-call | tf_op jit(solution)/shard_map/pallas_call | solution.py:70
  143.0 11.5 %all_to_all.241 = f32[56,16,128]{2,0,1:T(8,128)S(1)} all-to-all(f32[56,16,128]{2,0,1:T(8,128)S(1)} %pad_maximum_fusion.1), channel_id=1, replica_groups=mesh['row'=8,'col'=16] {'col'}, dimensions={1} | all-to-all | bytes 917504 | tf_op jit(solution)/shard_map/all_to_all | solution.py:128
  167.0 14.5 %all_to_all.242 = f32[32,8,256]{2,0,1:T(8,128)S(1)} all-to-all(f32[32,8,256]{2,0,1:T(8,128)S(1)} %pad_maximum_fusion.11), channel_id=1, replica_groups=mesh['row'=8,'col'=16] {'row'}, dimensions={1} | all-to-all | bytes 524288 | tf_op jit(solution)/shard_map/all_to_all | solution.py:138
  192.7 10.4 %all_to_all.243 = f32[32,16,128]{2,0,1:T(8,128)S(1)} all-to-all(f32[32,16,128]{2,0,1:T(8,128)S(1)} %pad_maximum_fusion.12), channel_id=1, replica_groups=mesh['row'=8,'col'=16] {'col'}, dimensions={1} | all-to-all | bytes 524288 | tf_op jit(solution)/shard_map/all_to_all | solution.py:109
  216.9 13.9 %shard_map.61 = (f32[2,24,2048]{2,1,0:T(8,128)}, f32[24,2048]{1,0:T(8,128)}, f32[24,128]{1,0:T(8,128)}) custom-call(s32[2]{0:T(128)} %fusion.40.flags_ref, f32[24,2048]{1,0:T(8,128)} %get-tuple-element.361.d_ref, f32[2,24,2048]{2,1,0:T(8,128)} %multiply_add_fusion.5.di_ref, bf16[2,1,2048,2048]{3,2,1,0:T(8,128)(2,1)} %bitcast.244), custom_call_target="tpu_custom_call" | custom-call | tf_op jit(solution)/shard_map/pallas_call | solution.py:70
  232.9 11.5 %all_to_all.244 = f32[56,16,128]{2,0,1:T(8,128)S(1)} all-to-all(f32[56,16,128]{2,0,1:T(8,128)S(1)} %pad_maximum_fusion.2), channel_id=1, replica_groups=mesh['row'=8,'col'=16] {'col'}, dimensions={1} | all-to-all | bytes 917504 | tf_op jit(solution)/shard_map/all_to_all | solution.py:128
  256.9 14.5 %all_to_all.245 = f32[32,8,256]{2,0,1:T(8,128)S(1)} all-to-all(f32[32,8,256]{2,0,1:T(8,128)S(1)} %pad_maximum_fusion.13), channel_id=1, replica_groups=mesh['row'=8,'col'=16] {'row'}, dimensions={1} | all-to-all | bytes 524288 | tf_op jit(solution)/shard_map/all_to_all | solution.py:138
  282.6 10.4 %all_to_all.246 = f32[32,16,128]{2,0,1:T(8,128)S(1)} all-to-all(f32[32,16,128]{2,0,1:T(8,128)S(1)} %pad_maximum_fusion.14), channel_id=1, replica_groups=mesh['row'=8,'col'=16] {'col'}, dimensions={1} | all-to-all | bytes 524288 | tf_op jit(solution)/shard_map/all_to_all | solution.py:109
  306.7 13.9 %shard_map.62 = (f32[2,24,2048]{2,1,0:T(8,128)}, f32[24,2048]{1,0:T(8,128)}, f32[24,128]{1,0:T(8,128)}) custom-call(s32[2]{0:T(128)} %fusion.40.flags_ref, f32[24,2048]{1,0:T(8,128)} %get-tuple-element.357.d_ref, f32[2,24,2048]{2,1,0:T(8,128)} %multiply_add_fusion.4.di_ref, bf16[2,1,2048,2048]{3,2,1,0:T(8,128)(2,1)} %bitcast.245), custom_call_target="tpu_custom_call" | custom-call | tf_op jit(solution)/shard_map/pallas_call | solution.py:70
  322.7 11.5 %all_to_all.247 = f32[56,16,128]{2,0,1:T(8,128)S(1)} all-to-all(f32[56,16,128]{2,0,1:T(8,128)S(1)} %pad_maximum_fusion.3), channel_id=1, replica_groups=mesh['row'=8,'col'=16] {'col'}, dimensions={1} | all-to-all | bytes 917504 | tf_op jit(solution)/shard_map/all_to_all | solution.py:128
  346.7 14.5 %all_to_all.248 = f32[32,8,256]{2,0,1:T(8,128)S(1)} all-to-all(f32[32,8,256]{2,0,1:T(8,128)S(1)} %pad_maximum_fusion.15), channel_id=1, replica_groups=mesh['row'=8,'col'=16] {'row'}, dimensions={1} | all-to-all | bytes 524288 | tf_op jit(solution)/shard_map/all_to_all | solution.py:138
  372.4 10.4 %all_to_all.249 = f32[32,16,128]{2,0,1:T(8,128)S(1)} all-to-all(f32[32,16,128]{2,0,1:T(8,128)S(1)} %pad_maximum_fusion.16), channel_id=1, replica_groups=mesh['row'=8,'col'=16] {'col'}, dimensions={1} | all-to-all | bytes 524288 | tf_op jit(solution)/shard_map/all_to_all | solution.py:109
  388.1 7.4 %all-to-all-done.25 = f32[48,16,128]{2,0,1:T(8,128)S(1)} async-done(((f32[48,16,128]{2,0,1:T(8,128)}), f32[48,16,128]{2,0,1:T(8,128)S(1)}, u32[]{:S(2)}, u32[]{:S(2)}) %all-to-all-start.25) | async-done | bytes 393248 | tf_op jit(solution)/shard_map/all_to_all | solution.py:114
  396.6 13.9 %shard_map.63 = (f32[2,24,2048]{2,1,0:T(8,128)}, f32[24,2048]{1,0:T(8,128)}, f32[24,128]{1,0:T(8,128)}) custom-call(s32[2]{0:T(128)} %fusion.40.flags_ref, f32[24,2048]{1,0:T(8,128)} %get-tuple-element.353.d_ref, f32[2,24,2048]{2,1,0:T(8,128)} %multiply_add_fusion.3.di_ref, bf16[2,1,2048,2048]{3,2,1,0:T(8,128)(2,1)} %bitcast.246), custom_call_target="tpu_custom_call" | custom-call | tf_op jit(solution)/shard_map/pallas_call | solution.py:70
  412.6 11.5 %all_to_all.250 = f32[56,16,128]{2,0,1:T(8,128)S(1)} all-to-all(f32[56,16,128]{2,0,1:T(8,128)S(1)} %pad_maximum_fusion.4), channel_id=1, replica_groups=mesh['row'=8,'col'=16] {'col'}, dimensions={1} | all-to-all | bytes 917504 | tf_op jit(solution)/shard_map/all_to_all | solution.py:128
  436.5 14.5 %all_to_all.251 = f32[32,8,256]{2,0,1:T(8,128)S(1)} all-to-all(f32[32,8,256]{2,0,1:T(8,128)S(1)} %pad_maximum_fusion.17), channel_id=1, replica_groups=mesh['row'=8,'col'=16] {'row'}, dimensions={1} | all-to-all | bytes 524288 | tf_op jit(solution)/shard_map/all_to_all | solution.py:138
  462.3 10.4 %all_to_all.252 = f32[32,16,128]{2,0,1:T(8,128)S(1)} all-to-all(f32[32,16,128]{2,0,1:T(8,128)S(1)} %pad_maximum_fusion.18), channel_id=1, replica_groups=mesh['row'=8,'col'=16] {'col'}, dimensions={1} | all-to-all | bytes 524288 | tf_op jit(solution)/shard_map/all_to_all | solution.py:109
  486.4 13.9 %shard_map.64 = (f32[2,24,2048]{2,1,0:T(8,128)}, f32[24,2048]{1,0:T(8,128)}, f32[24,128]{1,0:T(8,128)}) custom-call(s32[2]{0:T(128)} %fusion.40.flags_ref, f32[24,2048]{1,0:T(8,128)} %get-tuple-element.349.d_ref, f32[2,24,2048]{2,1,0:T(8,128)} %multiply_add_fusion.2.di_ref, bf16[2,1,2048,2048]{3,2,1,0:T(8,128)(2,1)} %bitcast.247), custom_call_target="tpu_custom_call" | custom-call | tf_op jit(solution)/shard_map/pallas_call | solution.py:70
  502.4 11.5 %all_to_all.253 = f32[56,16,128]{2,0,1:T(8,128)S(1)} all-to-all(f32[56,16,128]{2,0,1:T(8,128)S(1)} %pad_maximum_fusion.5), channel_id=1, replica_groups=mesh['row'=8,'col'=16] {'col'}, dimensions={1} | all-to-all | bytes 917504 | tf_op jit(solution)/shard_map/all_to_all | solution.py:128
  526.4 14.5 %all_to_all.254 = f32[32,8,256]{2,0,1:T(8,128)S(1)} all-to-all(f32[32,8,256]{2,0,1:T(8,128)S(1)} %pad_maximum_fusion.19), channel_id=1, replica_groups=mesh['row'=8,'col'=16] {'row'}, dimensions={1} | all-to-all | bytes 524288 | tf_op jit(solution)/shard_map/all_to_all | solution.py:138
  552.1 10.4 %all_to_all.255 = f32[32,16,128]{2,0,1:T(8,128)S(1)} all-to-all(f32[32,16,128]{2,0,1:T(8,128)S(1)} %pad_maximum_fusion.20), channel_id=1, replica_groups=mesh['row'=8,'col'=16] {'col'}, dimensions={1} | all-to-all | bytes 524288 | tf_op jit(solution)/shard_map/all_to_all | solution.py:109
  576.3 13.9 %shard_map.65 = (f32[2,24,2048]{2,1,0:T(8,128)}, f32[24,2048]{1,0:T(8,128)}, f32[24,128]{1,0:T(8,128)}) custom-call(s32[2]{0:T(128)} %fusion.40.flags_ref, f32[24,2048]{1,0:T(8,128)} %get-tuple-element.345.d_ref, f32[2,24,2048]{2,1,0:T(8,128)} %multiply_add_fusion.1.di_ref, bf16[2,1,2048,2048]{3,2,1,0:T(8,128)(2,1)} %bitcast.248), custom_call_target="tpu_custom_call" | custom-call | tf_op jit(solution)/shard_map/pallas_call | solution.py:70
  592.2 11.5 %all_to_all.256 = f32[56,16,128]{2,0,1:T(8,128)S(1)} all-to-all(f32[56,16,128]{2,0,1:T(8,128)S(1)} %pad_maximum_fusion.6), channel_id=1, replica_groups=mesh['row'=8,'col'=16] {'col'}, dimensions={1} | all-to-all | bytes 917504 | tf_op jit(solution)/shard_map/all_to_all | solution.py:128
  616.5 14.5 %all_to_all.257 = f32[32,8,256]{2,0,1:T(8,128)S(1)} all-to-all(f32[32,8,256]{2,0,1:T(8,128)S(1)} %pad_maximum_fusion.21), channel_id=1, replica_groups=mesh['row'=8,'col'=16] {'row'}, dimensions={1} | all-to-all | bytes 524288 | tf_op jit(solution)/shard_map/all_to_all | solution.py:138
  642.2 10.4 %all_to_all.258 = f32[32,16,128]{2,0,1:T(8,128)S(1)} all-to-all(f32[32,16,128]{2,0,1:T(8,128)S(1)} %pad_maximum_fusion.22), channel_id=1, replica_groups=mesh['row'=8,'col'=16] {'col'}, dimensions={1} | all-to-all | bytes 524288 | tf_op jit(solution)/shard_map/all_to_all | solution.py:109
  666.3 13.7 %shard_map.66 = (f32[2,24,2048]{2,1,0:T(8,128)}, f32[24,2048]{1,0:T(8,128)}, f32[24,128]{1,0:T(8,128)}) custom-call(s32[2]{0:T(128)} %fusion.40.flags_ref, f32[24,2048]{1,0:T(8,128)} %get-tuple-element.341.d_ref, f32[2,24,2048]{2,1,0:T(8,128)} %multiply_add_fusion.di_ref, bf16[2,1,2048,2048]{3,2,1,0:T(8,128)(2,1)} %bitcast.249), custom_call_target="tpu_custom_call" | custom-call | tf_op jit(solution)/shard_map/pallas_call | solution.py:70
  682.2 11.5 %all_to_all.259 = f32[56,16,128]{2,0,1:T(8,128)S(1)} all-to-all(f32[56,16,128]{2,0,1:T(8,128)S(1)} %pad_maximum_fusion.7), channel_id=1, replica_groups=mesh['row'=8,'col'=16] {'col'}, dimensions={1} | all-to-all | bytes 917504 | tf_op jit(solution)/shard_map/all_to_all | solution.py:128
  706.2 14.5 %all_to_all.260 = f32[32,8,256]{2,0,1:T(8,128)S(1)} all-to-all(f32[32,8,256]{2,0,1:T(8,128)S(1)} %pad_maximum_fusion.23), channel_id=1, replica_groups=mesh['row'=8,'col'=16] {'row'}, dimensions={1} | all-to-all | bytes 524288 | tf_op jit(solution)/shard_map/all_to_all | solution.py:138
  (373 shorter events, 336.5 us)
Async XLA Ops:
  0.6 102.0 %copy-start.14 = (f32[2048]{0:T(1024)S(1)}, f32[2048]{0:T(1024)}, u32[]{:S(2)}) copy-start(f32[2048]{0:T(1024)} %param.53) | copy-start | bytes 24580
  0.6 102.0 %copy-start = (f32[24,2048]{1,0:T(8,128)S(1)}, f32[24,2048]{1,0:T(8,128)}, u32[]{:S(2)}) copy-start(f32[24,2048]{1,0:T(8,128)} %d_ref.1) | copy-start | bytes 589828
  3.6 16.1 %all-to-all-start = ((f32[32,16,128]{2,0,1:T(8,128)}), f32[32,16,128]{2,0,1:T(8,128)S(1)}, u32[]{:S(2)}, u32[]{:S(2)}) async-start(f32[32,16,128]{2,0,1:T(8,128)} %copy.53), calls=%async_computation | async-start | bytes 524288 | tf_op jit(solution)/shard_map/all_to_all | solution.py:109
  20.5 12.4 %all-to-all-start.1 = ((f32[48,16,128]{2,0,1:T(8,128)}), f32[48,16,128]{2,0,1:T(8,128)S(1)}, u32[]{:S(2)}, u32[]{:S(2)}) async-start(f32[48,16,128]{2,0,1:T(8,128)} %broadcast_in_dim.306), calls=%async_computation.1 | async-start | bytes 786432 | tf_op jit(solution)/shard_map/all_to_all | solution.py:114
  33.9 92.3 %copy-start.7 = (f32[2,24,2048]{2,1,0:T(8,128)S(1)}, f32[2,24,2048]{2,1,0:T(8,128)}, u32[]{:S(2)}) copy-start(f32[2,24,2048]{2,1,0:T(8,128)} %reshape.1332.di_ref) | copy-start | bytes 1179652
  50.6 12.1 %all-to-all-start.2 = ((f32[56,16,128]{2,0,1:T(8,128)}), f32[56,16,128]{2,0,1:T(8,128)S(1)}, u32[]{:S(2)}, u32[]{:S(2)}) async-start(f32[56,16,128]{2,0,1:T(8,128)} %pad_maximum_fusion), calls=%async_computation.2 | async-start | bytes 917504 | tf_op jit(solution)/shard_map/all_to_all | solution.py:128
  63.6 10.7 %all-to-all-start.3 = ((f32[24,16,128]{2,0,1:T(8,128)}), f32[24,16,128]{2,0,1:T(8,128)S(1)}, u32[]{:S(2)}, u32[]{:S(2)}) async-start(f32[24,16,128]{2,0,1:T(8,128)} %select_select_fusion.7), calls=%async_computation.3 | async-start | bytes 393216 | tf_op jit(solution)/shard_map/all_to_all | solution.py:134
  75.9 15.7 %all-to-all-start.4 = ((f32[32,8,256]{2,0,1:T(8,128)}), f32[32,8,256]{2,0,1:T(8,128)S(1)}, u32[]{:S(2)}, u32[]{:S(2)}) async-start(f32[32,8,256]{2,0,1:T(8,128)} %pad_maximum_fusion.9), calls=%async_computation.4 | async-start | bytes 524288 | tf_op jit(solution)/shard_map/all_to_all | solution.py:138
  92.4 10.2 %all-to-all-start.5 = ((f32[24,8,256]{2,0,1:T(8,128)}), f32[24,8,256]{2,0,1:T(8,128)S(1)}, u32[]{:S(2)}, u32[]{:S(2)}) async-start(f32[24,8,256]{2,0,1:T(8,128)} %broadcast_in_dim.311), calls=%async_computation.5 | async-start | bytes 393216 | tf_op jit(solution)/shard_map/all_to_all | solution.py:140
  114.1 11.9 %all-to-all-start.7 = ((f32[48,16,128]{2,0,1:T(8,128)}), f32[48,16,128]{2,0,1:T(8,128)S(1)}, u32[]{:S(2)}, u32[]{:S(2)}) async-start(f32[48,16,128]{2,0,1:T(8,128)} %broadcast_in_dim.312), calls=%async_computation.7 | async-start | bytes 786432 | tf_op jit(solution)/shard_map/all_to_all | solution.py:114
  155.3 10.7 %all-to-all-start.9 = ((f32[24,16,128]{2,0,1:T(8,128)}), f32[24,16,128]{2,0,1:T(8,128)S(1)}, u32[]{:S(2)}, u32[]{:S(2)}) async-start(f32[24,16,128]{2,0,1:T(8,128)} %select_select_fusion.6), calls=%async_computation.9 | async-start | bytes 393216 | tf_op jit(solution)/shard_map/all_to_all | solution.py:134
  182.2 10.2 %all-to-all-start.11 = ((f32[24,8,256]{2,0,1:T(8,128)}), f32[24,8,256]{2,0,1:T(8,128)S(1)}, u32[]{:S(2)}, u32[]{:S(2)}) async-start(f32[24,8,256]{2,0,1:T(8,128)} %broadcast_in_dim.315), calls=%async_computation.11 | async-start | bytes 393216 | tf_op jit(solution)/shard_map/all_to_all | solution.py:140
  204.0 11.9 %all-to-all-start.13 = ((f32[48,16,128]{2,0,1:T(8,128)}), f32[48,16,128]{2,0,1:T(8,128)S(1)}, u32[]{:S(2)}, u32[]{:S(2)}) async-start(f32[48,16,128]{2,0,1:T(8,128)} %broadcast_in_dim.316), calls=%async_computation.13 | async-start | bytes 786432 | tf_op jit(solution)/shard_map/all_to_all | solution.py:114
  245.2 10.7 %all-to-all-start.15 = ((f32[24,16,128]{2,0,1:T(8,128)}), f32[24,16,128]{2,0,1:T(8,128)S(1)}, u32[]{:S(2)}, u32[]{:S(2)}) async-start(f32[24,16,128]{2,0,1:T(8,128)} %select_select_fusion.5), calls=%async_computation.15 | async-start | bytes 393216 | tf_op jit(solution)/shard_map/all_to_all | solution.py:134
  272.1 10.2 %all-to-all-start.17 = ((f32[24,8,256]{2,0,1:T(8,128)}), f32[24,8,256]{2,0,1:T(8,128)S(1)}, u32[]{:S(2)}, u32[]{:S(2)}) async-start(f32[24,8,256]{2,0,1:T(8,128)} %broadcast_in_dim.319), calls=%async_computation.17 | async-start | bytes 393216 | tf_op jit(solution)/shard_map/all_to_all | solution.py:140
  293.8 11.9 %all-to-all-start.19 = ((f32[48,16,128]{2,0,1:T(8,128)}), f32[48,16,128]{2,0,1:T(8,128)S(1)}, u32[]{:S(2)}, u32[]{:S(2)}) async-start(f32[48,16,128]{2,0,1:T(8,128)} %broadcast_in_dim.320), calls=%async_computation.19 | async-start | bytes 786432 | tf_op jit(solution)/shard_map/all_to_all | solution.py:114
  335.0 10.7 %all-to-all-start.21 = ((f32[24,16,128]{2,0,1:T(8,128)}), f32[24,16,128]{2,0,1:T(8,128)S(1)}, u32[]{:S(2)}, u32[]{:S(2)}) async-start(f32[24,16,128]{2,0,1:T(8,128)} %select_select_fusion.4), calls=%async_computation.21 | async-start | bytes 393216 | tf_op jit(solution)/shard_map/all_to_all | solution.py:134
  361.9 10.2 %all-to-all-start.23 = ((f32[24,8,256]{2,0,1:T(8,128)}), f32[24,8,256]{2,0,1:T(8,128)S(1)}, u32[]{:S(2)}, u32[]{:S(2)}) async-start(f32[24,8,256]{2,0,1:T(8,128)} %broadcast_in_dim.323), calls=%async_computation.23 | async-start | bytes 393216 | tf_op jit(solution)/shard_map/all_to_all | solution.py:140
  383.6 11.9 %all-to-all-start.25 = ((f32[48,16,128]{2,0,1:T(8,128)}), f32[48,16,128]{2,0,1:T(8,128)S(1)}, u32[]{:S(2)}, u32[]{:S(2)}) async-start(f32[48,16,128]{2,0,1:T(8,128)} %broadcast_in_dim.324), calls=%async_computation.25 | async-start | bytes 786432 | tf_op jit(solution)/shard_map/all_to_all | solution.py:114
  424.8 10.7 %all-to-all-start.27 = ((f32[24,16,128]{2,0,1:T(8,128)}), f32[24,16,128]{2,0,1:T(8,128)S(1)}, u32[]{:S(2)}, u32[]{:S(2)}) async-start(f32[24,16,128]{2,0,1:T(8,128)} %select_select_fusion.3), calls=%async_computation.27 | async-start | bytes 393216 | tf_op jit(solution)/shard_map/all_to_all | solution.py:134
  451.7 10.2 %all-to-all-start.29 = ((f32[24,8,256]{2,0,1:T(8,128)}), f32[24,8,256]{2,0,1:T(8,128)S(1)}, u32[]{:S(2)}, u32[]{:S(2)}) async-start(f32[24,8,256]{2,0,1:T(8,128)} %broadcast_in_dim.327), calls=%async_computation.29 | async-start | bytes 393216 | tf_op jit(solution)/shard_map/all_to_all | solution.py:140
  473.5 11.9 %all-to-all-start.31 = ((f32[48,16,128]{2,0,1:T(8,128)}), f32[48,16,128]{2,0,1:T(8,128)S(1)}, u32[]{:S(2)}, u32[]{:S(2)}) async-start(f32[48,16,128]{2,0,1:T(8,128)} %broadcast_in_dim.328), calls=%async_computation.31 | async-start | bytes 786432 | tf_op jit(solution)/shard_map/all_to_all | solution.py:114
  486.4 89.0 %copy-start.13 = (f32[2,24,2048]{2,1,0:T(8,128)S(1)}, f32[2,24,2048]{2,1,0:T(8,128)}, u32[]{:S(2)}) copy-start(f32[2,24,2048]{2,1,0:T(8,128)} %multiply_add_fusion.2.di_ref) | copy-start | bytes 1179652
  514.7 10.7 %all-to-all-start.33 = ((f32[24,16,128]{2,0,1:T(8,128)}), f32[24,16,128]{2,0,1:T(8,128)S(1)}, u32[]{:S(2)}, u32[]{:S(2)}) async-start(f32[24,16,128]{2,0,1:T(8,128)} %select_select_fusion.2), calls=%async_computation.33 | async-start | bytes 393216 | tf_op jit(solution)/shard_map/all_to_all | solution.py:134
  541.6 10.2 %all-to-all-start.35 = ((f32[24,8,256]{2,0,1:T(8,128)}), f32[24,8,256]{2,0,1:T(8,128)S(1)}, u32[]{:S(2)}, u32[]{:S(2)}) async-start(f32[24,8,256]{2,0,1:T(8,128)} %broadcast_in_dim.331), calls=%async_computation.35 | async-start | bytes 393216 | tf_op jit(solution)/shard_map/all_to_all | solution.py:140
  563.3 11.9 %all-to-all-start.37 = ((f32[48,16,128]{2,0,1:T(8,128)}), f32[48,16,128]{2,0,1:T(8,128)S(1)}, u32[]{:S(2)}, u32[]{:S(2)}) async-start(f32[48,16,128]{2,0,1:T(8,128)} %broadcast_in_dim.332), calls=%async_computation.37 | async-start | bytes 786432 | tf_op jit(solution)/shard_map/all_to_all | solution.py:114
  576.3 89.2 %copy-start.8 = (f32[2,24,2048]{2,1,0:T(8,128)S(1)}, f32[2,24,2048]{2,1,0:T(8,128)}, u32[]{:S(2)}) copy-start(f32[2,24,2048]{2,1,0:T(8,128)} %multiply_add_fusion.1.di_ref) | copy-start | bytes 1179652
  604.5 10.9 %all-to-all-start.39 = ((f32[24,16,128]{2,0,1:T(8,128)}), f32[24,16,128]{2,0,1:T(8,128)S(1)}, u32[]{:S(2)}, u32[]{:S(2)}) async-start(f32[24,16,128]{2,0,1:T(8,128)} %select_select_fusion.1), calls=%async_computation.39 | async-start | bytes 393216 | tf_op jit(solution)/shard_map/all_to_all | solution.py:134
  631.7 10.2 %all-to-all-start.41 = ((f32[24,8,256]{2,0,1:T(8,128)}), f32[24,8,256]{2,0,1:T(8,128)S(1)}, u32[]{:S(2)}, u32[]{:S(2)}) async-start(f32[24,8,256]{2,0,1:T(8,128)} %broadcast_in_dim.335), calls=%async_computation.41 | async-start | bytes 393216 | tf_op jit(solution)/shard_map/all_to_all | solution.py:140
  653.4 11.9 %all-to-all-start.43 = ((f32[48,16,128]{2,0,1:T(8,128)}), f32[48,16,128]{2,0,1:T(8,128)S(1)}, u32[]{:S(2)}, u32[]{:S(2)}) async-start(f32[48,16,128]{2,0,1:T(8,128)} %broadcast_in_dim.336), calls=%async_computation.43 | async-start | bytes 786432 | tf_op jit(solution)/shard_map/all_to_all | solution.py:114
  694.5 10.7 %all-to-all-start.45 = ((f32[24,16,128]{2,0,1:T(8,128)}), f32[24,16,128]{2,0,1:T(8,128)S(1)}, u32[]{:S(2)}, u32[]{:S(2)}) async-start(f32[24,16,128]{2,0,1:T(8,128)} %select_select_fusion), calls=%async_computation.45 | async-start | bytes 393216 | tf_op jit(solution)/shard_map/all_to_all | solution.py:134
  721.4 10.2 %all-to-all-start.47 = ((f32[24,8,256]{2,0,1:T(8,128)}), f32[24,8,256]{2,0,1:T(8,128)S(1)}, u32[]{:S(2)}, u32[]{:S(2)}) async-start(f32[24,8,256]{2,0,1:T(8,128)} %broadcast_in_dim.339), calls=%async_computation.47 | async-start | bytes 393216 | tf_op jit(solution)/shard_map/all_to_all | solution.py:140
  (11 other events, 872.8 us)

commit v8 on v6

--- a/solution.py
+++ b/solution.py
@@ -50,7 +50,7 @@
         p_ref[...] = acc
 
 
-def block_products(flags, d, di, blocks, tile=512):
+def block_products(flags, d, di, blocks, tile=1024):
     nb, _, order, _ = blocks.shape
     vecs = d.shape[0]
     grid_spec = pltpu.PrefetchScalarGridSpec(

time: 733 us -> 720 us (0.982)
  Pallas kernels: 111 us -> 98.5 us
    pallas_call x8, Pallas kernels: 111 us -> 98.5 us  [block_products(): pl.pallas_call(products_kernel, grid_spec=grid_spec, out_shape=[jax.Shape...]
where the time goes in v8:
time: 720 us; the launch traced here: 716 us
  blocking collectives  433 us (60%)
  Pallas kernels  98.5 us (14%)
  waiting for transfers between devices  74.7 us (10%)
  starting transfers between devices  45.6 us (6%)
  other arithmetic  32.9 us (5%)
  local copies, waits for them, and re-layouts  24.8 us (3%)
    all_to_all x16, blocking collectives, all_reduce(): y = lax.all_to_all(x.reshape(rows, n, w), axis, 1, 1, tiled=True)  212 us
    all_to_all x14, blocking collectives, all_reduce(): lax.all_to_all(jnp.broadcast_to(part[:, None, :], (rows, n, w)), axis, 1,...  148 us
    pallas_call x8, Pallas kernels, block_products(): pl.pallas_call(products_kernel, grid_spec=grid_spec, out_shape=[jax.Shape...  98.5 us
    all_to_all x7, blocking collectives, fetch(): y = lax.all_to_all(x, 'col', 1, 1, tiled=True)  72.4 us
    all_to_all x8, waiting for transfers between devices, fetch(): lax.all_to_all(jnp.broadcast_to(kept[:, None, :], (nb * vecs, n_col, w)),...  58 us
    all_to_all x8, starting transfers between devices, fetch(): lax.all_to_all(jnp.broadcast_to(kept[:, None, :], (nb * vecs, n_col, w)),...  29.1 us
  transfers between devices with their start and end apart: 11, of which 11 were waited for; matrix products, arithmetic and copies ran while one was open for 1% of the time, Pallas kernels for 0%

profile of v8, /device:TPU:1, one launch (start us, length us, event | category | flops | bytes accessed | tf_op | source)
XLA Modules:
  0.0 716.0 jit_solution(7063425843607161395)
XLA Ops:
  33.8 12.3 %shard_map.59 = (f32[2,24,2048]{2,1,0:T(8,128)}, f32[24,2048]{1,0:T(8,128)}, f32[24,128]{1,0:T(8,128)}) custom-call(s32[2]{0:T(128)} %fusion.56.flags_ref, f32[24,2048]{1,0:T(8,128)} %d_ref.1, f32[2,24,2048]{2,1,0:T(8,128)} %reshape.1204.di_ref, bf16[2,1,2048,2048]{3,2,1,0:T(8,128)(2,1)} %bitcast.402), custom_call_target="tpu_custom_call" | custom-call | tf_op jit(solution)/shard_map/pallas_call | solution.py:70
  48.3 11.2 %all_to_all.240 = f32[56,16,128]{2,0,1:T(8,128)S(1)} all-to-all(f32[56,16,128]{2,0,1:T(8,128)S(1)} %pad_maximum_fusion), channel_id=1, replica_groups=mesh['row'=8,'col'=16] {'col'}, dimensions={1} | all-to-all | bytes 917504 | tf_op jit(solution)/shard_map/all_to_all | solution.py:15
  73.7 15.7 %all_to_all.241 = f32[32,8,256]{2,0,1:T(8,128)S(1)} all-to-all(f32[32,8,256]{2,0,1:T(8,128)S(1)} %bitcast.427), channel_id=1, replica_groups=mesh['row'=8,'col'=16] {'row'}, dimensions={1} | all-to-all | bytes 524288 | tf_op jit(solution)/shard_map/all_to_all | solution.py:15
  125.3 12.3 %shard_map.60 = (f32[2,24,2048]{2,1,0:T(8,128)}, f32[24,2048]{1,0:T(8,128)}, f32[24,128]{1,0:T(8,128)}) custom-call(s32[2]{0:T(128)} %fusion.56.flags_ref, f32[24,2048]{1,0:T(8,128)} %get-tuple-element.365.d_ref, f32[2,24,2048]{2,1,0:T(8,128)} %multiply_add_fusion.6.di_ref, bf16[2,1,2048,2048]{3,2,1,0:T(8,128)(2,1)} %bitcast.403), custom_call_target="tpu_custom_call" | custom-call | tf_op jit(solution)/shard_map/pallas_call | solution.py:70
  139.8 11.5 %all_to_all.243 = f32[56,16,128]{2,0,1:T(8,128)S(1)} all-to-all(f32[56,16,128]{2,0,1:T(8,128)S(1)} %pad_maximum_fusion.1), channel_id=1, replica_groups=mesh['row'=8,'col'=16] {'col'}, dimensions={1} | all-to-all | bytes 917504 | tf_op jit(solution)/shard_map/all_to_all | solution.py:15
  151.4 11.2 %all_to_all.244 = f32[56,16,128]{2,0,1:T(8,128)S(1)} all-to-all(f32[56,16,128]{2,0,1:T(8,128)S(1)} %broadcast_in_dim.81), channel_id=1, replica_groups=mesh['row'=8,'col'=16] {'col'}, dimensions={1} | all-to-all | bytes 917504 | tf_op jit(solution)/shard_map/all_to_all | solution.py:17
  163.7 15.0 %all_to_all.245 = f32[32,8,256]{2,0,1:T(8,128)S(1)} all-to-all(f32[32,8,256]{2,0,1:T(8,128)S(1)} %bitcast.428), channel_id=1, replica_groups=mesh['row'=8,'col'=16] {'row'}, dimensions={1} | all-to-all | bytes 524288 | tf_op jit(solution)/shard_map/all_to_all | solution.py:15
  213.1 12.3 %shard_map.61 = (f32[2,24,2048]{2,1,0:T(8,128)}, f32[24,2048]{1,0:T(8,128)}, f32[24,128]{1,0:T(8,128)}) custom-call(s32[2]{0:T(128)} %fusion.56.flags_ref, f32[24,2048]{1,0:T(8,128)} %get-tuple-element.361.d_ref, f32[2,24,2048]{2,1,0:T(8,128)} %multiply_add_fusion.5.di_ref, bf16[2,1,2048,2048]{3,2,1,0:T(8,128)(2,1)} %bitcast.404), custom_call_target="tpu_custom_call" | custom-call | tf_op jit(solution)/shard_map/pallas_call | solution.py:70
  227.6 11.5 %all_to_all.248 = f32[56,16,128]{2,0,1:T(8,128)S(1)} all-to-all(f32[56,16,128]{2,0,1:T(8,128)S(1)} %pad_maximum_fusion.2), channel_id=1, replica_groups=mesh['row'=8,'col'=16] {'col'}, dimensions={1} | all-to-all | bytes 917504 | tf_op jit(solution)/shard_map/all_to_all | solution.py:15
  239.1 11.4 %all_to_all.249 = f32[56,16,128]{2,0,1:T(8,128)S(1)} all-to-all(f32[56,16,128]{2,0,1:T(8,128)S(1)} %broadcast_in_dim.84), channel_id=1, replica_groups=mesh['row'=8,'col'=16] {'col'}, dimensions={1} | all-to-all | bytes 917504 | tf_op jit(solution)/shard_map/all_to_all | solution.py:17
  251.6 15.0 %all_to_all.250 = f32[32,8,256]{2,0,1:T(8,128)S(1)} all-to-all(f32[32,8,256]{2,0,1:T(8,128)S(1)} %bitcast.429), channel_id=1, replica_groups=mesh['row'=8,'col'=16] {'row'}, dimensions={1} | all-to-all | bytes 524288 | tf_op jit(solution)/shard_map/all_to_all | solution.py:15
  276.9 10.3 %all_to_all.252 = f32[32,16,128]{2,0,1:T(8,128)S(1)} all-to-all(f32[32,16,128]{2,0,1:T(8,128)S(1)} %pad_maximum_fusion.11), channel_id=1, replica_groups=mesh['row'=8,'col'=16] {'col'}, dimensions={1} | all-to-all | bytes 524288 | tf_op jit(solution)/shard_map/all_to_all | solution.py:107
  300.9 12.3 %shard_map.62 = (f32[2,24,2048]{2,1,0:T(8,128)}, f32[24,2048]{1,0:T(8,128)}, f32[24,128]{1,0:T(8,128)}) custom-call(s32[2]{0:T(128)} %fusion.56.flags_ref, f32[24,2048]{1,0:T(8,128)} %get-tuple-element.357.d_ref, f32[2,24,2048]{2,1,0:T(8,128)} %multiply_add_fusion.4.di_ref, bf16[2,1,2048,2048]{3,2,1,0:T(8,128)(2,1)} %bitcast.405), custom_call_target="tpu_custom_call" | custom-call | tf_op jit(solution)/shard_map/pallas_call | solution.py:70
  315.4 11.5 %all_to_all.253 = f32[56,16,128]{2,0,1:T(8,128)S(1)} all-to-all(f32[56,16,128]{2,0,1:T(8,128)S(1)} %pad_maximum_fusion.3), channel_id=1, replica_groups=mesh['row'=8,'col'=16] {'col'}, dimensions={1} | all-to-all | bytes 917504 | tf_op jit(solution)/shard_map/all_to_all | solution.py:15
  327.0 11.2 %all_to_all.254 = f32[56,16,128]{2,0,1:T(8,128)S(1)} all-to-all(f32[56,16,128]{2,0,1:T(8,128)S(1)} %broadcast_in_dim.87), channel_id=1, replica_groups=mesh['row'=8,'col'=16] {'col'}, dimensions={1} | all-to-all | bytes 917504 | tf_op jit(solution)/shard_map/all_to_all | solution.py:17
  339.3 15.0 %all_to_all.255 = f32[32,8,256]{2,0,1:T(8,128)S(1)} all-to-all(f32[32,8,256]{2,0,1:T(8,128)S(1)} %bitcast.430), channel_id=1, replica_groups=mesh['row'=8,'col'=16] {'row'}, dimensions={1} | all-to-all | bytes 524288 | tf_op jit(solution)/shard_map/all_to_all | solution.py:15
  388.7 12.3 %shard_map.63 = (f32[2,24,2048]{2,1,0:T(8,128)}, f32[24,2048]{1,0:T(8,128)}, f32[24,128]{1,0:T(8,128)}) custom-call(s32[2]{0:T(128)} %fusion.56.flags_ref, f32[24,2048]{1,0:T(8,128)} %get-tuple-element.353.d_ref, f32[2,24,2048]{2,1,0:T(8,128)} %multiply_add_fusion.3.di_ref, bf16[2,1,2048,2048]{3,2,1,0:T(8,128)(2,1)} %bitcast.406), custom_call_target="tpu_custom_call" | custom-call | tf_op jit(solution)/shard_map/pallas_call | solution.py:70
  403.2 11.5 %all_to_all.258 = f32[56,16,128]{2,0,1:T(8,128)S(1)} all-to-all(f32[56,16,128]{2,0,1:T(8,128)S(1)} %pad_maximum_fusion.4), channel_id=1, replica_groups=mesh['row'=8,'col'=16] {'col'}, dimensions={1} | all-to-all | bytes 917504 | tf_op jit(solution)/shard_map/all_to_all | solution.py:15
  414.7 11.2 %all_to_all.259 = f32[56,16,128]{2,0,1:T(8,128)S(1)} all-to-all(f32[56,16,128]{2,0,1:T(8,128)S(1)} %broadcast_in_dim.90), channel_id=1, replica_groups=mesh['row'=8,'col'=16] {'col'}, dimensions={1} | all-to-all | bytes 917504 | tf_op jit(solution)/shard_map/all_to_all | solution.py:17
  427.0 15.0 %all_to_all.260 = f32[32,8,256]{2,0,1:T(8,128)S(1)} all-to-all(f32[32,8,256]{2,0,1:T(8,128)S(1)} %bitcast.431), channel_id=1, replica_groups=mesh['row'=8,'col'=16] {'row'}, dimensions={1} | all-to-all | bytes 524288 | tf_op jit(solution)/shard_map/all_to_all | solution.py:15
  476.4 12.3 %shard_map.64 = (f32[2,24,2048]{2,1,0:T(8,128)}, f32[24,2048]{1,0:T(8,128)}, f32[24,128]{1,0:T(8,128)}) custom-call(s32[2]{0:T(128)} %fusion.56.flags_ref, f32[24,2048]{1,0:T(8,128)} %get-tuple-element.349.d_ref, f32[2,24,2048]{2,1,0:T(8,128)} %multiply_add_fusion.2.di_ref, bf16[2,1,2048,2048]{3,2,1,0:T(8,128)(2,1)} %bitcast.407), custom_call_target="tpu_custom_call" | custom-call | tf_op jit(solution)/shard_map/pallas_call | solution.py:70
  490.9 11.5 %all_to_all.263 = f32[56,16,128]{2,0,1:T(8,128)S(1)} all-to-all(f32[56,16,128]{2,0,1:T(8,128)S(1)} %pad_maximum_fusion.5), channel_id=1, replica_groups=mesh['row'=8,'col'=16] {'col'}, dimensions={1} | all-to-all | bytes 917504 | tf_op jit(solution)/shard_map/all_to_all | solution.py:15
  502.4 11.2 %all_to_all.264 = f32[56,16,128]{2,0,1:T(8,128)S(1)} all-to-all(f32[56,16,128]{2,0,1:T(8,128)S(1)} %broadcast_in_dim.93), channel_id=1, replica_groups=mesh['row'=8,'col'=16] {'col'}, dimensions={1} | all-to-all | bytes 917504 | tf_op jit(solution)/shard_map/all_to_all | solution.py:17
  514.7 15.0 %all_to_all.265 = f32[32,8,256]{2,0,1:T(8,128)S(1)} all-to-all(f32[32,8,256]{2,0,1:T(8,128)S(1)} %bitcast.432), channel_id=1, replica_groups=mesh['row'=8,'col'=16] {'row'}, dimensions={1} | all-to-all | bytes 524288 | tf_op jit(solution)/shard_map/all_to_all | solution.py:15
  564.1 12.3 %shard_map.65 = (f32[2,24,2048]{2,1,0:T(8,128)}, f32[24,2048]{1,0:T(8,128)}, f32[24,128]{1,0:T(8,128)}) custom-call(s32[2]{0:T(128)} %fusion.56.flags_ref, f32[24,2048]{1,0:T(8,128)} %get-tuple-element.345.d_ref, f32[2,24,2048]{2,1,0:T(8,128)} %multiply_add_fusion.1.di_ref, bf16[2,1,2048,2048]{3,2,1,0:T(8,128)(2,1)} %bitcast.408), custom_call_target="tpu_custom_call" | custom-call | tf_op jit(solution)/shard_map/pallas_call | solution.py:70
  578.6 11.5 %all_to_all.268 = f32[56,16,128]{2,0,1:T(8,128)S(1)} all-to-all(f32[56,16,128]{2,0,1:T(8,128)S(1)} %pad_maximum_fusion.6), channel_id=1, replica_groups=mesh['row'=8,'col'=16] {'col'}, dimensions={1} | all-to-all | bytes 917504 | tf_op jit(solution)/shard_map/all_to_all | solution.py:15
  590.1 11.2 %all_to_all.269 = f32[56,16,128]{2,0,1:T(8,128)S(1)} all-to-all(f32[56,16,128]{2,0,1:T(8,128)S(1)} %broadcast_in_dim.96), channel_id=1, replica_groups=mesh['row'=8,'col'=16] {'col'}, dimensions={1} | all-to-all | bytes 917504 | tf_op jit(solution)/shard_map/all_to_all | solution.py:17
  602.5 15.0 %all_to_all.270 = f32[32,8,256]{2,0,1:T(8,128)S(1)} all-to-all(f32[32,8,256]{2,0,1:T(8,128)S(1)} %bitcast.433), channel_id=1, replica_groups=mesh['row'=8,'col'=16] {'row'}, dimensions={1} | all-to-all | bytes 524288 | tf_op jit(solution)/shard_map/all_to_all | solution.py:15
  651.8 12.2 %shard_map.66 = (f32[2,24,2048]{2,1,0:T(8,128)}, f32[24,2048]{1,0:T(8,128)}, f32[24,128]{1,0:T(8,128)}) custom-call(s32[2]{0:T(128)} %fusion.56.flags_ref, f32[24,2048]{1,0:T(8,128)} %get-tuple-element.341.d_ref, f32[2,24,2048]{2,1,0:T(8,128)} %multiply_add_fusion.di_ref, bf16[2,1,2048,2048]{3,2,1,0:T(8,128)(2,1)} %bitcast.409), custom_call_target="tpu_custom_call" | custom-call | tf_op jit(solution)/shard_map/pallas_call | solution.py:70
  666.2 11.5 %all_to_all.273 = f32[56,16,128]{2,0,1:T(8,128)S(1)} all-to-all(f32[56,16,128]{2,0,1:T(8,128)S(1)} %pad_maximum_fusion.7), channel_id=1, replica_groups=mesh['row'=8,'col'=16] {'col'}, dimensions={1} | all-to-all | bytes 917504 | tf_op jit(solution)/shard_map/all_to_all | solution.py:15
  677.7 11.2 %all_to_all.274 = f32[56,16,128]{2,0,1:T(8,128)S(1)} all-to-all(f32[56,16,128]{2,0,1:T(8,128)S(1)} %broadcast_in_dim.99), channel_id=1, replica_groups=mesh['row'=8,'col'=16] {'col'}, dimensions={1} | all-to-all | bytes 917504 | tf_op jit(solution)/shard_map/all_to_all | solution.py:17
  690.0 15.0 %all_to_all.275 = f32[32,8,256]{2,0,1:T(8,128)S(1)} all-to-all(f32[32,8,256]{2,0,1:T(8,128)S(1)} %bitcast.434), channel_id=1, replica_groups=mesh['row'=8,'col'=16] {'row'}, dimensions={1} | all-to-all | bytes 524288 | tf_op jit(solution)/shard_map/all_to_all | solution.py:15
  (372 shorter events, 309.3 us)
Async XLA Ops:
  3.5 16.1 %all-to-all-start = ((f32[32,16,128]{2,0,1:T(8,128)}), f32[32,16,128]{2,0,1:T(8,128)S(1)}, u32[]{:S(2)}, u32[]{:S(2)}) async-start(f32[32,16,128]{2,0,1:T(8,128)} %copy.85), calls=%async_computation | async-start | bytes 524288 | tf_op jit(solution)/shard_map/all_to_all | solution.py:107
  12.1 88.9 %copy-start = (f32[24,2048]{1,0:T(8,128)S(1)}, f32[24,2048]{1,0:T(8,128)}, u32[]{:S(2)}) copy-start(f32[24,2048]{1,0:T(8,128)} %d_ref.1) | copy-start | bytes 589828
  12.1 88.9 %copy-start.14 = (f32[2048]{0:T(1024)S(1)}, f32[2048]{0:T(1024)}, u32[]{:S(2)}) copy-start(f32[2048]{0:T(1024)} %param.53) | copy-start | bytes 24580
  20.5 12.4 %all-to-all-start.1 = ((f32[48,16,128]{2,0,1:T(8,128)}), f32[48,16,128]{2,0,1:T(8,128)S(1)}, u32[]{:S(2)}, u32[]{:S(2)}) async-start(f32[48,16,128]{2,0,1:T(8,128)} %broadcast_in_dim.76), calls=%async_computation.1 | async-start | bytes 786432 | tf_op jit(solution)/shard_map/all_to_all | solution.py:112
  33.8 90.7 %copy-start.7 = (f32[2,24,2048]{2,1,0:T(8,128)S(1)}, f32[2,24,2048]{2,1,0:T(8,128)}, u32[]{:S(2)}) copy-start(f32[2,24,2048]{2,1,0:T(8,128)} %reshape.1204.di_ref) | copy-start | bytes 1179652
  60.4 12.2 %all-to-all-start.3 = ((f32[56,16,128]{2,0,1:T(8,128)}), f32[56,16,128]{2,0,1:T(8,128)S(1)}, u32[]{:S(2)}, u32[]{:S(2)}) async-start(f32[56,16,128]{2,0,1:T(8,128)} %broadcast_in_dim.77), calls=%async_computation.3 | async-start | bytes 917504 | tf_op jit(solution)/shard_map/all_to_all | solution.py:17
  90.1 10.8 %all-to-all-start.5 = ((f32[32,8,256]{2,0,1:T(8,128)}), f32[32,8,256]{2,0,1:T(8,128)S(1)}, u32[]{:S(2)}, u32[]{:S(2)}) async-start(f32[32,8,256]{2,0,1:T(8,128)} %broadcast_in_dim.79), calls=%async_computation.5 | async-start | bytes 524288 | tf_op jit(solution)/shard_map/all_to_all | solution.py:17
  112.5 11.8 %all-to-all-start.7 = ((f32[48,16,128]{2,0,1:T(8,128)}), f32[48,16,128]{2,0,1:T(8,128)S(1)}, u32[]{:S(2)}, u32[]{:S(2)}) async-start(f32[48,16,128]{2,0,1:T(8,128)} %broadcast_in_dim.80), calls=%async_computation.7 | async-start | bytes 786432 | tf_op jit(solution)/shard_map/all_to_all | solution.py:112
  117.0 71.8 %copy-start.1 = (f32[24,2048]{1,0:T(8,128)S(1)}, f32[24,2048]{1,0:T(8,128)}, u32[]{:S(2)}) copy-start(f32[24,2048]{1,0:T(8,128)} %get-tuple-element.365.d_ref) | copy-start | bytes 589828
  125.3 86.9 %copy-start.9 = (f32[2,24,2048]{2,1,0:T(8,128)S(1)}, f32[2,24,2048]{2,1,0:T(8,128)}, u32[]{:S(2)}) copy-start(f32[2,24,2048]{2,1,0:T(8,128)} %multiply_add_fusion.6.di_ref) | copy-start | bytes 1179652
  200.2 11.8 %all-to-all-start.13 = ((f32[48,16,128]{2,0,1:T(8,128)}), f32[48,16,128]{2,0,1:T(8,128)S(1)}, u32[]{:S(2)}, u32[]{:S(2)}) async-start(f32[48,16,128]{2,0,1:T(8,128)} %broadcast_in_dim.83), calls=%async_computation.13 | async-start | bytes 786432 | tf_op jit(solution)/shard_map/all_to_all | solution.py:112
  204.7 71.9 %copy-start.2 = (f32[24,2048]{1,0:T(8,128)S(1)}, f32[24,2048]{1,0:T(8,128)}, u32[]{:S(2)}) copy-start(f32[24,2048]{1,0:T(8,128)} %get-tuple-element.361.d_ref) | copy-start | bytes 589828
  213.1 87.0 %copy-start.10 = (f32[2,24,2048]{2,1,0:T(8,128)S(1)}, f32[2,24,2048]{2,1,0:T(8,128)}, u32[]{:S(2)}) copy-start(f32[2,24,2048]{2,1,0:T(8,128)} %multiply_add_fusion.5.di_ref) | copy-start | bytes 1179652
  288.1 11.8 %all-to-all-start.19 = ((f32[48,16,128]{2,0,1:T(8,128)}), f32[48,16,128]{2,0,1:T(8,128)S(1)}, u32[]{:S(2)}, u32[]{:S(2)}) async-start(f32[48,16,128]{2,0,1:T(8,128)} %broadcast_in_dim.86), calls=%async_computation.19 | async-start | bytes 786432 | tf_op jit(solution)/shard_map/all_to_all | solution.py:112
  292.6 71.8 %copy-start.3 = (f32[24,2048]{1,0:T(8,128)S(1)}, f32[24,2048]{1,0:T(8,128)}, u32[]{:S(2)}) copy-start(f32[24,2048]{1,0:T(8,128)} %get-tuple-element.357.d_ref) | copy-start | bytes 589828
  300.9 86.9 %copy-start.11 = (f32[2,24,2048]{2,1,0:T(8,128)S(1)}, f32[2,24,2048]{2,1,0:T(8,128)}, u32[]{:S(2)}) copy-start(f32[2,24,2048]{2,1,0:T(8,128)} %multiply_add_fusion.4.di_ref) | copy-start | bytes 1179652
  375.8 11.8 %all-to-all-start.25 = ((f32[48,16,128]{2,0,1:T(8,128)}), f32[48,16,128]{2,0,1:T(8,128)S(1)}, u32[]{:S(2)}, u32[]{:S(2)}) async-start(f32[48,16,128]{2,0,1:T(8,128)} %broadcast_in_dim.89), calls=%async_computation.25 | async-start | bytes 786432 | tf_op jit(solution)/shard_map/all_to_all | solution.py:112
  380.3 71.8 %copy-start.4 = (f32[24,2048]{1,0:T(8,128)S(1)}, f32[24,2048]{1,0:T(8,128)}, u32[]{:S(2)}) copy-start(f32[24,2048]{1,0:T(8,128)} %get-tuple-element.353.d_ref) | copy-start | bytes 589828
  388.7 86.9 %copy-start.12 = (f32[2,24,2048]{2,1,0:T(8,128)S(1)}, f32[2,24,2048]{2,1,0:T(8,128)}, u32[]{:S(2)}) copy-start(f32[2,24,2048]{2,1,0:T(8,128)} %multiply_add_fusion.3.di_ref) | copy-start | bytes 1179652
  463.5 11.8 %all-to-all-start.31 = ((f32[48,16,128]{2,0,1:T(8,128)}), f32[48,16,128]{2,0,1:T(8,128)S(1)}, u32[]{:S(2)}, u32[]{:S(2)}) async-start(f32[48,16,128]{2,0,1:T(8,128)} %broadcast_in_dim.92), calls=%async_computation.31 | async-start | bytes 786432 | tf_op jit(solution)/shard_map/all_to_all | solution.py:112
  468.2 71.5 %copy-start.5 = (f32[24,2048]{1,0:T(8,128)S(1)}, f32[24,2048]{1,0:T(8,128)}, u32[]{:S(2)}) copy-start(f32[24,2048]{1,0:T(8,128)} %get-tuple-element.349.d_ref) | copy-start | bytes 589828
  476.4 86.9 %copy-start.13 = (f32[2,24,2048]{2,1,0:T(8,128)S(1)}, f32[2,24,2048]{2,1,0:T(8,128)}, u32[]{:S(2)}) copy-start(f32[2,24,2048]{2,1,0:T(8,128)} %multiply_add_fusion.2.di_ref) | copy-start | bytes 1179652
  551.2 11.8 %all-to-all-start.37 = ((f32[48,16,128]{2,0,1:T(8,128)}), f32[48,16,128]{2,0,1:T(8,128)S(1)}, u32[]{:S(2)}, u32[]{:S(2)}) async-start(f32[48,16,128]{2,0,1:T(8,128)} %broadcast_in_dim.95), calls=%async_computation.37 | async-start | bytes 786432 | tf_op jit(solution)/shard_map/all_to_all | solution.py:112
  555.7 71.8 %copy-start.6 = (f32[24,2048]{1,0:T(8,128)S(1)}, f32[24,2048]{1,0:T(8,128)}, u32[]{:S(2)}) copy-start(f32[24,2048]{1,0:T(8,128)} %get-tuple-element.345.d_ref) | copy-start | bytes 589828
  564.1 86.9 %copy-start.8 = (f32[2,24,2048]{2,1,0:T(8,128)S(1)}, f32[2,24,2048]{2,1,0:T(8,128)}, u32[]{:S(2)}) copy-start(f32[2,24,2048]{2,1,0:T(8,128)} %multiply_add_fusion.1.di_ref) | copy-start | bytes 1179652
  639.0 11.8 %all-to-all-start.43 = ((f32[48,16,128]{2,0,1:T(8,128)}), f32[48,16,128]{2,0,1:T(8,128)S(1)}, u32[]{:S(2)}, u32[]{:S(2)}) async-start(f32[48,16,128]{2,0,1:T(8,128)} %broadcast_in_dim.98), calls=%async_computation.43 | async-start | bytes 786432 | tf_op jit(solution)/shard_map/all_to_all | solution.py:112
  643.5 71.6 %copy-start.15 = (f32[24,2048]{1,0:T(8,128)S(1)}, f32[24,2048]{1,0:T(8,128)}, u32[]{:S(2)}) copy-start(f32[24,2048]{1,0:T(8,128)} %get-tuple-element.341.d_ref) | copy-start | bytes 589828

commit v9 on v5

--- a/solution.py
+++ b/solution.py
@@ -12,10 +12,9 @@
 def all_reduce(x, axis, n):
     rows, width = x.shape
     w = width // n
-    y = lax.all_to_all(x.reshape(rows, n, w), axis, 1, 1, tiled=True)
-    part = jnp.sum(y, axis=1)
-    z = lax.all_to_all(jnp.broadcast_to(part[:, None, :], (rows, n, w)), axis, 1, 1, tiled=True)
-    return z.reshape(rows, width)
+    y = lax.all_to_all(x, axis, 1, 1, tiled=True)
+    part = jnp.sum(y.reshape(rows, n, w), axis=1)
+    return lax.all_to_all(jnp.tile(part, (1, n)), axis, 1, 1, tiled=True)
 
 
 def products_kernel(flags_ref, d_ref, di_ref, k_ref, fwd_ref, m_ref, p_ref):
@@ -50,7 +49,7 @@
         p_ref[...] = acc
 
 
-def block_products(flags, d, di, blocks, tile=512):
+def block_products(flags, d, di, blocks, tile=1024):
     nb, _, order, _ = blocks.shape
     vecs = d.shape[0]
     grid_spec = pltpu.PrefetchScalarGridSpec(
@@ -99,9 +98,17 @@
         noise = noise_var[None, :]
 
         def fetch(res):
-            sent = [jnp.where(owner[k], res, 0.0) for k in range(nb)]
-            out = all_reduce(pack(sent, jnp.sum(res * res, axis=1)), "col", n_col)
-            return out[: nb * vecs].reshape(nb, vecs, width), out[nb * vecs, :vecs]
+            w = width // n_col
+            norms = jnp.sum(res * res, axis=1)
+            tail = jnp.zeros((PAD, n_col, w), jnp.float32).at[0, :, :vecs].set(jnp.broadcast_to(norms, (n_col, vecs)))
+            x = jnp.concatenate([res, tail.reshape(PAD, width)], axis=0)
+            y = lax.all_to_all(x, "col", 1, 1, tiled=True)
+            norm = jnp.sum(y[vecs].reshape(n_col, w)[:, :vecs], axis=0)
+            kept = jnp.concatenate(
+                [lax.dynamic_slice_in_dim(y[:vecs], rows[k] * w, w, axis=1) for k in range(nb)], axis=0
+            )
+            z = lax.all_to_all(jnp.tile(kept, (1, n_col)), "col", 1, 1, tiled=True)
+            return z.reshape(nb, vecs, width), norm
 
         solution = jnp.zeros_like(rhs)
         residual = rhs

time: 750 us -> 720 us (0.960)
  blocking collectives: 556 us -> 433 us
  waiting for transfers between devices: 14.2 us -> 76.9 us
  starting transfers between devices: 7.91 us -> 45.1 us
  Pallas kernels: 111 us -> 98.5 us
    all_to_all x46 -> x37, blocking collectives: 556 us -> 433 us  [the longest x16 212 us: all_reduce(): y = lax.all_to_all(x, axis, 1, 1, tiled=True)]
    all_to_all x2 -> x11, waiting for transfers between devices: 14.2 us -> 76.9 us  [the longest x8 58.1 us: fetch(): z = lax.all_to_all(jnp.tile(kept, (1, n_col)), 'col', 1, 1, tiled=True)]
    all_to_all x2 -> x11, starting transfers between devices: 7.91 us -> 45.1 us  [the longest x8 28.6 us: fetch(): z = lax.all_to_all(jnp.tile(kept, (1, n_col)), 'col', 1, 1, tiled=True)]
    pallas_call x8, Pallas kernels: 111 us -> 98.5 us  [block_products(): pl.pallas_call(products_kernel, grid_spec=grid_spec, out_shape=[jax.Shape...]
    another operation x0 -> x24, local copies, waits for them, and re-layouts: none -> 8.04 us  [the longest x8 6.17 us: fetch(): z = lax.all_to_all(jnp.tile(kept, (1, n_col)), 'col', 1, 1, tiled=True)]
  transfers between devices with their start and end apart: 2 -> 11, of which waited for: 2 -> 11; matrix products, arithmetic and copies ran while one was open for 0% -> 1% of each run, Pallas kernels for 0% -> 0%
where the time goes in v9:
time: 720 us; the launch traced here: 716 us
  blocking collectives  433 us (60%)
  Pallas kernels  98.5 us (14%)
  waiting for transfers between devices  76.9 us (11%)
  starting transfers between devices  45.1 us (6%)
  other arithmetic  32.7 us (5%)
  local copies, waits for them, and re-layouts  24.9 us (3%)
    all_to_all x16, blocking collectives, all_reduce(): y = lax.all_to_all(x, axis, 1, 1, tiled=True)  212 us
    all_to_all x14, blocking collectives, all_reduce(): return lax.all_to_all(jnp.tile(part, (1, n)), axis, 1, 1, tiled=True)  148 us
    pallas_call x8, Pallas kernels, block_products(): pl.pallas_call(products_kernel, grid_spec=grid_spec, out_shape=[jax.Shape...  98.5 us
    all_to_all x7, blocking collectives, fetch(): y = lax.all_to_all(x, 'col', 1, 1, tiled=True)  72.4 us
    all_to_all x8, waiting for transfers between devices, fetch(): z = lax.all_to_all(jnp.tile(kept, (1, n_col)), 'col', 1, 1, tiled=True)  58.1 us
    all_to_all x8, starting transfers between devices, fetch(): z = lax.all_to_all(jnp.tile(kept, (1, n_col)), 'col', 1, 1, tiled=True)  28.6 us
  transfers between devices with their start and end apart: 11, of which 11 were waited for; matrix products, arithmetic and copies ran while one was open for 1% of the time, Pallas kernels for 0%

profile of v9, /device:TPU:1, one launch (start us, length us, event | category | flops | bytes accessed | tf_op | source)
XLA Modules:
  0.0 715.8 jit_solution(10359076599864902254)
XLA Ops:
  33.4 12.3 %shard_map.59 = (f32[2,24,2048]{2,1,0:T(8,128)}, f32[24,2048]{1,0:T(8,128)}, f32[24,128]{1,0:T(8,128)}) custom-call(s32[2]{0:T(128)} %fusion.56.flags_ref, f32[24,2048]{1,0:T(8,128)} %d_ref.1, f32[2,24,2048]{2,1,0:T(8,128)} %reshape.1387.di_ref, bf16[2,1,2048,2048]{3,2,1,0:T(8,128)(2,1)} %bitcast.418), custom_call_target="tpu_custom_call" | custom-call | tf_op jit(solution)/shard_map/pallas_call | solution.py:69
  47.9 11.3 %all_to_all.360 = f32[56,16,128]{2,0,1:T(8,128)S(1)} all-to-all(f32[56,16,128]{2,0,1:T(8,128)S(1)} %pad_maximum_fusion), channel_id=1, replica_groups=mesh['row'=8,'col'=16] {'col'}, dimensions={1} | all-to-all | bytes 917504 | tf_op jit(solution)/shard_map/all_to_all | solution.py:15
  73.3 16.0 %all_to_all.361 = f32[32,8,256]{2,0,1:T(8,128)S(1)} all-to-all(f32[32,8,256]{2,0,1:T(8,128)S(1)} %bitcast.443), channel_id=1, replica_groups=mesh['row'=8,'col'=16] {'row'}, dimensions={1} | all-to-all | bytes 524288 | tf_op jit(solution)/shard_map/all_to_all | solution.py:15
  125.3 12.3 %shard_map.60 = (f32[2,24,2048]{2,1,0:T(8,128)}, f32[24,2048]{1,0:T(8,128)}, f32[24,128]{1,0:T(8,128)}) custom-call(s32[2]{0:T(128)} %fusion.56.flags_ref, f32[24,2048]{1,0:T(8,128)} %get-tuple-element.365.d_ref, f32[2,24,2048]{2,1,0:T(8,128)} %multiply_add_fusion.6.di_ref, bf16[2,1,2048,2048]{3,2,1,0:T(8,128)(2,1)} %bitcast.419), custom_call_target="tpu_custom_call" | custom-call | tf_op jit(solution)/shard_map/pallas_call | solution.py:69
  139.8 11.5 %all_to_all.363 = f32[56,16,128]{2,0,1:T(8,128)S(1)} all-to-all(f32[56,16,128]{2,0,1:T(8,128)S(1)} %pad_maximum_fusion.1), channel_id=1, replica_groups=mesh['row'=8,'col'=16] {'col'}, dimensions={1} | all-to-all | bytes 917504 | tf_op jit(solution)/shard_map/all_to_all | solution.py:15
  151.3 11.2 %all_to_all.364 = f32[56,16,128]{2,0,1:T(8,128)S(1)} all-to-all(f32[56,16,128]{2,0,1:T(8,128)S(1)} %tile.52), channel_id=1, replica_groups=mesh['row'=8,'col'=16] {'col'}, dimensions={1} | all-to-all | bytes 917504 | tf_op jit(solution)/shard_map/all_to_all | solution.py:17
  163.7 15.0 %all_to_all.365 = f32[32,8,256]{2,0,1:T(8,128)S(1)} all-to-all(f32[32,8,256]{2,0,1:T(8,128)S(1)} %bitcast.444), channel_id=1, replica_groups=mesh['row'=8,'col'=16] {'row'}, dimensions={1} | all-to-all | bytes 524288 | tf_op jit(solution)/shard_map/all_to_all | solution.py:15
  213.0 12.3 %shard_map.61 = (f32[2,24,2048]{2,1,0:T(8,128)}, f32[24,2048]{1,0:T(8,128)}, f32[24,128]{1,0:T(8,128)}) custom-call(s32[2]{0:T(128)} %fusion.56.flags_ref, f32[24,2048]{1,0:T(8,128)} %get-tuple-element.361.d_ref, f32[2,24,2048]{2,1,0:T(8,128)} %multiply_add_fusion.5.di_ref, bf16[2,1,2048,2048]{3,2,1,0:T(8,128)(2,1)} %bitcast.420), custom_call_target="tpu_custom_call" | custom-call | tf_op jit(solution)/shard_map/pallas_call | solution.py:69
  227.5 11.5 %all_to_all.368 = f32[56,16,128]{2,0,1:T(8,128)S(1)} all-to-all(f32[56,16,128]{2,0,1:T(8,128)S(1)} %pad_maximum_fusion.2), channel_id=1, replica_groups=mesh['row'=8,'col'=16] {'col'}, dimensions={1} | all-to-all | bytes 917504 | tf_op jit(solution)/shard_map/all_to_all | solution.py:15
  239.1 11.4 %all_to_all.369 = f32[56,16,128]{2,0,1:T(8,128)S(1)} all-to-all(f32[56,16,128]{2,0,1:T(8,128)S(1)} %tile.55), channel_id=1, replica_groups=mesh['row'=8,'col'=16] {'col'}, dimensions={1} | all-to-all | bytes 917504 | tf_op jit(solution)/shard_map/all_to_all | solution.py:17
  251.5 14.8 %all_to_all.370 = f32[32,8,256]{2,0,1:T(8,128)S(1)} all-to-all(f32[32,8,256]{2,0,1:T(8,128)S(1)} %bitcast.445), channel_id=1, replica_groups=mesh['row'=8,'col'=16] {'row'}, dimensions={1} | all-to-all | bytes 524288 | tf_op jit(solution)/shard_map/all_to_all | solution.py:15
  300.7 12.3 %shard_map.62 = (f32[2,24,2048]{2,1,0:T(8,128)}, f32[24,2048]{1,0:T(8,128)}, f32[24,128]{1,0:T(8,128)}) custom-call(s32[2]{0:T(128)} %fusion.56.flags_ref, f32[24,2048]{1,0:T(8,128)} %get-tuple-element.357.d_ref, f32[2,24,2048]{2,1,0:T(8,128)} %multiply_add_fusion.4.di_ref, bf16[2,1,2048,2048]{3,2,1,0:T(8,128)(2,1)} %bitcast.421), custom_call_target="tpu_custom_call" | custom-call | tf_op jit(solution)/shard_map/pallas_call | solution.py:69
  315.2 11.5 %all_to_all.373 = f32[56,16,128]{2,0,1:T(8,128)S(1)} all-to-all(f32[56,16,128]{2,0,1:T(8,128)S(1)} %pad_maximum_fusion.3), channel_id=1, replica_groups=mesh['row'=8,'col'=16] {'col'}, dimensions={1} | all-to-all | bytes 917504 | tf_op jit(solution)/shard_map/all_to_all | solution.py:15
  326.8 11.2 %all_to_all.374 = f32[56,16,128]{2,0,1:T(8,128)S(1)} all-to-all(f32[56,16,128]{2,0,1:T(8,128)S(1)} %tile.58), channel_id=1, replica_groups=mesh['row'=8,'col'=16] {'col'}, dimensions={1} | all-to-all | bytes 917504 | tf_op jit(solution)/shard_map/all_to_all | solution.py:17
  339.1 15.0 %all_to_all.375 = f32[32,8,256]{2,0,1:T(8,128)S(1)} all-to-all(f32[32,8,256]{2,0,1:T(8,128)S(1)} %bitcast.446), channel_id=1, replica_groups=mesh['row'=8,'col'=16] {'row'}, dimensions={1} | all-to-all | bytes 524288 | tf_op jit(solution)/shard_map/all_to_all | solution.py:15
  364.4 10.3 %all_to_all.377 = f32[32,16,128]{2,0,1:T(8,128)S(1)} all-to-all(f32[32,16,128]{2,0,1:T(8,128)S(1)} %pad_maximum_fusion.12), channel_id=1, replica_groups=mesh['row'=8,'col'=16] {'col'}, dimensions={1} | all-to-all | bytes 524288 | tf_op jit(solution)/shard_map/all_to_all | solution.py:105
  388.4 12.3 %shard_map.63 = (f32[2,24,2048]{2,1,0:T(8,128)}, f32[24,2048]{1,0:T(8,128)}, f32[24,128]{1,0:T(8,128)}) custom-call(s32[2]{0:T(128)} %fusion.56.flags_ref, f32[24,2048]{1,0:T(8,128)} %get-tuple-element.353.d_ref, f32[2,24,2048]{2,1,0:T(8,128)} %multiply_add_fusion.3.di_ref, bf16[2,1,2048,2048]{3,2,1,0:T(8,128)(2,1)} %bitcast.422), custom_call_target="tpu_custom_call" | custom-call | tf_op jit(solution)/shard_map/pallas_call | solution.py:69
  402.9 11.5 %all_to_all.378 = f32[56,16,128]{2,0,1:T(8,128)S(1)} all-to-all(f32[56,16,128]{2,0,1:T(8,128)S(1)} %pad_maximum_fusion.4), channel_id=1, replica_groups=mesh['row'=8,'col'=16] {'col'}, dimensions={1} | all-to-all | bytes 917504 | tf_op jit(solution)/shard_map/all_to_all | solution.py:15
  414.5 11.2 %all_to_all.379 = f32[56,16,128]{2,0,1:T(8,128)S(1)} all-to-all(f32[56,16,128]{2,0,1:T(8,128)S(1)} %tile.61), channel_id=1, replica_groups=mesh['row'=8,'col'=16] {'col'}, dimensions={1} | all-to-all | bytes 917504 | tf_op jit(solution)/shard_map/all_to_all | solution.py:17
  426.8 15.0 %all_to_all.380 = f32[32,8,256]{2,0,1:T(8,128)S(1)} all-to-all(f32[32,8,256]{2,0,1:T(8,128)S(1)} %bitcast.447), channel_id=1, replica_groups=mesh['row'=8,'col'=16] {'row'}, dimensions={1} | all-to-all | bytes 524288 | tf_op jit(solution)/shard_map/all_to_all | solution.py:15
  476.1 12.3 %shard_map.64 = (f32[2,24,2048]{2,1,0:T(8,128)}, f32[24,2048]{1,0:T(8,128)}, f32[24,128]{1,0:T(8,128)}) custom-call(s32[2]{0:T(128)} %fusion.56.flags_ref, f32[24,2048]{1,0:T(8,128)} %get-tuple-element.349.d_ref, f32[2,24,2048]{2,1,0:T(8,128)} %multiply_add_fusion.2.di_ref, bf16[2,1,2048,2048]{3,2,1,0:T(8,128)(2,1)} %bitcast.423), custom_call_target="tpu_custom_call" | custom-call | tf_op jit(solution)/shard_map/pallas_call | solution.py:69
  490.6 11.5 %all_to_all.383 = f32[56,16,128]{2,0,1:T(8,128)S(1)} all-to-all(f32[56,16,128]{2,0,1:T(8,128)S(1)} %pad_maximum_fusion.5), channel_id=1, replica_groups=mesh['row'=8,'col'=16] {'col'}, dimensions={1} | all-to-all | bytes 917504 | tf_op jit(solution)/shard_map/all_to_all | solution.py:15
  502.2 11.2 %all_to_all.384 = f32[56,16,128]{2,0,1:T(8,128)S(1)} all-to-all(f32[56,16,128]{2,0,1:T(8,128)S(1)} %tile.64), channel_id=1, replica_groups=mesh['row'=8,'col'=16] {'col'}, dimensions={1} | all-to-all | bytes 917504 | tf_op jit(solution)/shard_map/all_to_all | solution.py:17
  514.5 15.0 %all_to_all.385 = f32[32,8,256]{2,0,1:T(8,128)S(1)} all-to-all(f32[32,8,256]{2,0,1:T(8,128)S(1)} %bitcast.448), channel_id=1, replica_groups=mesh['row'=8,'col'=16] {'row'}, dimensions={1} | all-to-all | bytes 524288 | tf_op jit(solution)/shard_map/all_to_all | solution.py:15
  563.9 12.3 %shard_map.65 = (f32[2,24,2048]{2,1,0:T(8,128)}, f32[24,2048]{1,0:T(8,128)}, f32[24,128]{1,0:T(8,128)}) custom-call(s32[2]{0:T(128)} %fusion.56.flags_ref, f32[24,2048]{1,0:T(8,128)} %get-tuple-element.345.d_ref, f32[2,24,2048]{2,1,0:T(8,128)} %multiply_add_fusion.1.di_ref, bf16[2,1,2048,2048]{3,2,1,0:T(8,128)(2,1)} %bitcast.424), custom_call_target="tpu_custom_call" | custom-call | tf_op jit(solution)/shard_map/pallas_call | solution.py:69
  578.4 11.5 %all_to_all.388 = f32[56,16,128]{2,0,1:T(8,128)S(1)} all-to-all(f32[56,16,128]{2,0,1:T(8,128)S(1)} %pad_maximum_fusion.6), channel_id=1, replica_groups=mesh['row'=8,'col'=16] {'col'}, dimensions={1} | all-to-all | bytes 917504 | tf_op jit(solution)/shard_map/all_to_all | solution.py:15
  589.9 11.2 %all_to_all.389 = f32[56,16,128]{2,0,1:T(8,128)S(1)} all-to-all(f32[56,16,128]{2,0,1:T(8,128)S(1)} %tile.67), channel_id=1, replica_groups=mesh['row'=8,'col'=16] {'col'}, dimensions={1} | all-to-all | bytes 917504 | tf_op jit(solution)/shard_map/all_to_all | solution.py:17
  602.2 15.0 %all_to_all.390 = f32[32,8,256]{2,0,1:T(8,128)S(1)} all-to-all(f32[32,8,256]{2,0,1:T(8,128)S(1)} %bitcast.449), channel_id=1, replica_groups=mesh['row'=8,'col'=16] {'row'}, dimensions={1} | all-to-all | bytes 524288 | tf_op jit(solution)/shard_map/all_to_all | solution.py:15
  651.6 12.2 %shard_map.66 = (f32[2,24,2048]{2,1,0:T(8,128)}, f32[24,2048]{1,0:T(8,128)}, f32[24,128]{1,0:T(8,128)}) custom-call(s32[2]{0:T(128)} %fusion.56.flags_ref, f32[24,2048]{1,0:T(8,128)} %get-tuple-element.341.d_ref, f32[2,24,2048]{2,1,0:T(8,128)} %multiply_add_fusion.di_ref, bf16[2,1,2048,2048]{3,2,1,0:T(8,128)(2,1)} %bitcast.425), custom_call_target="tpu_custom_call" | custom-call | tf_op jit(solution)/shard_map/pallas_call | solution.py:69
  666.0 11.5 %all_to_all.393 = f32[56,16,128]{2,0,1:T(8,128)S(1)} all-to-all(f32[56,16,128]{2,0,1:T(8,128)S(1)} %pad_maximum_fusion.7), channel_id=1, replica_groups=mesh['row'=8,'col'=16] {'col'}, dimensions={1} | all-to-all | bytes 917504 | tf_op jit(solution)/shard_map/all_to_all | solution.py:15
  677.5 11.2 %all_to_all.394 = f32[56,16,128]{2,0,1:T(8,128)S(1)} all-to-all(f32[56,16,128]{2,0,1:T(8,128)S(1)} %tile.70), channel_id=1, replica_groups=mesh['row'=8,'col'=16] {'col'}, dimensions={1} | all-to-all | bytes 917504 | tf_op jit(solution)/shard_map/all_to_all | solution.py:17
  689.8 15.0 %all_to_all.395 = f32[32,8,256]{2,0,1:T(8,128)S(1)} all-to-all(f32[32,8,256]{2,0,1:T(8,128)S(1)} %bitcast.450), channel_id=1, replica_groups=mesh['row'=8,'col'=16] {'row'}, dimensions={1} | all-to-all | bytes 524288 | tf_op jit(solution)/shard_map/all_to_all | solution.py:15
  (380 shorter events, 311.1 us)
Async XLA Ops:
  3.5 16.1 %all-to-all-start = ((f32[32,16,128]{2,0,1:T(8,128)}), f32[32,16,128]{2,0,1:T(8,128)S(1)}, u32[]{:S(2)}, u32[]{:S(2)}) async-start(f32[32,16,128]{2,0,1:T(8,128)} %copy.85), calls=%async_computation | async-start | bytes 524288 | tf_op jit(solution)/shard_map/all_to_all | solution.py:105
  12.1 88.9 %copy-start = (f32[24,2048]{1,0:T(8,128)S(1)}, f32[24,2048]{1,0:T(8,128)}, u32[]{:S(2)}) copy-start(f32[24,2048]{1,0:T(8,128)} %d_ref.1) | copy-start | bytes 589828
  12.1 88.9 %copy-start.14 = (f32[2048]{0:T(1024)S(1)}, f32[2048]{0:T(1024)}, u32[]{:S(2)}) copy-start(f32[2048]{0:T(1024)} %param.53) | copy-start | bytes 24580
  20.5 12.0 %all-to-all-start.1 = ((f32[48,16,128]{2,0,1:T(8,128)}), f32[48,16,128]{2,0,1:T(8,128)S(1)}, u32[]{:S(2)}, u32[]{:S(2)}) async-start(f32[48,16,128]{2,0,1:T(8,128)} %tile.48), calls=%async_computation.1 | async-start | bytes 786432 | tf_op jit(solution)/shard_map/all_to_all | solution.py:110
  33.4 91.0 %copy-start.7 = (f32[2,24,2048]{2,1,0:T(8,128)S(1)}, f32[2,24,2048]{2,1,0:T(8,128)}, u32[]{:S(2)}) copy-start(f32[2,24,2048]{2,1,0:T(8,128)} %reshape.1387.di_ref) | copy-start | bytes 1179652
  60.1 12.1 %all-to-all-start.3 = ((f32[56,16,128]{2,0,1:T(8,128)}), f32[56,16,128]{2,0,1:T(8,128)S(1)}, u32[]{:S(2)}, u32[]{:S(2)}) async-start(f32[56,16,128]{2,0,1:T(8,128)} %tile.49), calls=%async_computation.3 | async-start | bytes 917504 | tf_op jit(solution)/shard_map/all_to_all | solution.py:17
  90.1 10.8 %all-to-all-start.5 = ((f32[32,8,256]{2,0,1:T(8,128)}), f32[32,8,256]{2,0,1:T(8,128)S(1)}, u32[]{:S(2)}, u32[]{:S(2)}) async-start(f32[32,8,256]{2,0,1:T(8,128)} %tile.50), calls=%async_computation.5 | async-start | bytes 524288 | tf_op jit(solution)/shard_map/all_to_all | solution.py:17
  112.5 11.8 %all-to-all-start.7 = ((f32[48,16,128]{2,0,1:T(8,128)}), f32[48,16,128]{2,0,1:T(8,128)S(1)}, u32[]{:S(2)}, u32[]{:S(2)}) async-start(f32[48,16,128]{2,0,1:T(8,128)} %tile.51), calls=%async_computation.7 | async-start | bytes 786432 | tf_op jit(solution)/shard_map/all_to_all | solution.py:110
  116.9 71.7 %copy-start.1 = (f32[24,2048]{1,0:T(8,128)S(1)}, f32[24,2048]{1,0:T(8,128)}, u32[]{:S(2)}) copy-start(f32[24,2048]{1,0:T(8,128)} %get-tuple-element.365.d_ref) | copy-start | bytes 589828
  125.3 86.9 %copy-start.9 = (f32[2,24,2048]{2,1,0:T(8,128)S(1)}, f32[2,24,2048]{2,1,0:T(8,128)}, u32[]{:S(2)}) copy-start(f32[2,24,2048]{2,1,0:T(8,128)} %multiply_add_fusion.6.di_ref) | copy-start | bytes 1179652
  200.2 11.8 %all-to-all-start.13 = ((f32[48,16,128]{2,0,1:T(8,128)}), f32[48,16,128]{2,0,1:T(8,128)S(1)}, u32[]{:S(2)}, u32[]{:S(2)}) async-start(f32[48,16,128]{2,0,1:T(8,128)} %tile.54), calls=%async_computation.13 | async-start | bytes 786432 | tf_op jit(solution)/shard_map/all_to_all | solution.py:110
  204.7 71.7 %copy-start.2 = (f32[24,2048]{1,0:T(8,128)S(1)}, f32[24,2048]{1,0:T(8,128)}, u32[]{:S(2)}) copy-start(f32[24,2048]{1,0:T(8,128)} %get-tuple-element.361.d_ref) | copy-start | bytes 589828
  213.0 86.9 %copy-start.10 = (f32[2,24,2048]{2,1,0:T(8,128)S(1)}, f32[2,24,2048]{2,1,0:T(8,128)}, u32[]{:S(2)}) copy-start(f32[2,24,2048]{2,1,0:T(8,128)} %multiply_add_fusion.5.di_ref) | copy-start | bytes 1179652
  287.9 11.8 %all-to-all-start.19 = ((f32[48,16,128]{2,0,1:T(8,128)}), f32[48,16,128]{2,0,1:T(8,128)S(1)}, u32[]{:S(2)}, u32[]{:S(2)}) async-start(f32[48,16,128]{2,0,1:T(8,128)} %tile.57), calls=%async_computation.19 | async-start | bytes 786432 | tf_op jit(solution)/shard_map/all_to_all | solution.py:110
  292.4 71.7 %copy-start.3 = (f32[24,2048]{1,0:T(8,128)S(1)}, f32[24,2048]{1,0:T(8,128)}, u32[]{:S(2)}) copy-start(f32[24,2048]{1,0:T(8,128)} %get-tuple-element.357.d_ref) | copy-start | bytes 589828
  300.7 86.9 %copy-start.11 = (f32[2,24,2048]{2,1,0:T(8,128)S(1)}, f32[2,24,2048]{2,1,0:T(8,128)}, u32[]{:S(2)}) copy-start(f32[2,24,2048]{2,1,0:T(8,128)} %multiply_add_fusion.4.di_ref) | copy-start | bytes 1179652
  375.6 11.8 %all-to-all-start.25 = ((f32[48,16,128]{2,0,1:T(8,128)}), f32[48,16,128]{2,0,1:T(8,128)S(1)}, u32[]{:S(2)}, u32[]{:S(2)}) async-start(f32[48,16,128]{2,0,1:T(8,128)} %tile.60), calls=%async_computation.25 | async-start | bytes 786432 | tf_op jit(solution)/shard_map/all_to_all | solution.py:110
  380.1 71.7 %copy-start.4 = (f32[24,2048]{1,0:T(8,128)S(1)}, f32[24,2048]{1,0:T(8,128)}, u32[]{:S(2)}) copy-start(f32[24,2048]{1,0:T(8,128)} %get-tuple-element.353.d_ref) | copy-start | bytes 589828
  388.4 86.9 %copy-start.12 = (f32[2,24,2048]{2,1,0:T(8,128)S(1)}, f32[2,24,2048]{2,1,0:T(8,128)}, u32[]{:S(2)}) copy-start(f32[2,24,2048]{2,1,0:T(8,128)} %multiply_add_fusion.3.di_ref) | copy-start | bytes 1179652
  463.3 11.8 %all-to-all-start.31 = ((f32[48,16,128]{2,0,1:T(8,128)}), f32[48,16,128]{2,0,1:T(8,128)S(1)}, u32[]{:S(2)}, u32[]{:S(2)}) async-start(f32[48,16,128]{2,0,1:T(8,128)} %tile.63), calls=%async_computation.31 | async-start | bytes 786432 | tf_op jit(solution)/shard_map/all_to_all | solution.py:110
  468.0 71.5 %copy-start.5 = (f32[24,2048]{1,0:T(8,128)S(1)}, f32[24,2048]{1,0:T(8,128)}, u32[]{:S(2)}) copy-start(f32[24,2048]{1,0:T(8,128)} %get-tuple-element.349.d_ref) | copy-start | bytes 589828
  476.1 86.9 %copy-start.13 = (f32[2,24,2048]{2,1,0:T(8,128)S(1)}, f32[2,24,2048]{2,1,0:T(8,128)}, u32[]{:S(2)}) copy-start(f32[2,24,2048]{2,1,0:T(8,128)} %multiply_add_fusion.2.di_ref) | copy-start | bytes 1179652
  551.0 11.8 %all-to-all-start.37 = ((f32[48,16,128]{2,0,1:T(8,128)}), f32[48,16,128]{2,0,1:T(8,128)S(1)}, u32[]{:S(2)}, u32[]{:S(2)}) async-start(f32[48,16,128]{2,0,1:T(8,128)} %tile.66), calls=%async_computation.37 | async-start | bytes 786432 | tf_op jit(solution)/shard_map/all_to_all | solution.py:110
  555.5 71.8 %copy-start.6 = (f32[24,2048]{1,0:T(8,128)S(1)}, f32[24,2048]{1,0:T(8,128)}, u32[]{:S(2)}) copy-start(f32[24,2048]{1,0:T(8,128)} %get-tuple-element.345.d_ref) | copy-start | bytes 589828
  563.9 86.9 %copy-start.8 = (f32[2,24,2048]{2,1,0:T(8,128)S(1)}, f32[2,24,2048]{2,1,0:T(8,128)}, u32[]{:S(2)}) copy-start(f32[2,24,2048]{2,1,0:T(8,128)} %multiply_add_fusion.1.di_ref) | copy-start | bytes 1179652
  638.7 11.8 %all-to-all-start.43 = ((f32[48,16,128]{2,0,1:T(8,128)}), f32[48,16,128]{2,0,1:T(8,128)S(1)}, u32[]{:S(2)}, u32[]{:S(2)}) async-start(f32[48,16,128]{2,0,1:T(8,128)} %tile.69), calls=%async_computation.43 | async-start | bytes 786432 | tf_op jit(solution)/shard_map/all_to_all | solution.py:110
  643.2 71.6 %copy-start.15 = (f32[24,2048]{1,0:T(8,128)S(1)}, f32[24,2048]{1,0:T(8,128)}, u32[]{:S(2)}) copy-start(f32[24,2048]{1,0:T(8,128)} %get-tuple-element.341.d_ref) | copy-start | bytes 589828

commit v10 on v9

--- a/solution.py
+++ b/solution.py
@@ -110,11 +110,8 @@
             z = lax.all_to_all(jnp.tile(kept, (1, n_col)), "col", 1, 1, tiled=True)
             return z.reshape(nb, vecs, width), norm
 
-        solution = jnp.zeros_like(rhs)
-        residual = rhs
-        direction = rhs
-        dir_rows, norm_now = fetch(rhs)
-        for step in range(ITERS):
+        def step(carry, fetch_next):
+            solution, residual, direction, dir_rows, norm_now = carry
             fwd, mirrored, lanes = block_products(flags, direction, dir_rows, blocks)
             forward = [fwd[k] for k in range(nb)]
             part = jnp.sum(lanes, axis=1)
@@ -129,12 +126,18 @@
             alpha = norm_now / curvature
             solution = solution + alpha[:, None] * direction
             residual = residual - alpha[:, None] * image
-            if step + 1 < ITERS:
+            if fetch_next:
                 res_rows, norm_next = fetch(residual)
                 beta = norm_next / norm_now
                 direction = residual + beta[:, None] * direction
                 dir_rows = res_rows + beta[None, :, None] * dir_rows
                 norm_now = norm_next
+            return solution, residual, direction, dir_rows, norm_now
+
+        dir_rows, norm_now = fetch(rhs)
+        carry = (jnp.zeros_like(rhs), rhs, rhs, dir_rows, norm_now)
+        carry = lax.fori_loop(0, ITERS - 1, lambda i, c: step(c, True), carry)
+        solution, residual = step(carry, False)[:2]
         return (solution, residual)
 
     return on_device

time: 720 us -> 738 us (1.025)
  blocking collectives: 433 us -> 310 us
  waiting for transfers between devices: 76.9 us -> 167 us
  starting transfers between devices: 45.1 us -> 92.2 us
  local copies, waits for them, and re-layouts: 24.9 us -> 33.1 us
    all_to_all x7 -> x0, blocking collectives: 72.4 us -> none  [fetch(): y = lax.all_to_all(x, 'col', 1, 1, tiled=True)]
    all_to_all x1 -> x8, waiting for transfers between devices: 5.02 us -> 57.5 us  [fetch(): y = lax.all_to_all(x, 'col', 1, 1, tiled=True)]
    all_to_all x14 -> x9, blocking collectives: 148 us -> 99.6 us  [all_reduce(): return lax.all_to_all(jnp.tile(part, (1, n)), axis, 1, 1, tiled=True)]
    all_to_all x2 -> x7, waiting for transfers between devices: 13.8 us -> 45.5 us  [all_reduce(): return lax.all_to_all(jnp.tile(part, (1, n)), axis, 1, 1, tiled=True)]
    all_to_all x1 -> x8, starting transfers between devices: 8.59 us -> 33.3 us  [fetch(): y = lax.all_to_all(x, 'col', 1, 1, tiled=True)]
    all_to_all x2 -> x7, starting transfers between devices: 7.91 us -> 30.5 us  [all_reduce(): return lax.all_to_all(jnp.tile(part, (1, n)), axis, 1, 1, tiled=True)]
    while x0 -> x56, local copies, waits for them, and re-layouts: none -> 8.27 us
    unnamed x65 -> x9, local copies, waits for them, and re-layouts: 10.1 us -> 2.12 us
  transfers between devices with their start and end apart: 11 -> 23, of which waited for: 11 -> 23; matrix products, arithmetic and copies ran while one was open for 1% -> 0% of each run, Pallas kernels for 0% -> 0%
where the time goes in v10:
time: 738 us; the launch traced here: 732 us
  blocking collectives  310 us (42%)
  waiting for transfers between devices  167 us (23%)
  Pallas kernels  95.9 us (13%)
  starting transfers between devices  92.2 us (12%)
  local copies, waits for them, and re-layouts  33.1 us (4%)
  other arithmetic  28.3 us (4%)
    all_to_all x16, blocking collectives, all_reduce(): y = lax.all_to_all(x, axis, 1, 1, tiled=True)  211 us
    all_to_all x9, blocking collectives, all_reduce(): return lax.all_to_all(jnp.tile(part, (1, n)), axis, 1, 1, tiled=True)  99.6 us
    pallas_call x8, Pallas kernels, block_products(): pl.pallas_call(products_kernel, grid_spec=grid_spec, out_shape=[jax.Shape...  95.9 us
    all_to_all x8, waiting for transfers between devices, fetch(): z = lax.all_to_all(jnp.tile(kept, (1, n_col)), 'col', 1, 1, tiled=True)  64.4 us
    all_to_all x8, waiting for transfers between devices, fetch(): y = lax.all_to_all(x, 'col', 1, 1, tiled=True)  57.5 us
    all_to_all x7, waiting for transfers between devices, all_reduce(): return lax.all_to_all(jnp.tile(part, (1, n)), axis, 1, 1, tiled=True)  45.5 us
    all_to_all x8, starting transfers between devices, fetch(): y = lax.all_to_all(x, 'col', 1, 1, tiled=True)  33.3 us
    all_to_all x7, starting transfers between devices, all_reduce(): return lax.all_to_all(jnp.tile(part, (1, n)), axis, 1, 1, tiled=True)  30.5 us
  transfers between devices with their start and end apart: 23, of which 23 were waited for; matrix products, arithmetic and copies ran while one was open for 0% of the time, Pallas kernels for 0%

profile of v10, /device:TPU:1, one launch (start us, length us, event | category | flops | bytes accessed | tf_op | source)
XLA Modules:
  0.0 732.4 jit_solution(9737243562173821674)
XLA Ops:
  31.7 636.1 %while.27 = (s32[]{:T(128)}, f32[24,2048]{1,0:T(8,128)S(1)}, f32[24,2048]{1,0:T(8,128)S(1)}, f32[24,2048]{1,0:T(8,128)S(1)}, f32[2,24,2048]{2,1,0:T(8,128)S(1)},...) while((s32[]{:T(128)}, f32[24,2048]{1,0:T(8,128)S(1)}, ...), condition=%wide.region_9.10_spmd.clone, body=%wide.region_2.9_spmd.clone.sunk | while | flops 1747331 | bytes 22028252 | solution.py:139
  32.7 12.0 %eval_jaxpr.4 = (f32[2,24,2048]{2,1,0:T(8,128)}, f32[24,2048]{1,0:T(8,128)}, f32[24,128]{1,0:T(8,128)}) custom-call(s32[2]{0:T(128)S(1)} %get-tuple-element.507.flags_ref, f32[24,2048]{1,0:T(8,128)S(1)} %get-tuple-element.487.d_ref, f32[2,24,2048]{2,1,0:T(8,128)S(1)} %get-tuple-element.488.di_ref, bf16[2,1,2048,2048]{3,2,1,0:T(8,128)(2,1)} %get-tuple-element.508.k_ref), custom_call_target="tpu_custom_call" | custom-call | tf_op jit(solution)/shard_map/while/body/eval_jaxpr/pallas_call | solution.py:69
  46.8 11.3 %all_to_all.124 = f32[56,16,128]{2,0,1:T(8,128)S(1)} all-to-all(f32[56,16,128]{2,0,1:T(8,128)S(1)} %pad_maximum_fusion.9), channel_id=1, replica_groups=mesh['row'=8,'col'=16] {'col'}, dimensions={1} | all-to-all | bytes 917504 | tf_op jit(solution)/shard_map/while/body/eval_jaxpr/all_to_all | solution.py:15
  58.2 11.2 %all_to_all.125 = f32[56,16,128]{2,0,1:T(8,128)S(1)} all-to-all(f32[56,16,128]{2,0,1:T(8,128)S(1)} %tile.36), channel_id=1, replica_groups=mesh['row'=8,'col'=16] {'col'}, dimensions={1} | all-to-all | bytes 917504 | tf_op jit(solution)/shard_map/while/body/eval_jaxpr/all_to_all | solution.py:17
  70.5 16.4 %all_to_all.126 = f32[32,8,256]{2,0,1:T(8,128)S(1)} all-to-all(f32[32,8,256]{2,0,1:T(8,128)S(1)} %bitcast.158), channel_id=1, replica_groups=mesh['row'=8,'col'=16] {'row'}, dimensions={1} | all-to-all | bytes 524288 | tf_op jit(solution)/shard_map/while/body/eval_jaxpr/all_to_all | solution.py:15
  124.8 12.0 %eval_jaxpr.4 = (f32[2,24,2048]{2,1,0:T(8,128)}, f32[24,2048]{1,0:T(8,128)}, f32[24,128]{1,0:T(8,128)}) custom-call(s32[2]{0:T(128)S(1)} %get-tuple-element.507.flags_ref, f32[24,2048]{1,0:T(8,128)S(1)} %get-tuple-element.487.d_ref, f32[2,24,2048]{2,1,0:T(8,128)S(1)} %get-tuple-element.488.di_ref, bf16[2,1,2048,2048]{3,2,1,0:T(8,128)(2,1)} %get-tuple-element.508.k_ref), custom_call_target="tpu_custom_call" | custom-call | tf_op jit(solution)/shard_map/while/body/eval_jaxpr/pallas_call | solution.py:69
  139.0 11.5 %all_to_all.124 = f32[56,16,128]{2,0,1:T(8,128)S(1)} all-to-all(f32[56,16,128]{2,0,1:T(8,128)S(1)} %pad_maximum_fusion.9), channel_id=1, replica_groups=mesh['row'=8,'col'=16] {'col'}, dimensions={1} | all-to-all | bytes 917504 | tf_op jit(solution)/shard_map/while/body/eval_jaxpr/all_to_all | solution.py:15
  150.5 11.2 %all_to_all.125 = f32[56,16,128]{2,0,1:T(8,128)S(1)} all-to-all(f32[56,16,128]{2,0,1:T(8,128)S(1)} %tile.36), channel_id=1, replica_groups=mesh['row'=8,'col'=16] {'col'}, dimensions={1} | all-to-all | bytes 917504 | tf_op jit(solution)/shard_map/while/body/eval_jaxpr/all_to_all | solution.py:17
  162.8 14.7 %all_to_all.126 = f32[32,8,256]{2,0,1:T(8,128)S(1)} all-to-all(f32[32,8,256]{2,0,1:T(8,128)S(1)} %bitcast.158), channel_id=1, replica_groups=mesh['row'=8,'col'=16] {'row'}, dimensions={1} | all-to-all | bytes 524288 | tf_op jit(solution)/shard_map/while/body/eval_jaxpr/all_to_all | solution.py:15
  215.5 12.0 %eval_jaxpr.4 = (f32[2,24,2048]{2,1,0:T(8,128)}, f32[24,2048]{1,0:T(8,128)}, f32[24,128]{1,0:T(8,128)}) custom-call(s32[2]{0:T(128)S(1)} %get-tuple-element.507.flags_ref, f32[24,2048]{1,0:T(8,128)S(1)} %get-tuple-element.487.d_ref, f32[2,24,2048]{2,1,0:T(8,128)S(1)} %get-tuple-element.488.di_ref, bf16[2,1,2048,2048]{3,2,1,0:T(8,128)(2,1)} %get-tuple-element.508.k_ref), custom_call_target="tpu_custom_call" | custom-call | tf_op jit(solution)/shard_map/while/body/eval_jaxpr/pallas_call | solution.py:69
  229.7 11.5 %all_to_all.124 = f32[56,16,128]{2,0,1:T(8,128)S(1)} all-to-all(f32[56,16,128]{2,0,1:T(8,128)S(1)} %pad_maximum_fusion.9), channel_id=1, replica_groups=mesh['row'=8,'col'=16] {'col'}, dimensions={1} | all-to-all | bytes 917504 | tf_op jit(solution)/shard_map/while/body/eval_jaxpr/all_to_all | solution.py:15
  241.2 11.2 %all_to_all.125 = f32[56,16,128]{2,0,1:T(8,128)S(1)} all-to-all(f32[56,16,128]{2,0,1:T(8,128)S(1)} %tile.36), channel_id=1, replica_groups=mesh['row'=8,'col'=16] {'col'}, dimensions={1} | all-to-all | bytes 917504 | tf_op jit(solution)/shard_map/while/body/eval_jaxpr/all_to_all | solution.py:17
  253.5 14.7 %all_to_all.126 = f32[32,8,256]{2,0,1:T(8,128)S(1)} all-to-all(f32[32,8,256]{2,0,1:T(8,128)S(1)} %bitcast.158), channel_id=1, replica_groups=mesh['row'=8,'col'=16] {'row'}, dimensions={1} | all-to-all | bytes 524288 | tf_op jit(solution)/shard_map/while/body/eval_jaxpr/all_to_all | solution.py:15
  306.2 12.0 %eval_jaxpr.4 = (f32[2,24,2048]{2,1,0:T(8,128)}, f32[24,2048]{1,0:T(8,128)}, f32[24,128]{1,0:T(8,128)}) custom-call(s32[2]{0:T(128)S(1)} %get-tuple-element.507.flags_ref, f32[24,2048]{1,0:T(8,128)S(1)} %get-tuple-element.487.d_ref, f32[2,24,2048]{2,1,0:T(8,128)S(1)} %get-tuple-element.488.di_ref, bf16[2,1,2048,2048]{3,2,1,0:T(8,128)(2,1)} %get-tuple-element.508.k_ref), custom_call_target="tpu_custom_call" | custom-call | tf_op jit(solution)/shard_map/while/body/eval_jaxpr/pallas_call | solution.py:69
  320.3 11.5 %all_to_all.124 = f32[56,16,128]{2,0,1:T(8,128)S(1)} all-to-all(f32[56,16,128]{2,0,1:T(8,128)S(1)} %pad_maximum_fusion.9), channel_id=1, replica_groups=mesh['row'=8,'col'=16] {'col'}, dimensions={1} | all-to-all | bytes 917504 | tf_op jit(solution)/shard_map/while/body/eval_jaxpr/all_to_all | solution.py:15
  331.8 11.2 %all_to_all.125 = f32[56,16,128]{2,0,1:T(8,128)S(1)} all-to-all(f32[56,16,128]{2,0,1:T(8,128)S(1)} %tile.36), channel_id=1, replica_groups=mesh['row'=8,'col'=16] {'col'}, dimensions={1} | all-to-all | bytes 917504 | tf_op jit(solution)/shard_map/while/body/eval_jaxpr/all_to_all | solution.py:17
  344.2 14.7 %all_to_all.126 = f32[32,8,256]{2,0,1:T(8,128)S(1)} all-to-all(f32[32,8,256]{2,0,1:T(8,128)S(1)} %bitcast.158), channel_id=1, replica_groups=mesh['row'=8,'col'=16] {'row'}, dimensions={1} | all-to-all | bytes 524288 | tf_op jit(solution)/shard_map/while/body/eval_jaxpr/all_to_all | solution.py:15
  396.8 12.0 %eval_jaxpr.4 = (f32[2,24,2048]{2,1,0:T(8,128)}, f32[24,2048]{1,0:T(8,128)}, f32[24,128]{1,0:T(8,128)}) custom-call(s32[2]{0:T(128)S(1)} %get-tuple-element.507.flags_ref, f32[24,2048]{1,0:T(8,128)S(1)} %get-tuple-element.487.d_ref, f32[2,24,2048]{2,1,0:T(8,128)S(1)} %get-tuple-element.488.di_ref, bf16[2,1,2048,2048]{3,2,1,0:T(8,128)(2,1)} %get-tuple-element.508.k_ref), custom_call_target="tpu_custom_call" | custom-call | tf_op jit(solution)/shard_map/while/body/eval_jaxpr/pallas_call | solution.py:69
  411.0 11.5 %all_to_all.124 = f32[56,16,128]{2,0,1:T(8,128)S(1)} all-to-all(f32[56,16,128]{2,0,1:T(8,128)S(1)} %pad_maximum_fusion.9), channel_id=1, replica_groups=mesh['row'=8,'col'=16] {'col'}, dimensions={1} | all-to-all | bytes 917504 | tf_op jit(solution)/shard_map/while/body/eval_jaxpr/all_to_all | solution.py:15
  422.5 11.2 %all_to_all.125 = f32[56,16,128]{2,0,1:T(8,128)S(1)} all-to-all(f32[56,16,128]{2,0,1:T(8,128)S(1)} %tile.36), channel_id=1, replica_groups=mesh['row'=8,'col'=16] {'col'}, dimensions={1} | all-to-all | bytes 917504 | tf_op jit(solution)/shard_map/while/body/eval_jaxpr/all_to_all | solution.py:17
  434.8 14.7 %all_to_all.126 = f32[32,8,256]{2,0,1:T(8,128)S(1)} all-to-all(f32[32,8,256]{2,0,1:T(8,128)S(1)} %bitcast.158), channel_id=1, replica_groups=mesh['row'=8,'col'=16] {'row'}, dimensions={1} | all-to-all | bytes 524288 | tf_op jit(solution)/shard_map/while/body/eval_jaxpr/all_to_all | solution.py:15
  487.5 12.0 %eval_jaxpr.4 = (f32[2,24,2048]{2,1,0:T(8,128)}, f32[24,2048]{1,0:T(8,128)}, f32[24,128]{1,0:T(8,128)}) custom-call(s32[2]{0:T(128)S(1)} %get-tuple-element.507.flags_ref, f32[24,2048]{1,0:T(8,128)S(1)} %get-tuple-element.487.d_ref, f32[2,24,2048]{2,1,0:T(8,128)S(1)} %get-tuple-element.488.di_ref, bf16[2,1,2048,2048]{3,2,1,0:T(8,128)(2,1)} %get-tuple-element.508.k_ref), custom_call_target="tpu_custom_call" | custom-call | tf_op jit(solution)/shard_map/while/body/eval_jaxpr/pallas_call | solution.py:69
  501.6 11.5 %all_to_all.124 = f32[56,16,128]{2,0,1:T(8,128)S(1)} all-to-all(f32[56,16,128]{2,0,1:T(8,128)S(1)} %pad_maximum_fusion.9), channel_id=1, replica_groups=mesh['row'=8,'col'=16] {'col'}, dimensions={1} | all-to-all | bytes 917504 | tf_op jit(solution)/shard_map/while/body/eval_jaxpr/all_to_all | solution.py:15
  513.2 11.2 %all_to_all.125 = f32[56,16,128]{2,0,1:T(8,128)S(1)} all-to-all(f32[56,16,128]{2,0,1:T(8,128)S(1)} %tile.36), channel_id=1, replica_groups=mesh['row'=8,'col'=16] {'col'}, dimensions={1} | all-to-all | bytes 917504 | tf_op jit(solution)/shard_map/while/body/eval_jaxpr/all_to_all | solution.py:17
  525.5 14.7 %all_to_all.126 = f32[32,8,256]{2,0,1:T(8,128)S(1)} all-to-all(f32[32,8,256]{2,0,1:T(8,128)S(1)} %bitcast.158), channel_id=1, replica_groups=mesh['row'=8,'col'=16] {'row'}, dimensions={1} | all-to-all | bytes 524288 | tf_op jit(solution)/shard_map/while/body/eval_jaxpr/all_to_all | solution.py:15
  578.1 12.0 %eval_jaxpr.4 = (f32[2,24,2048]{2,1,0:T(8,128)}, f32[24,2048]{1,0:T(8,128)}, f32[24,128]{1,0:T(8,128)}) custom-call(s32[2]{0:T(128)S(1)} %get-tuple-element.507.flags_ref, f32[24,2048]{1,0:T(8,128)S(1)} %get-tuple-element.487.d_ref, f32[2,24,2048]{2,1,0:T(8,128)S(1)} %get-tuple-element.488.di_ref, bf16[2,1,2048,2048]{3,2,1,0:T(8,128)(2,1)} %get-tuple-element.508.k_ref), custom_call_target="tpu_custom_call" | custom-call | tf_op jit(solution)/shard_map/while/body/eval_jaxpr/pallas_call | solution.py:69
  592.3 11.5 %all_to_all.124 = f32[56,16,128]{2,0,1:T(8,128)S(1)} all-to-all(f32[56,16,128]{2,0,1:T(8,128)S(1)} %pad_maximum_fusion.9), channel_id=1, replica_groups=mesh['row'=8,'col'=16] {'col'}, dimensions={1} | all-to-all | bytes 917504 | tf_op jit(solution)/shard_map/while/body/eval_jaxpr/all_to_all | solution.py:15
  616.1 14.7 %all_to_all.126 = f32[32,8,256]{2,0,1:T(8,128)S(1)} all-to-all(f32[32,8,256]{2,0,1:T(8,128)S(1)} %bitcast.158), channel_id=1, replica_groups=mesh['row'=8,'col'=16] {'row'}, dimensions={1} | all-to-all | bytes 524288 | tf_op jit(solution)/shard_map/while/body/eval_jaxpr/all_to_all | solution.py:15
  668.8 12.0 %shard_map.59 = (f32[2,24,2048]{2,1,0:T(8,128)}, f32[24,2048]{1,0:T(8,128)}, f32[24,128]{1,0:T(8,128)}) custom-call(s32[2]{0:T(128)S(1)} %get-tuple-element.525, f32[24,2048]{1,0:T(8,128)S(1)} %get-tuple-element.257.d_ref, f32[2,24,2048]{2,1,0:T(8,128)S(1)} %get-tuple-element.258.di_ref, bf16[2,1,2048,2048]{3,2,1,0:T(8,128)(2,1)} %get-tuple-element.518), custom_call_target="tpu_custom_call" | custom-call | tf_op jit(solution)/shard_map/pallas_call | solution.py:69
  682.9 11.5 %all_to_all.120 = f32[56,16,128]{2,0,1:T(8,128)S(1)} all-to-all(f32[56,16,128]{2,0,1:T(8,128)S(1)} %pad_maximum_fusion.3), channel_id=1, replica_groups=mesh['row'=8,'col'=16] {'col'}, dimensions={1} | all-to-all | bytes 917504 | tf_op jit(solution)/shard_map/all_to_all | solution.py:15
  694.5 11.2 %all_to_all.121 = f32[56,16,128]{2,0,1:T(8,128)S(1)} all-to-all(f32[56,16,128]{2,0,1:T(8,128)S(1)} %tile.13), channel_id=1, replica_groups=mesh['row'=8,'col'=16] {'col'}, dimensions={1} | all-to-all | bytes 917504 | tf_op jit(solution)/shard_map/all_to_all | solution.py:17
  706.8 14.7 %all_to_all.122 = f32[32,8,256]{2,0,1:T(8,128)S(1)} all-to-all(f32[32,8,256]{2,0,1:T(8,128)S(1)} %bitcast.171), channel_id=1, replica_groups=mesh['row'=8,'col'=16] {'row'}, dimensions={1} | all-to-all | bytes 524288 | tf_op jit(solution)/shard_map/all_to_all | solution.py:15
  (402 shorter events, 342.0 us)
Async XLA Ops:
  2.6 16.1 %all-to-all-start.6 = ((f32[32,16,128]{2,0,1:T(8,128)}), f32[32,16,128]{2,0,1:T(8,128)S(1)}, u32[]{:S(2)}, u32[]{:S(2)}) async-start(f32[32,16,128]{2,0,1:T(8,128)} %copy.31), calls=%async_computation.6 | async-start | bytes 524288 | tf_op jit(solution)/shard_map/all_to_all | solution.py:105
  19.5 12.0 %all-to-all-start.7 = ((f32[48,16,128]{2,0,1:T(8,128)}), f32[48,16,128]{2,0,1:T(8,128)S(1)}, u32[]{:S(2)}, u32[]{:S(2)}) async-start(f32[48,16,128]{2,0,1:T(8,128)} %tile.12), calls=%async_computation.7 | async-start | bytes 786432 | tf_op jit(solution)/shard_map/all_to_all | solution.py:110
  31.7 66.8 %copy-start = (f32[1,2048]{1,0:T(1,128)S(1)}, f32[1,2048]{1,0:T(1,128)}, u32[]{:S(2)}) copy-start(f32[1,2048]{1,0:T(1,128)} %get-tuple-element.511) | copy-start | bytes 24580 | tf_op jit(solution)/shard_map/while
  87.6 10.8 %all-to-all-start.3 = ((f32[32,8,256]{2,0,1:T(8,128)}), f32[32,8,256]{2,0,1:T(8,128)S(1)}, u32[]{:S(2)}, u32[]{:S(2)}) async-start(f32[32,8,256]{2,0,1:T(8,128)} %tile.37), calls=%async_computation.3 | async-start | bytes 524288 | tf_op jit(solution)/shard_map/while/body/eval_jaxpr/all_to_all | solution.py:17
  99.7 11.0 %all-to-all-start.4 = ((f32[32,16,128]{2,0,1:T(8,128)}), f32[32,16,128]{2,0,1:T(8,128)S(1)}, u32[]{:S(2)}, u32[]{:S(2)}) async-start(f32[32,16,128]{2,0,1:T(8,128)} %copy.100), calls=%async_computation.4 | async-start | bytes 524288 | tf_op jit(solution)/shard_map/while/body/eval_jaxpr/all_to_all | solution.py:105
  111.6 11.9 %all-to-all-start.5 = ((f32[48,16,128]{2,0,1:T(8,128)}), f32[48,16,128]{2,0,1:T(8,128)S(1)}, u32[]{:S(2)}, u32[]{:S(2)}) async-start(f32[48,16,128]{2,0,1:T(8,128)} %tile.38), calls=%async_computation.5 | async-start | bytes 786432 | tf_op jit(solution)/shard_map/while/body/eval_jaxpr/all_to_all | solution.py:110
  123.9 65.3 %copy-start = (f32[1,2048]{1,0:T(1,128)S(1)}, f32[1,2048]{1,0:T(1,128)}, u32[]{:S(2)}) copy-start(f32[1,2048]{1,0:T(1,128)} %get-tuple-element.511) | copy-start | bytes 24580 | tf_op jit(solution)/shard_map/while
  178.3 10.8 %all-to-all-start.3 = ((f32[32,8,256]{2,0,1:T(8,128)}), f32[32,8,256]{2,0,1:T(8,128)S(1)}, u32[]{:S(2)}, u32[]{:S(2)}) async-start(f32[32,8,256]{2,0,1:T(8,128)} %tile.37), calls=%async_computation.3 | async-start | bytes 524288 | tf_op jit(solution)/shard_map/while/body/eval_jaxpr/all_to_all | solution.py:17
  190.4 11.0 %all-to-all-start.4 = ((f32[32,16,128]{2,0,1:T(8,128)}), f32[32,16,128]{2,0,1:T(8,128)S(1)}, u32[]{:S(2)}, u32[]{:S(2)}) async-start(f32[32,16,128]{2,0,1:T(8,128)} %copy.100), calls=%async_computation.4 | async-start | bytes 524288 | tf_op jit(solution)/shard_map/while/body/eval_jaxpr/all_to_all | solution.py:105
  202.3 11.9 %all-to-all-start.5 = ((f32[48,16,128]{2,0,1:T(8,128)}), f32[48,16,128]{2,0,1:T(8,128)S(1)}, u32[]{:S(2)}, u32[]{:S(2)}) async-start(f32[48,16,128]{2,0,1:T(8,128)} %tile.38), calls=%async_computation.5 | async-start | bytes 786432 | tf_op jit(solution)/shard_map/while/body/eval_jaxpr/all_to_all | solution.py:110
  214.6 65.3 %copy-start = (f32[1,2048]{1,0:T(1,128)S(1)}, f32[1,2048]{1,0:T(1,128)}, u32[]{:S(2)}) copy-start(f32[1,2048]{1,0:T(1,128)} %get-tuple-element.511) | copy-start | bytes 24580 | tf_op jit(solution)/shard_map/while
  268.9 10.8 %all-to-all-start.3 = ((f32[32,8,256]{2,0,1:T(8,128)}), f32[32,8,256]{2,0,1:T(8,128)S(1)}, u32[]{:S(2)}, u32[]{:S(2)}) async-start(f32[32,8,256]{2,0,1:T(8,128)} %tile.37), calls=%async_computation.3 | async-start | bytes 524288 | tf_op jit(solution)/shard_map/while/body/eval_jaxpr/all_to_all | solution.py:17
  281.0 11.0 %all-to-all-start.4 = ((f32[32,16,128]{2,0,1:T(8,128)}), f32[32,16,128]{2,0,1:T(8,128)S(1)}, u32[]{:S(2)}, u32[]{:S(2)}) async-start(f32[32,16,128]{2,0,1:T(8,128)} %copy.100), calls=%async_computation.4 | async-start | bytes 524288 | tf_op jit(solution)/shard_map/while/body/eval_jaxpr/all_to_all | solution.py:105
  292.9 11.9 %all-to-all-start.5 = ((f32[48,16,128]{2,0,1:T(8,128)}), f32[48,16,128]{2,0,1:T(8,128)S(1)}, u32[]{:S(2)}, u32[]{:S(2)}) async-start(f32[48,16,128]{2,0,1:T(8,128)} %tile.38), calls=%async_computation.5 | async-start | bytes 786432 | tf_op jit(solution)/shard_map/while/body/eval_jaxpr/all_to_all | solution.py:110
  305.2 65.3 %copy-start = (f32[1,2048]{1,0:T(1,128)S(1)}, f32[1,2048]{1,0:T(1,128)}, u32[]{:S(2)}) copy-start(f32[1,2048]{1,0:T(1,128)} %get-tuple-element.511) | copy-start | bytes 24580 | tf_op jit(solution)/shard_map/while
  359.6 10.8 %all-to-all-start.3 = ((f32[32,8,256]{2,0,1:T(8,128)}), f32[32,8,256]{2,0,1:T(8,128)S(1)}, u32[]{:S(2)}, u32[]{:S(2)}) async-start(f32[32,8,256]{2,0,1:T(8,128)} %tile.37), calls=%async_computation.3 | async-start | bytes 524288 | tf_op jit(solution)/shard_map/while/body/eval_jaxpr/all_to_all | solution.py:17
  371.7 11.0 %all-to-all-start.4 = ((f32[32,16,128]{2,0,1:T(8,128)}), f32[32,16,128]{2,0,1:T(8,128)S(1)}, u32[]{:S(2)}, u32[]{:S(2)}) async-start(f32[32,16,128]{2,0,1:T(8,128)} %copy.100), calls=%async_computation.4 | async-start | bytes 524288 | tf_op jit(solution)/shard_map/while/body/eval_jaxpr/all_to_all | solution.py:105
  383.6 11.9 %all-to-all-start.5 = ((f32[48,16,128]{2,0,1:T(8,128)}), f32[48,16,128]{2,0,1:T(8,128)S(1)}, u32[]{:S(2)}, u32[]{:S(2)}) async-start(f32[48,16,128]{2,0,1:T(8,128)} %tile.38), calls=%async_computation.5 | async-start | bytes 786432 | tf_op jit(solution)/shard_map/while/body/eval_jaxpr/all_to_all | solution.py:110
  395.9 65.3 %copy-start = (f32[1,2048]{1,0:T(1,128)S(1)}, f32[1,2048]{1,0:T(1,128)}, u32[]{:S(2)}) copy-start(f32[1,2048]{1,0:T(1,128)} %get-tuple-element.511) | copy-start | bytes 24580 | tf_op jit(solution)/shard_map/while
  450.2 10.8 %all-to-all-start.3 = ((f32[32,8,256]{2,0,1:T(8,128)}), f32[32,8,256]{2,0,1:T(8,128)S(1)}, u32[]{:S(2)}, u32[]{:S(2)}) async-start(f32[32,8,256]{2,0,1:T(8,128)} %tile.37), calls=%async_computation.3 | async-start | bytes 524288 | tf_op jit(solution)/shard_map/while/body/eval_jaxpr/all_to_all | solution.py:17
  462.3 11.0 %all-to-all-start.4 = ((f32[32,16,128]{2,0,1:T(8,128)}), f32[32,16,128]{2,0,1:T(8,128)S(1)}, u32[]{:S(2)}, u32[]{:S(2)}) async-start(f32[32,16,128]{2,0,1:T(8,128)} %copy.100), calls=%async_computation.4 | async-start | bytes 524288 | tf_op jit(solution)/shard_map/while/body/eval_jaxpr/all_to_all | solution.py:105
  474.2 11.9 %all-to-all-start.5 = ((f32[48,16,128]{2,0,1:T(8,128)}), f32[48,16,128]{2,0,1:T(8,128)S(1)}, u32[]{:S(2)}, u32[]{:S(2)}) async-start(f32[48,16,128]{2,0,1:T(8,128)} %tile.38), calls=%async_computation.5 | async-start | bytes 786432 | tf_op jit(solution)/shard_map/while/body/eval_jaxpr/all_to_all | solution.py:110
  486.6 65.3 %copy-start = (f32[1,2048]{1,0:T(1,128)S(1)}, f32[1,2048]{1,0:T(1,128)}, u32[]{:S(2)}) copy-start(f32[1,2048]{1,0:T(1,128)} %get-tuple-element.511) | copy-start | bytes 24580 | tf_op jit(solution)/shard_map/while
  540.9 10.8 %all-to-all-start.3 = ((f32[32,8,256]{2,0,1:T(8,128)}), f32[32,8,256]{2,0,1:T(8,128)S(1)}, u32[]{:S(2)}, u32[]{:S(2)}) async-start(f32[32,8,256]{2,0,1:T(8,128)} %tile.37), calls=%async_computation.3 | async-start | bytes 524288 | tf_op jit(solution)/shard_map/while/body/eval_jaxpr/all_to_all | solution.py:17
  553.0 11.0 %all-to-all-start.4 = ((f32[32,16,128]{2,0,1:T(8,128)}), f32[32,16,128]{2,0,1:T(8,128)S(1)}, u32[]{:S(2)}, u32[]{:S(2)}) async-start(f32[32,16,128]{2,0,1:T(8,128)} %copy.100), calls=%async_computation.4 | async-start | bytes 524288 | tf_op jit(solution)/shard_map/while/body/eval_jaxpr/all_to_all | solution.py:105
  564.9 11.9 %all-to-all-start.5 = ((f32[48,16,128]{2,0,1:T(8,128)}), f32[48,16,128]{2,0,1:T(8,128)S(1)}, u32[]{:S(2)}, u32[]{:S(2)}) async-start(f32[48,16,128]{2,0,1:T(8,128)} %tile.38), calls=%async_computation.5 | async-start | bytes 786432 | tf_op jit(solution)/shard_map/while/body/eval_jaxpr/all_to_all | solution.py:110
  577.2 65.3 %copy-start = (f32[1,2048]{1,0:T(1,128)S(1)}, f32[1,2048]{1,0:T(1,128)}, u32[]{:S(2)}) copy-start(f32[1,2048]{1,0:T(1,128)} %get-tuple-element.511) | copy-start | bytes 24580 | tf_op jit(solution)/shard_map/while
  631.6 10.8 %all-to-all-start.3 = ((f32[32,8,256]{2,0,1:T(8,128)}), f32[32,8,256]{2,0,1:T(8,128)S(1)}, u32[]{:S(2)}, u32[]{:S(2)}) async-start(f32[32,8,256]{2,0,1:T(8,128)} %tile.37), calls=%async_computation.3 | async-start | bytes 524288 | tf_op jit(solution)/shard_map/while/body/eval_jaxpr/all_to_all | solution.py:17
  643.6 11.0 %all-to-all-start.4 = ((f32[32,16,128]{2,0,1:T(8,128)}), f32[32,16,128]{2,0,1:T(8,128)S(1)}, u32[]{:S(2)}, u32[]{:S(2)}) async-start(f32[32,16,128]{2,0,1:T(8,128)} %copy.100), calls=%async_computation.4 | async-start | bytes 524288 | tf_op jit(solution)/shard_map/while/body/eval_jaxpr/all_to_all | solution.py:105
  655.6 11.9 %all-to-all-start.5 = ((f32[48,16,128]{2,0,1:T(8,128)}), f32[48,16,128]{2,0,1:T(8,128)S(1)}, u32[]{:S(2)}, u32[]{:S(2)}) async-start(f32[48,16,128]{2,0,1:T(8,128)} %tile.38), calls=%async_computation.5 | async-start | bytes 786432 | tf_op jit(solution)/shard_map/while/body/eval_jaxpr/all_to_all | solution.py:110
  667.9 63.6 %copy-start.1 = (f32[1,2048]{1,0:T(1,128)S(1)}, f32[1,2048]{1,0:T(1,128)}, u32[]{:S(2)}) copy-start(f32[1,2048]{1,0:T(1,128)} %get-tuple-element.523) | copy-start | bytes 24580

commit v11 on v9

--- a/solution.py
+++ b/solution.py
@@ -17,7 +17,7 @@
     return lax.all_to_all(jnp.tile(part, (1, n)), axis, 1, 1, tiled=True)
 
 
-def products_kernel(flags_ref, d_ref, di_ref, k_ref, fwd_ref, m_ref, p_ref):
+def products_kernel(flags_ref, d_ref, nz_ref, di_ref, k_ref, fwd_ref, m_ref, p_ref):
     k = pl.program_id(0)
     i = pl.program_id(1)
 
@@ -44,12 +44,14 @@
     @pl.when((k == pl.num_programs(0) - 1) & (i == pl.num_programs(1) - 1))
     def _():
         acc = p_ref[...]
+        scale = jnp.where(flags_ref[k + 1] != 0, 1.0, 0.0)
         for j in range(m_ref.shape[1] // 128):
-            acc = acc + d_ref[:, j * 128:(j + 1) * 128] * m_ref[:, j * 128:(j + 1) * 128]
+            dj = d_ref[:, j * 128:(j + 1) * 128]
+            acc = acc + dj * m_ref[:, j * 128:(j + 1) * 128] + scale * (dj * (nz_ref[:, j * 128:(j + 1) * 128] * dj))
         p_ref[...] = acc
 
 
-def block_products(flags, d, di, blocks, tile=1024):
+def block_products(flags, d, nz, di, blocks, tile=1024):
     nb, _, order, _ = blocks.shape
     vecs = d.shape[0]
     grid_spec = pltpu.PrefetchScalarGridSpec(
@@ -57,6 +59,7 @@
         grid=(nb, order // tile),
         in_specs=[
             pl.BlockSpec((vecs, order), lambda k, i, f: (0, 0)),
+            pl.BlockSpec((1, order), lambda k, i, f: (0, 0)),
             pl.BlockSpec((None, vecs, tile), lambda k, i, f: (k, 0, i)),
             pl.BlockSpec((None, None, tile, order), lambda k, i, f: (k, 0, i, 0)),
         ],
@@ -75,7 +78,7 @@
             jax.ShapeDtypeStruct((vecs, 128), jnp.float32),
         ],
         compiler_params=pltpu.CompilerParams(dimension_semantics=("arbitrary", "arbitrary")),
-    )(flags, d, di, blocks)
+    )(flags, d, nz, di, blocks)
 
 
 def pack(blocks, scalars):
@@ -93,7 +96,7 @@
         vecs, width = rhs.shape
         col = lax.axis_index("col")
         first_row = lax.axis_index("row") == 0
-        flags = (col >= rows).astype(jnp.int32)
+        flags = jnp.concatenate([(col >= rows).astype(jnp.int32), (lax.axis_index("row") == 0).astype(jnp.int32)[None]])
         owner = [col == rows[k] for k in range(nb)]
         noise = noise_var[None, :]
 
@@ -115,10 +118,9 @@
         direction = rhs
         dir_rows, norm_now = fetch(rhs)
         for step in range(ITERS):
-            fwd, mirrored, lanes = block_products(flags, direction, dir_rows, blocks)
+            fwd, mirrored, lanes = block_products(flags, direction, noise, dir_rows, blocks)
             forward = [fwd[k] for k in range(nb)]
             part = jnp.sum(lanes, axis=1)
-            part = part + jnp.where(first_row, jnp.sum(direction * (noise * direction), axis=1), 0.0)
             out = all_reduce(pack(forward, part), "col", n_col)
             terms = mirrored
             for k in range(nb):

time: 720 us -> 720 us (level)
    reduce_sum x8 -> x0, other arithmetic: 7.29 us -> none  [on_device(): jnp.sum(direction * (noise * direction), axis=1)]
where the time goes in v11:
time: 720 us; the launch traced here: 716 us
  blocking collectives  433 us (60%)
  Pallas kernels  98.8 us (14%)
  waiting for transfers between devices  78 us (11%)
  starting transfers between devices  45.1 us (6%)
  other arithmetic  31.9 us (4%)
  local copies, waits for them, and re-layouts  24.9 us (3%)
    all_to_all x16, blocking collectives, all_reduce(): y = lax.all_to_all(x, axis, 1, 1, tiled=True)  212 us
    all_to_all x14, blocking collectives, all_reduce(): return lax.all_to_all(jnp.tile(part, (1, n)), axis, 1, 1, tiled=True)  148 us
    pallas_call x8, Pallas kernels, block_products(): pl.pallas_call(products_kernel, grid_spec=grid_spec, out_shape=[jax.Shape...  98.8 us
    all_to_all x7, blocking collectives, fetch(): y = lax.all_to_all(x, 'col', 1, 1, tiled=True)  72.4 us
    all_to_all x8, waiting for transfers between devices, fetch(): z = lax.all_to_all(jnp.tile(kept, (1, n_col)), 'col', 1, 1, tiled=True)  59.2 us
    all_to_all x8, starting transfers between devices, fetch(): z = lax.all_to_all(jnp.tile(kept, (1, n_col)), 'col', 1, 1, tiled=True)  28.6 us
  transfers between devices with their start and end apart: 11, of which 11 were waited for; matrix products, arithmetic and copies ran while one was open for 1% of the time, Pallas kernels for 0%

profile of v11, /device:TPU:1, one launch (start us, length us, event | category | flops | bytes accessed | tf_op | source)
XLA Modules:
  0.0 716.5 jit_solution(4923746698168945643)
XLA Ops:
  33.4 12.4 %shard_map.59 = (f32[2,24,2048]{2,1,0:T(8,128)}, f32[24,2048]{1,0:T(8,128)}, f32[24,128]{1,0:T(8,128)}) custom-call(s32[3]{0:T(128)} %add_convert_fusion.flags_ref, f32[24,2048]{1,0:T(8,128)} %d_ref.1, f32[1,2048]{1,0:T(1,128)} %bitcast.421, f32[2,24,2048]{2,1,0:T(8,128)} %reshape.1291.di_ref, bf16[2,1,2048,2048]{3,2,1,0:T(8,128)(2,1)} %bitcast.412), custom_call_target="tpu_custom_call" | custom-call | tf_op jit(solution)/shard_map/pallas_call | solution.py:72
  47.9 11.3 %all_to_all.360 = f32[56,16,128]{2,0,1:T(8,128)S(1)} all-to-all(f32[56,16,128]{2,0,1:T(8,128)S(1)} %pad_maximum_fusion), channel_id=1, replica_groups=mesh['row'=8,'col'=16] {'col'}, dimensions={1} | all-to-all | bytes 917504 | tf_op jit(solution)/shard_map/all_to_all | solution.py:15
  73.3 16.0 %all_to_all.361 = f32[32,8,256]{2,0,1:T(8,128)S(1)} all-to-all(f32[32,8,256]{2,0,1:T(8,128)S(1)} %bitcast.445), channel_id=1, replica_groups=mesh['row'=8,'col'=16] {'row'}, dimensions={1} | all-to-all | bytes 524288 | tf_op jit(solution)/shard_map/all_to_all | solution.py:15
  125.4 12.4 %shard_map.60 = (f32[2,24,2048]{2,1,0:T(8,128)}, f32[24,2048]{1,0:T(8,128)}, f32[24,128]{1,0:T(8,128)}) custom-call(s32[3]{0:T(128)} %add_convert_fusion.flags_ref, f32[24,2048]{1,0:T(8,128)} %multiply_add_fusion.14.d_ref, f32[1,2048]{1,0:T(1,128)} %bitcast.422, f32[2,24,2048]{2,1,0:T(8,128)} %multiply_add_fusion.6.di_ref, bf16[2,1,2048,2048]{3,2,1,0:T(8,128)(2,1)} %bitcast.413), custom_call_target="tpu_custom_call" | custom-call | tf_op jit(solution)/shard_map/pallas_call | solution.py:72
  139.9 11.5 %all_to_all.363 = f32[56,16,128]{2,0,1:T(8,128)S(1)} all-to-all(f32[56,16,128]{2,0,1:T(8,128)S(1)} %pad_maximum_fusion.1), channel_id=1, replica_groups=mesh['row'=8,'col'=16] {'col'}, dimensions={1} | all-to-all | bytes 917504 | tf_op jit(solution)/shard_map/all_to_all | solution.py:15
  151.4 11.2 %all_to_all.364 = f32[56,16,128]{2,0,1:T(8,128)S(1)} all-to-all(f32[56,16,128]{2,0,1:T(8,128)S(1)} %tile.52), channel_id=1, replica_groups=mesh['row'=8,'col'=16] {'col'}, dimensions={1} | all-to-all | bytes 917504 | tf_op jit(solution)/shard_map/all_to_all | solution.py:17
  163.7 15.0 %all_to_all.365 = f32[32,8,256]{2,0,1:T(8,128)S(1)} all-to-all(f32[32,8,256]{2,0,1:T(8,128)S(1)} %bitcast.446), channel_id=1, replica_groups=mesh['row'=8,'col'=16] {'row'}, dimensions={1} | all-to-all | bytes 524288 | tf_op jit(solution)/shard_map/all_to_all | solution.py:15
  213.2 12.4 %shard_map.61 = (f32[2,24,2048]{2,1,0:T(8,128)}, f32[24,2048]{1,0:T(8,128)}, f32[24,128]{1,0:T(8,128)}) custom-call(s32[3]{0:T(128)} %add_convert_fusion.flags_ref, f32[24,2048]{1,0:T(8,128)} %multiply_add_fusion.13.d_ref, f32[1,2048]{1,0:T(1,128)} %bitcast.423, f32[2,24,2048]{2,1,0:T(8,128)} %multiply_add_fusion.5.di_ref, bf16[2,1,2048,2048]{3,2,1,0:T(8,128)(2,1)} %bitcast.414), custom_call_target="tpu_custom_call" | custom-call | tf_op jit(solution)/shard_map/pallas_call | solution.py:72
  227.7 11.5 %all_to_all.368 = f32[56,16,128]{2,0,1:T(8,128)S(1)} all-to-all(f32[56,16,128]{2,0,1:T(8,128)S(1)} %pad_maximum_fusion.2), channel_id=1, replica_groups=mesh['row'=8,'col'=16] {'col'}, dimensions={1} | all-to-all | bytes 917504 | tf_op jit(solution)/shard_map/all_to_all | solution.py:15
  239.2 11.4 %all_to_all.369 = f32[56,16,128]{2,0,1:T(8,128)S(1)} all-to-all(f32[56,16,128]{2,0,1:T(8,128)S(1)} %tile.55), channel_id=1, replica_groups=mesh['row'=8,'col'=16] {'col'}, dimensions={1} | all-to-all | bytes 917504 | tf_op jit(solution)/shard_map/all_to_all | solution.py:17
  251.7 14.8 %all_to_all.370 = f32[32,8,256]{2,0,1:T(8,128)S(1)} all-to-all(f32[32,8,256]{2,0,1:T(8,128)S(1)} %bitcast.447), channel_id=1, replica_groups=mesh['row'=8,'col'=16] {'row'}, dimensions={1} | all-to-all | bytes 524288 | tf_op jit(solution)/shard_map/all_to_all | solution.py:15
  276.9 10.3 %all_to_all.372 = f32[32,16,128]{2,0,1:T(8,128)S(1)} all-to-all(f32[32,16,128]{2,0,1:T(8,128)S(1)} %pad_maximum_fusion.11), channel_id=1, replica_groups=mesh['row'=8,'col'=16] {'col'}, dimensions={1} | all-to-all | bytes 524288 | tf_op jit(solution)/shard_map/all_to_all | solution.py:108
  301.0 12.4 %shard_map.62 = (f32[2,24,2048]{2,1,0:T(8,128)}, f32[24,2048]{1,0:T(8,128)}, f32[24,128]{1,0:T(8,128)}) custom-call(s32[3]{0:T(128)} %add_convert_fusion.flags_ref, f32[24,2048]{1,0:T(8,128)} %multiply_add_fusion.12.d_ref, f32[1,2048]{1,0:T(1,128)} %bitcast.424, f32[2,24,2048]{2,1,0:T(8,128)} %multiply_add_fusion.4.di_ref, bf16[2,1,2048,2048]{3,2,1,0:T(8,128)(2,1)} %bitcast.415), custom_call_target="tpu_custom_call" | custom-call | tf_op jit(solution)/shard_map/pallas_call | solution.py:72
  315.5 11.5 %all_to_all.373 = f32[56,16,128]{2,0,1:T(8,128)S(1)} all-to-all(f32[56,16,128]{2,0,1:T(8,128)S(1)} %pad_maximum_fusion.3), channel_id=1, replica_groups=mesh['row'=8,'col'=16] {'col'}, dimensions={1} | all-to-all | bytes 917504 | tf_op jit(solution)/shard_map/all_to_all | solution.py:15
  327.0 11.2 %all_to_all.374 = f32[56,16,128]{2,0,1:T(8,128)S(1)} all-to-all(f32[56,16,128]{2,0,1:T(8,128)S(1)} %tile.58), channel_id=1, replica_groups=mesh['row'=8,'col'=16] {'col'}, dimensions={1} | all-to-all | bytes 917504 | tf_op jit(solution)/shard_map/all_to_all | solution.py:17
  339.3 15.0 %all_to_all.375 = f32[32,8,256]{2,0,1:T(8,128)S(1)} all-to-all(f32[32,8,256]{2,0,1:T(8,128)S(1)} %bitcast.448), channel_id=1, replica_groups=mesh['row'=8,'col'=16] {'row'}, dimensions={1} | all-to-all | bytes 524288 | tf_op jit(solution)/shard_map/all_to_all | solution.py:15
  388.8 12.4 %shard_map.63 = (f32[2,24,2048]{2,1,0:T(8,128)}, f32[24,2048]{1,0:T(8,128)}, f32[24,128]{1,0:T(8,128)}) custom-call(s32[3]{0:T(128)} %add_convert_fusion.flags_ref, f32[24,2048]{1,0:T(8,128)} %multiply_add_fusion.11.d_ref, f32[1,2048]{1,0:T(1,128)} %bitcast.425, f32[2,24,2048]{2,1,0:T(8,128)} %multiply_add_fusion.3.di_ref, bf16[2,1,2048,2048]{3,2,1,0:T(8,128)(2,1)} %bitcast.416), custom_call_target="tpu_custom_call" | custom-call | tf_op jit(solution)/shard_map/pallas_call | solution.py:72
  403.3 11.5 %all_to_all.378 = f32[56,16,128]{2,0,1:T(8,128)S(1)} all-to-all(f32[56,16,128]{2,0,1:T(8,128)S(1)} %pad_maximum_fusion.4), channel_id=1, replica_groups=mesh['row'=8,'col'=16] {'col'}, dimensions={1} | all-to-all | bytes 917504 | tf_op jit(solution)/shard_map/all_to_all | solution.py:15
  414.8 11.2 %all_to_all.379 = f32[56,16,128]{2,0,1:T(8,128)S(1)} all-to-all(f32[56,16,128]{2,0,1:T(8,128)S(1)} %tile.61), channel_id=1, replica_groups=mesh['row'=8,'col'=16] {'col'}, dimensions={1} | all-to-all | bytes 917504 | tf_op jit(solution)/shard_map/all_to_all | solution.py:17
  427.1 15.0 %all_to_all.380 = f32[32,8,256]{2,0,1:T(8,128)S(1)} all-to-all(f32[32,8,256]{2,0,1:T(8,128)S(1)} %bitcast.449), channel_id=1, replica_groups=mesh['row'=8,'col'=16] {'row'}, dimensions={1} | all-to-all | bytes 524288 | tf_op jit(solution)/shard_map/all_to_all | solution.py:15
  476.6 12.4 %shard_map.64 = (f32[2,24,2048]{2,1,0:T(8,128)}, f32[24,2048]{1,0:T(8,128)}, f32[24,128]{1,0:T(8,128)}) custom-call(s32[3]{0:T(128)} %add_convert_fusion.flags_ref, f32[24,2048]{1,0:T(8,128)} %multiply_add_fusion.10.d_ref, f32[1,2048]{1,0:T(1,128)} %bitcast.426, f32[2,24,2048]{2,1,0:T(8,128)} %multiply_add_fusion.2.di_ref, bf16[2,1,2048,2048]{3,2,1,0:T(8,128)(2,1)} %bitcast.417), custom_call_target="tpu_custom_call" | custom-call | tf_op jit(solution)/shard_map/pallas_call | solution.py:72
  491.1 11.5 %all_to_all.383 = f32[56,16,128]{2,0,1:T(8,128)S(1)} all-to-all(f32[56,16,128]{2,0,1:T(8,128)S(1)} %pad_maximum_fusion.5), channel_id=1, replica_groups=mesh['row'=8,'col'=16] {'col'}, dimensions={1} | all-to-all | bytes 917504 | tf_op jit(solution)/shard_map/all_to_all | solution.py:15
  502.6 11.2 %all_to_all.384 = f32[56,16,128]{2,0,1:T(8,128)S(1)} all-to-all(f32[56,16,128]{2,0,1:T(8,128)S(1)} %tile.64), channel_id=1, replica_groups=mesh['row'=8,'col'=16] {'col'}, dimensions={1} | all-to-all | bytes 917504 | tf_op jit(solution)/shard_map/all_to_all | solution.py:17
  515.0 15.0 %all_to_all.385 = f32[32,8,256]{2,0,1:T(8,128)S(1)} all-to-all(f32[32,8,256]{2,0,1:T(8,128)S(1)} %bitcast.450), channel_id=1, replica_groups=mesh['row'=8,'col'=16] {'row'}, dimensions={1} | all-to-all | bytes 524288 | tf_op jit(solution)/shard_map/all_to_all | solution.py:15
  564.4 12.4 %shard_map.65 = (f32[2,24,2048]{2,1,0:T(8,128)}, f32[24,2048]{1,0:T(8,128)}, f32[24,128]{1,0:T(8,128)}) custom-call(s32[3]{0:T(128)} %add_convert_fusion.flags_ref, f32[24,2048]{1,0:T(8,128)} %multiply_add_fusion.9.d_ref, f32[1,2048]{1,0:T(1,128)} %bitcast.427, f32[2,24,2048]{2,1,0:T(8,128)} %multiply_add_fusion.1.di_ref, bf16[2,1,2048,2048]{3,2,1,0:T(8,128)(2,1)} %bitcast.418), custom_call_target="tpu_custom_call" | custom-call | tf_op jit(solution)/shard_map/pallas_call | solution.py:72
  578.9 11.5 %all_to_all.388 = f32[56,16,128]{2,0,1:T(8,128)S(1)} all-to-all(f32[56,16,128]{2,0,1:T(8,128)S(1)} %pad_maximum_fusion.6), channel_id=1, replica_groups=mesh['row'=8,'col'=16] {'col'}, dimensions={1} | all-to-all | bytes 917504 | tf_op jit(solution)/shard_map/all_to_all | solution.py:15
  590.4 11.2 %all_to_all.389 = f32[56,16,128]{2,0,1:T(8,128)S(1)} all-to-all(f32[56,16,128]{2,0,1:T(8,128)S(1)} %tile.67), channel_id=1, replica_groups=mesh['row'=8,'col'=16] {'col'}, dimensions={1} | all-to-all | bytes 917504 | tf_op jit(solution)/shard_map/all_to_all | solution.py:17
  602.8 15.0 %all_to_all.390 = f32[32,8,256]{2,0,1:T(8,128)S(1)} all-to-all(f32[32,8,256]{2,0,1:T(8,128)S(1)} %bitcast.451), channel_id=1, replica_groups=mesh['row'=8,'col'=16] {'row'}, dimensions={1} | all-to-all | bytes 524288 | tf_op jit(solution)/shard_map/all_to_all | solution.py:15
  652.2 12.2 %shard_map.66 = (f32[2,24,2048]{2,1,0:T(8,128)}, f32[24,2048]{1,0:T(8,128)}, f32[24,128]{1,0:T(8,128)}) custom-call(s32[3]{0:T(128)} %add_convert_fusion.flags_ref, f32[24,2048]{1,0:T(8,128)} %multiply_add_fusion.8.d_ref, f32[1,2048]{1,0:T(1,128)} %bitcast.428, f32[2,24,2048]{2,1,0:T(8,128)} %multiply_add_fusion.di_ref, bf16[2,1,2048,2048]{3,2,1,0:T(8,128)(2,1)} %bitcast.419), custom_call_target="tpu_custom_call" | custom-call | tf_op jit(solution)/shard_map/pallas_call | solution.py:72
  666.6 11.5 %all_to_all.393 = f32[56,16,128]{2,0,1:T(8,128)S(1)} all-to-all(f32[56,16,128]{2,0,1:T(8,128)S(1)} %pad_maximum_fusion.7), channel_id=1, replica_groups=mesh['row'=8,'col'=16] {'col'}, dimensions={1} | all-to-all | bytes 917504 | tf_op jit(solution)/shard_map/all_to_all | solution.py:15
  678.1 11.2 %all_to_all.394 = f32[56,16,128]{2,0,1:T(8,128)S(1)} all-to-all(f32[56,16,128]{2,0,1:T(8,128)S(1)} %tile.70), channel_id=1, replica_groups=mesh['row'=8,'col'=16] {'col'}, dimensions={1} | all-to-all | bytes 917504 | tf_op jit(solution)/shard_map/all_to_all | solution.py:17
  690.4 15.0 %all_to_all.395 = f32[32,8,256]{2,0,1:T(8,128)S(1)} all-to-all(f32[32,8,256]{2,0,1:T(8,128)S(1)} %bitcast.452), channel_id=1, replica_groups=mesh['row'=8,'col'=16] {'row'}, dimensions={1} | all-to-all | bytes 524288 | tf_op jit(solution)/shard_map/all_to_all | solution.py:15
  (387 shorter events, 311.4 us)
Async XLA Ops:
  3.5 16.1 %all-to-all-start = ((f32[32,16,128]{2,0,1:T(8,128)}), f32[32,16,128]{2,0,1:T(8,128)S(1)}, u32[]{:S(2)}, u32[]{:S(2)}) async-start(f32[32,16,128]{2,0,1:T(8,128)} %copy.85), calls=%async_computation | async-start | bytes 524288 | tf_op jit(solution)/shard_map/all_to_all | solution.py:108
  12.1 88.9 %copy-start = (f32[24,2048]{1,0:T(8,128)S(1)}, f32[24,2048]{1,0:T(8,128)}, u32[]{:S(2)}) copy-start(f32[24,2048]{1,0:T(8,128)} %d_ref.1) | copy-start | bytes 589828
  12.1 88.9 %copy-start.14 = (f32[2048]{0:T(1024)S(1)}, f32[2048]{0:T(1024)}, u32[]{:S(2)}) copy-start(f32[2048]{0:T(1024)} %param.53) | copy-start | bytes 24580
  20.4 12.0 %all-to-all-start.1 = ((f32[48,16,128]{2,0,1:T(8,128)}), f32[48,16,128]{2,0,1:T(8,128)S(1)}, u32[]{:S(2)}, u32[]{:S(2)}) async-start(f32[48,16,128]{2,0,1:T(8,128)} %tile.48), calls=%async_computation.1 | async-start | bytes 786432 | tf_op jit(solution)/shard_map/all_to_all | solution.py:113
  33.4 91.1 %copy-start.7 = (f32[2,24,2048]{2,1,0:T(8,128)S(1)}, f32[2,24,2048]{2,1,0:T(8,128)}, u32[]{:S(2)}) copy-start(f32[2,24,2048]{2,1,0:T(8,128)} %reshape.1291.di_ref) | copy-start | bytes 1179652
  60.1 12.1 %all-to-all-start.3 = ((f32[56,16,128]{2,0,1:T(8,128)}), f32[56,16,128]{2,0,1:T(8,128)S(1)}, u32[]{:S(2)}, u32[]{:S(2)}) async-start(f32[56,16,128]{2,0,1:T(8,128)} %tile.49), calls=%async_computation.3 | async-start | bytes 917504 | tf_op jit(solution)/shard_map/all_to_all | solution.py:17
  90.1 10.8 %all-to-all-start.5 = ((f32[32,8,256]{2,0,1:T(8,128)}), f32[32,8,256]{2,0,1:T(8,128)S(1)}, u32[]{:S(2)}, u32[]{:S(2)}) async-start(f32[32,8,256]{2,0,1:T(8,128)} %tile.50), calls=%async_computation.5 | async-start | bytes 524288 | tf_op jit(solution)/shard_map/all_to_all | solution.py:17
  112.5 11.8 %all-to-all-start.7 = ((f32[48,16,128]{2,0,1:T(8,128)}), f32[48,16,128]{2,0,1:T(8,128)S(1)}, u32[]{:S(2)}, u32[]{:S(2)}) async-start(f32[48,16,128]{2,0,1:T(8,128)} %tile.51), calls=%async_computation.7 | async-start | bytes 786432 | tf_op jit(solution)/shard_map/all_to_all | solution.py:113
  116.1 72.7 %copy-start.15 = (f32[2048]{0:T(1024)S(1)}, f32[2048]{0:T(1024)}, u32[]{:S(2)}) copy-start(f32[2048]{0:T(1024)} %param.53) | copy-start | bytes 24580
  116.8 72.0 %copy-start.1 = (f32[24,2048]{1,0:T(8,128)S(1)}, f32[24,2048]{1,0:T(8,128)}, u32[]{:S(2)}) copy-start(f32[24,2048]{1,0:T(8,128)} %multiply_add_fusion.14.d_ref) | copy-start | bytes 589828
  125.4 86.9 %copy-start.9 = (f32[2,24,2048]{2,1,0:T(8,128)S(1)}, f32[2,24,2048]{2,1,0:T(8,128)}, u32[]{:S(2)}) copy-start(f32[2,24,2048]{2,1,0:T(8,128)} %multiply_add_fusion.6.di_ref) | copy-start | bytes 1179652
  200.3 11.8 %all-to-all-start.13 = ((f32[48,16,128]{2,0,1:T(8,128)}), f32[48,16,128]{2,0,1:T(8,128)S(1)}, u32[]{:S(2)}, u32[]{:S(2)}) async-start(f32[48,16,128]{2,0,1:T(8,128)} %tile.54), calls=%async_computation.13 | async-start | bytes 786432 | tf_op jit(solution)/shard_map/all_to_all | solution.py:113
  203.9 72.7 %copy-start.16 = (f32[2048]{0:T(1024)S(1)}, f32[2048]{0:T(1024)}, u32[]{:S(2)}) copy-start(f32[2048]{0:T(1024)} %param.53) | copy-start | bytes 24580
  204.6 72.0 %copy-start.2 = (f32[24,2048]{1,0:T(8,128)S(1)}, f32[24,2048]{1,0:T(8,128)}, u32[]{:S(2)}) copy-start(f32[24,2048]{1,0:T(8,128)} %multiply_add_fusion.13.d_ref) | copy-start | bytes 589828
  213.2 86.9 %copy-start.10 = (f32[2,24,2048]{2,1,0:T(8,128)S(1)}, f32[2,24,2048]{2,1,0:T(8,128)}, u32[]{:S(2)}) copy-start(f32[2,24,2048]{2,1,0:T(8,128)} %multiply_add_fusion.5.di_ref) | copy-start | bytes 1179652
  288.1 11.8 %all-to-all-start.19 = ((f32[48,16,128]{2,0,1:T(8,128)}), f32[48,16,128]{2,0,1:T(8,128)S(1)}, u32[]{:S(2)}, u32[]{:S(2)}) async-start(f32[48,16,128]{2,0,1:T(8,128)} %tile.57), calls=%async_computation.19 | async-start | bytes 786432 | tf_op jit(solution)/shard_map/all_to_all | solution.py:113
  291.7 72.7 %copy-start.17 = (f32[2048]{0:T(1024)S(1)}, f32[2048]{0:T(1024)}, u32[]{:S(2)}) copy-start(f32[2048]{0:T(1024)} %param.53) | copy-start | bytes 24580
  292.4 72.0 %copy-start.3 = (f32[24,2048]{1,0:T(8,128)S(1)}, f32[24,2048]{1,0:T(8,128)}, u32[]{:S(2)}) copy-start(f32[24,2048]{1,0:T(8,128)} %multiply_add_fusion.12.d_ref) | copy-start | bytes 589828
  301.0 86.9 %copy-start.11 = (f32[2,24,2048]{2,1,0:T(8,128)S(1)}, f32[2,24,2048]{2,1,0:T(8,128)}, u32[]{:S(2)}) copy-start(f32[2,24,2048]{2,1,0:T(8,128)} %multiply_add_fusion.4.di_ref) | copy-start | bytes 1179652
  375.9 11.8 %all-to-all-start.25 = ((f32[48,16,128]{2,0,1:T(8,128)}), f32[48,16,128]{2,0,1:T(8,128)S(1)}, u32[]{:S(2)}, u32[]{:S(2)}) async-start(f32[48,16,128]{2,0,1:T(8,128)} %tile.60), calls=%async_computation.25 | async-start | bytes 786432 | tf_op jit(solution)/shard_map/all_to_all | solution.py:113
  379.5 72.7 %copy-start.18 = (f32[2048]{0:T(1024)S(1)}, f32[2048]{0:T(1024)}, u32[]{:S(2)}) copy-start(f32[2048]{0:T(1024)} %param.53) | copy-start | bytes 24580
  380.2 72.0 %copy-start.4 = (f32[24,2048]{1,0:T(8,128)S(1)}, f32[24,2048]{1,0:T(8,128)}, u32[]{:S(2)}) copy-start(f32[24,2048]{1,0:T(8,128)} %multiply_add_fusion.11.d_ref) | copy-start | bytes 589828
  388.8 86.9 %copy-start.12 = (f32[2,24,2048]{2,1,0:T(8,128)S(1)}, f32[2,24,2048]{2,1,0:T(8,128)}, u32[]{:S(2)}) copy-start(f32[2,24,2048]{2,1,0:T(8,128)} %multiply_add_fusion.3.di_ref) | copy-start | bytes 1179652
  463.7 11.8 %all-to-all-start.31 = ((f32[48,16,128]{2,0,1:T(8,128)}), f32[48,16,128]{2,0,1:T(8,128)S(1)}, u32[]{:S(2)}, u32[]{:S(2)}) async-start(f32[48,16,128]{2,0,1:T(8,128)} %tile.63), calls=%async_computation.31 | async-start | bytes 786432 | tf_op jit(solution)/shard_map/all_to_all | solution.py:113
  467.5 72.5 %copy-start.19 = (f32[2048]{0:T(1024)S(1)}, f32[2048]{0:T(1024)}, u32[]{:S(2)}) copy-start(f32[2048]{0:T(1024)} %param.53) | copy-start | bytes 24580
  476.6 87.0 %copy-start.13 = (f32[2,24,2048]{2,1,0:T(8,128)S(1)}, f32[2,24,2048]{2,1,0:T(8,128)}, u32[]{:S(2)}) copy-start(f32[2,24,2048]{2,1,0:T(8,128)} %multiply_add_fusion.2.di_ref) | copy-start | bytes 1179652
  551.5 11.8 %all-to-all-start.37 = ((f32[48,16,128]{2,0,1:T(8,128)}), f32[48,16,128]{2,0,1:T(8,128)S(1)}, u32[]{:S(2)}, u32[]{:S(2)}) async-start(f32[48,16,128]{2,0,1:T(8,128)} %tile.66), calls=%async_computation.37 | async-start | bytes 786432 | tf_op jit(solution)/shard_map/all_to_all | solution.py:113
  555.1 72.7 %copy-start.20 = (f32[2048]{0:T(1024)S(1)}, f32[2048]{0:T(1024)}, u32[]{:S(2)}) copy-start(f32[2048]{0:T(1024)} %param.53) | copy-start | bytes 24580
  555.8 72.0 %copy-start.6 = (f32[24,2048]{1,0:T(8,128)S(1)}, f32[24,2048]{1,0:T(8,128)}, u32[]{:S(2)}) copy-start(f32[24,2048]{1,0:T(8,128)} %multiply_add_fusion.9.d_ref) | copy-start | bytes 589828
  564.4 87.0 %copy-start.8 = (f32[2,24,2048]{2,1,0:T(8,128)S(1)}, f32[2,24,2048]{2,1,0:T(8,128)}, u32[]{:S(2)}) copy-start(f32[2,24,2048]{2,1,0:T(8,128)} %multiply_add_fusion.1.di_ref) | copy-start | bytes 1179652
  639.3 11.8 %all-to-all-start.43 = ((f32[48,16,128]{2,0,1:T(8,128)}), f32[48,16,128]{2,0,1:T(8,128)S(1)}, u32[]{:S(2)}, u32[]{:S(2)}) async-start(f32[48,16,128]{2,0,1:T(8,128)} %tile.69), calls=%async_computation.43 | async-start | bytes 786432 | tf_op jit(solution)/shard_map/all_to_all | solution.py:113
  642.9 72.6 %copy-start.21 = (f32[2048]{0:T(1024)S(1)}, f32[2048]{0:T(1024)}, u32[]{:S(2)}) copy-start(f32[2048]{0:T(1024)} %param.53) | copy-start | bytes 24580
  (2 other events, 143.6 us)

commit v12 on v9

--- a/solution.py
+++ b/solution.py
@@ -49,7 +49,7 @@
         p_ref[...] = acc
 
 
-def block_products(flags, d, di, blocks, tile=1024):
+def block_products(flags, d, di, blocks, tile=2048):
     nb, _, order, _ = blocks.shape
     vecs = d.shape[0]
     grid_spec = pltpu.PrefetchScalarGridSpec(

time: 720 us -> 735 us (1.021); the launches traced: 716 us -> 723 us
  no operation moved by 1% of the time
where the time goes in v12:
time: 735 us; the launch traced here: 723 us
  blocking collectives  433 us (59%)
  Pallas kernels  105 us (14%)
  waiting for transfers between devices  77.1 us (10%)
  starting transfers between devices  45.5 us (6%)
  other arithmetic  32.7 us (4%)
  local copies, waits for them, and re-layouts  24.9 us (3%)
    all_to_all x16, blocking collectives, all_reduce(): y = lax.all_to_all(x, axis, 1, 1, tiled=True)  213 us
    all_to_all x14, blocking collectives, all_reduce(): return lax.all_to_all(jnp.tile(part, (1, n)), axis, 1, 1, tiled=True)  148 us
    pallas_call x8, Pallas kernels, block_products(): pl.pallas_call(products_kernel, grid_spec=grid_spec, out_shape=[jax.Shape...  105 us
    all_to_all x7, blocking collectives, fetch(): y = lax.all_to_all(x, 'col', 1, 1, tiled=True)  72.4 us
    all_to_all x8, waiting for transfers between devices, fetch(): z = lax.all_to_all(jnp.tile(kept, (1, n_col)), 'col', 1, 1, tiled=True)  58.3 us
    all_to_all x8, starting transfers between devices, fetch(): z = lax.all_to_all(jnp.tile(kept, (1, n_col)), 'col', 1, 1, tiled=True)  29 us
  transfers between devices with their start and end apart: 11, of which 11 were waited for; matrix products, arithmetic and copies ran while one was open for 1% of the time, Pallas kernels for 0%

profile of v12, /device:TPU:1, one launch (start us, length us, event | category | flops | bytes accessed | tf_op | source)
XLA Modules:
  0.0 723.1 jit_solution(2892528582776576336)
XLA Ops:
  33.4 13.1 %shard_map.59 = (f32[2,24,2048]{2,1,0:T(8,128)}, f32[24,2048]{1,0:T(8,128)}, f32[24,128]{1,0:T(8,128)}) custom-call(s32[2]{0:T(128)} %fusion.56.flags_ref, f32[24,2048]{1,0:T(8,128)} %d_ref.1, f32[2,24,2048]{2,1,0:T(8,128)} %reshape.1387.di_ref, bf16[2,1,2048,2048]{3,2,1,0:T(8,128)(2,1)} %bitcast.418), custom_call_target="tpu_custom_call" | custom-call | tf_op jit(solution)/shard_map/pallas_call | solution.py:69
  48.7 11.3 %all_to_all.360 = f32[56,16,128]{2,0,1:T(8,128)S(1)} all-to-all(f32[56,16,128]{2,0,1:T(8,128)S(1)} %pad_maximum_fusion), channel_id=1, replica_groups=mesh['row'=8,'col'=16] {'col'}, dimensions={1} | all-to-all | bytes 917504 | tf_op jit(solution)/shard_map/all_to_all | solution.py:15
  74.1 16.0 %all_to_all.361 = f32[32,8,256]{2,0,1:T(8,128)S(1)} all-to-all(f32[32,8,256]{2,0,1:T(8,128)S(1)} %bitcast.443), channel_id=1, replica_groups=mesh['row'=8,'col'=16] {'row'}, dimensions={1} | all-to-all | bytes 524288 | tf_op jit(solution)/shard_map/all_to_all | solution.py:15
  126.1 13.1 %shard_map.60 = (f32[2,24,2048]{2,1,0:T(8,128)}, f32[24,2048]{1,0:T(8,128)}, f32[24,128]{1,0:T(8,128)}) custom-call(s32[2]{0:T(128)} %fusion.56.flags_ref, f32[24,2048]{1,0:T(8,128)} %get-tuple-element.365.d_ref, f32[2,24,2048]{2,1,0:T(8,128)} %multiply_add_fusion.6.di_ref, bf16[2,1,2048,2048]{3,2,1,0:T(8,128)(2,1)} %bitcast.419), custom_call_target="tpu_custom_call" | custom-call | tf_op jit(solution)/shard_map/pallas_call | solution.py:69
  141.4 11.5 %all_to_all.363 = f32[56,16,128]{2,0,1:T(8,128)S(1)} all-to-all(f32[56,16,128]{2,0,1:T(8,128)S(1)} %pad_maximum_fusion.1), channel_id=1, replica_groups=mesh['row'=8,'col'=16] {'col'}, dimensions={1} | all-to-all | bytes 917504 | tf_op jit(solution)/shard_map/all_to_all | solution.py:15
  152.9 11.2 %all_to_all.364 = f32[56,16,128]{2,0,1:T(8,128)S(1)} all-to-all(f32[56,16,128]{2,0,1:T(8,128)S(1)} %tile.52), channel_id=1, replica_groups=mesh['row'=8,'col'=16] {'col'}, dimensions={1} | all-to-all | bytes 917504 | tf_op jit(solution)/shard_map/all_to_all | solution.py:17
  165.2 15.0 %all_to_all.365 = f32[32,8,256]{2,0,1:T(8,128)S(1)} all-to-all(f32[32,8,256]{2,0,1:T(8,128)S(1)} %bitcast.444), channel_id=1, replica_groups=mesh['row'=8,'col'=16] {'row'}, dimensions={1} | all-to-all | bytes 524288 | tf_op jit(solution)/shard_map/all_to_all | solution.py:15
  214.7 13.1 %shard_map.61 = (f32[2,24,2048]{2,1,0:T(8,128)}, f32[24,2048]{1,0:T(8,128)}, f32[24,128]{1,0:T(8,128)}) custom-call(s32[2]{0:T(128)} %fusion.56.flags_ref, f32[24,2048]{1,0:T(8,128)} %get-tuple-element.361.d_ref, f32[2,24,2048]{2,1,0:T(8,128)} %multiply_add_fusion.5.di_ref, bf16[2,1,2048,2048]{3,2,1,0:T(8,128)(2,1)} %bitcast.420), custom_call_target="tpu_custom_call" | custom-call | tf_op jit(solution)/shard_map/pallas_call | solution.py:69
  230.0 11.5 %all_to_all.368 = f32[56,16,128]{2,0,1:T(8,128)S(1)} all-to-all(f32[56,16,128]{2,0,1:T(8,128)S(1)} %pad_maximum_fusion.2), channel_id=1, replica_groups=mesh['row'=8,'col'=16] {'col'}, dimensions={1} | all-to-all | bytes 917504 | tf_op jit(solution)/shard_map/all_to_all | solution.py:15
  241.5 11.2 %all_to_all.369 = f32[56,16,128]{2,0,1:T(8,128)S(1)} all-to-all(f32[56,16,128]{2,0,1:T(8,128)S(1)} %tile.55), channel_id=1, replica_groups=mesh['row'=8,'col'=16] {'col'}, dimensions={1} | all-to-all | bytes 917504 | tf_op jit(solution)/shard_map/all_to_all | solution.py:17
  253.9 15.0 %all_to_all.370 = f32[32,8,256]{2,0,1:T(8,128)S(1)} all-to-all(f32[32,8,256]{2,0,1:T(8,128)S(1)} %bitcast.445), channel_id=1, replica_groups=mesh['row'=8,'col'=16] {'row'}, dimensions={1} | all-to-all | bytes 524288 | tf_op jit(solution)/shard_map/all_to_all | solution.py:15
  279.2 10.3 %all_to_all.372 = f32[32,16,128]{2,0,1:T(8,128)S(1)} all-to-all(f32[32,16,128]{2,0,1:T(8,128)S(1)} %pad_maximum_fusion.11), channel_id=1, replica_groups=mesh['row'=8,'col'=16] {'col'}, dimensions={1} | all-to-all | bytes 524288 | tf_op jit(solution)/shard_map/all_to_all | solution.py:105
  303.2 13.1 %shard_map.62 = (f32[2,24,2048]{2,1,0:T(8,128)}, f32[24,2048]{1,0:T(8,128)}, f32[24,128]{1,0:T(8,128)}) custom-call(s32[2]{0:T(128)} %fusion.56.flags_ref, f32[24,2048]{1,0:T(8,128)} %get-tuple-element.357.d_ref, f32[2,24,2048]{2,1,0:T(8,128)} %multiply_add_fusion.4.di_ref, bf16[2,1,2048,2048]{3,2,1,0:T(8,128)(2,1)} %bitcast.421), custom_call_target="tpu_custom_call" | custom-call | tf_op jit(solution)/shard_map/pallas_call | solution.py:69
  318.5 11.5 %all_to_all.373 = f32[56,16,128]{2,0,1:T(8,128)S(1)} all-to-all(f32[56,16,128]{2,0,1:T(8,128)S(1)} %pad_maximum_fusion.3), channel_id=1, replica_groups=mesh['row'=8,'col'=16] {'col'}, dimensions={1} | all-to-all | bytes 917504 | tf_op jit(solution)/shard_map/all_to_all | solution.py:15
  330.0 11.2 %all_to_all.374 = f32[56,16,128]{2,0,1:T(8,128)S(1)} all-to-all(f32[56,16,128]{2,0,1:T(8,128)S(1)} %tile.58), channel_id=1, replica_groups=mesh['row'=8,'col'=16] {'col'}, dimensions={1} | all-to-all | bytes 917504 | tf_op jit(solution)/shard_map/all_to_all | solution.py:17
  342.3 15.0 %all_to_all.375 = f32[32,8,256]{2,0,1:T(8,128)S(1)} all-to-all(f32[32,8,256]{2,0,1:T(8,128)S(1)} %bitcast.446), channel_id=1, replica_groups=mesh['row'=8,'col'=16] {'row'}, dimensions={1} | all-to-all | bytes 524288 | tf_op jit(solution)/shard_map/all_to_all | solution.py:15
  391.9 13.1 %shard_map.63 = (f32[2,24,2048]{2,1,0:T(8,128)}, f32[24,2048]{1,0:T(8,128)}, f32[24,128]{1,0:T(8,128)}) custom-call(s32[2]{0:T(128)} %fusion.56.flags_ref, f32[24,2048]{1,0:T(8,128)} %get-tuple-element.353.d_ref, f32[2,24,2048]{2,1,0:T(8,128)} %multiply_add_fusion.3.di_ref, bf16[2,1,2048,2048]{3,2,1,0:T(8,128)(2,1)} %bitcast.422), custom_call_target="tpu_custom_call" | custom-call | tf_op jit(solution)/shard_map/pallas_call | solution.py:69
  407.2 11.5 %all_to_all.378 = f32[56,16,128]{2,0,1:T(8,128)S(1)} all-to-all(f32[56,16,128]{2,0,1:T(8,128)S(1)} %pad_maximum_fusion.4), channel_id=1, replica_groups=mesh['row'=8,'col'=16] {'col'}, dimensions={1} | all-to-all | bytes 917504 | tf_op jit(solution)/shard_map/all_to_all | solution.py:15
  418.7 11.2 %all_to_all.379 = f32[56,16,128]{2,0,1:T(8,128)S(1)} all-to-all(f32[56,16,128]{2,0,1:T(8,128)S(1)} %tile.61), channel_id=1, replica_groups=mesh['row'=8,'col'=16] {'col'}, dimensions={1} | all-to-all | bytes 917504 | tf_op jit(solution)/shard_map/all_to_all | solution.py:17
  431.0 15.0 %all_to_all.380 = f32[32,8,256]{2,0,1:T(8,128)S(1)} all-to-all(f32[32,8,256]{2,0,1:T(8,128)S(1)} %bitcast.447), channel_id=1, replica_groups=mesh['row'=8,'col'=16] {'row'}, dimensions={1} | all-to-all | bytes 524288 | tf_op jit(solution)/shard_map/all_to_all | solution.py:15
  480.4 13.1 %shard_map.64 = (f32[2,24,2048]{2,1,0:T(8,128)}, f32[24,2048]{1,0:T(8,128)}, f32[24,128]{1,0:T(8,128)}) custom-call(s32[2]{0:T(128)} %fusion.56.flags_ref, f32[24,2048]{1,0:T(8,128)} %get-tuple-element.349.d_ref, f32[2,24,2048]{2,1,0:T(8,128)} %multiply_add_fusion.2.di_ref, bf16[2,1,2048,2048]{3,2,1,0:T(8,128)(2,1)} %bitcast.423), custom_call_target="tpu_custom_call" | custom-call | tf_op jit(solution)/shard_map/pallas_call | solution.py:69
  495.7 11.5 %all_to_all.383 = f32[56,16,128]{2,0,1:T(8,128)S(1)} all-to-all(f32[56,16,128]{2,0,1:T(8,128)S(1)} %pad_maximum_fusion.5), channel_id=1, replica_groups=mesh['row'=8,'col'=16] {'col'}, dimensions={1} | all-to-all | bytes 917504 | tf_op jit(solution)/shard_map/all_to_all | solution.py:15
  507.2 11.2 %all_to_all.384 = f32[56,16,128]{2,0,1:T(8,128)S(1)} all-to-all(f32[56,16,128]{2,0,1:T(8,128)S(1)} %tile.64), channel_id=1, replica_groups=mesh['row'=8,'col'=16] {'col'}, dimensions={1} | all-to-all | bytes 917504 | tf_op jit(solution)/shard_map/all_to_all | solution.py:17
  519.5 15.0 %all_to_all.385 = f32[32,8,256]{2,0,1:T(8,128)S(1)} all-to-all(f32[32,8,256]{2,0,1:T(8,128)S(1)} %bitcast.448), channel_id=1, replica_groups=mesh['row'=8,'col'=16] {'row'}, dimensions={1} | all-to-all | bytes 524288 | tf_op jit(solution)/shard_map/all_to_all | solution.py:15
  569.1 13.1 %shard_map.65 = (f32[2,24,2048]{2,1,0:T(8,128)}, f32[24,2048]{1,0:T(8,128)}, f32[24,128]{1,0:T(8,128)}) custom-call(s32[2]{0:T(128)} %fusion.56.flags_ref, f32[24,2048]{1,0:T(8,128)} %get-tuple-element.345.d_ref, f32[2,24,2048]{2,1,0:T(8,128)} %multiply_add_fusion.1.di_ref, bf16[2,1,2048,2048]{3,2,1,0:T(8,128)(2,1)} %bitcast.424), custom_call_target="tpu_custom_call" | custom-call | tf_op jit(solution)/shard_map/pallas_call | solution.py:69
  584.4 11.5 %all_to_all.388 = f32[56,16,128]{2,0,1:T(8,128)S(1)} all-to-all(f32[56,16,128]{2,0,1:T(8,128)S(1)} %pad_maximum_fusion.6), channel_id=1, replica_groups=mesh['row'=8,'col'=16] {'col'}, dimensions={1} | all-to-all | bytes 917504 | tf_op jit(solution)/shard_map/all_to_all | solution.py:15
  595.9 11.2 %all_to_all.389 = f32[56,16,128]{2,0,1:T(8,128)S(1)} all-to-all(f32[56,16,128]{2,0,1:T(8,128)S(1)} %tile.67), channel_id=1, replica_groups=mesh['row'=8,'col'=16] {'col'}, dimensions={1} | all-to-all | bytes 917504 | tf_op jit(solution)/shard_map/all_to_all | solution.py:17
  608.3 15.0 %all_to_all.390 = f32[32,8,256]{2,0,1:T(8,128)S(1)} all-to-all(f32[32,8,256]{2,0,1:T(8,128)S(1)} %bitcast.449), channel_id=1, replica_groups=mesh['row'=8,'col'=16] {'row'}, dimensions={1} | all-to-all | bytes 524288 | tf_op jit(solution)/shard_map/all_to_all | solution.py:15
  657.6 13.0 %shard_map.66 = (f32[2,24,2048]{2,1,0:T(8,128)}, f32[24,2048]{1,0:T(8,128)}, f32[24,128]{1,0:T(8,128)}) custom-call(s32[2]{0:T(128)} %fusion.56.flags_ref, f32[24,2048]{1,0:T(8,128)} %get-tuple-element.341.d_ref, f32[2,24,2048]{2,1,0:T(8,128)} %multiply_add_fusion.di_ref, bf16[2,1,2048,2048]{3,2,1,0:T(8,128)(2,1)} %bitcast.425), custom_call_target="tpu_custom_call" | custom-call | tf_op jit(solution)/shard_map/pallas_call | solution.py:69
  672.8 11.5 %all_to_all.393 = f32[56,16,128]{2,0,1:T(8,128)S(1)} all-to-all(f32[56,16,128]{2,0,1:T(8,128)S(1)} %pad_maximum_fusion.7), channel_id=1, replica_groups=mesh['row'=8,'col'=16] {'col'}, dimensions={1} | all-to-all | bytes 917504 | tf_op jit(solution)/shard_map/all_to_all | solution.py:15
  684.3 11.2 %all_to_all.394 = f32[56,16,128]{2,0,1:T(8,128)S(1)} all-to-all(f32[56,16,128]{2,0,1:T(8,128)S(1)} %tile.70), channel_id=1, replica_groups=mesh['row'=8,'col'=16] {'col'}, dimensions={1} | all-to-all | bytes 917504 | tf_op jit(solution)/shard_map/all_to_all | solution.py:17
  696.6 15.0 %all_to_all.395 = f32[32,8,256]{2,0,1:T(8,128)S(1)} all-to-all(f32[32,8,256]{2,0,1:T(8,128)S(1)} %bitcast.450), channel_id=1, replica_groups=mesh['row'=8,'col'=16] {'row'}, dimensions={1} | all-to-all | bytes 524288 | tf_op jit(solution)/shard_map/all_to_all | solution.py:15
  (380 shorter events, 311.7 us)
Async XLA Ops:
  3.5 16.1 %all-to-all-start = ((f32[32,16,128]{2,0,1:T(8,128)}), f32[32,16,128]{2,0,1:T(8,128)S(1)}, u32[]{:S(2)}, u32[]{:S(2)}) async-start(f32[32,16,128]{2,0,1:T(8,128)} %copy.85), calls=%async_computation | async-start | bytes 524288 | tf_op jit(solution)/shard_map/all_to_all | solution.py:105
  12.1 89.7 %copy-start = (f32[24,2048]{1,0:T(8,128)S(1)}, f32[24,2048]{1,0:T(8,128)}, u32[]{:S(2)}) copy-start(f32[24,2048]{1,0:T(8,128)} %d_ref.1) | copy-start | bytes 589828
  12.1 89.7 %copy-start.14 = (f32[2048]{0:T(1024)S(1)}, f32[2048]{0:T(1024)}, u32[]{:S(2)}) copy-start(f32[2048]{0:T(1024)} %param.53) | copy-start | bytes 24580
  20.5 12.0 %all-to-all-start.1 = ((f32[48,16,128]{2,0,1:T(8,128)}), f32[48,16,128]{2,0,1:T(8,128)S(1)}, u32[]{:S(2)}, u32[]{:S(2)}) async-start(f32[48,16,128]{2,0,1:T(8,128)} %tile.48), calls=%async_computation.1 | async-start | bytes 786432 | tf_op jit(solution)/shard_map/all_to_all | solution.py:110
  33.4 91.8 %copy-start.7 = (f32[2,24,2048]{2,1,0:T(8,128)S(1)}, f32[2,24,2048]{2,1,0:T(8,128)}, u32[]{:S(2)}) copy-start(f32[2,24,2048]{2,1,0:T(8,128)} %reshape.1387.di_ref) | copy-start | bytes 1179652
  60.8 12.1 %all-to-all-start.3 = ((f32[56,16,128]{2,0,1:T(8,128)}), f32[56,16,128]{2,0,1:T(8,128)S(1)}, u32[]{:S(2)}, u32[]{:S(2)}) async-start(f32[56,16,128]{2,0,1:T(8,128)} %tile.49), calls=%async_computation.3 | async-start | bytes 917504 | tf_op jit(solution)/shard_map/all_to_all | solution.py:17
  90.8 10.8 %all-to-all-start.5 = ((f32[32,8,256]{2,0,1:T(8,128)}), f32[32,8,256]{2,0,1:T(8,128)S(1)}, u32[]{:S(2)}, u32[]{:S(2)}) async-start(f32[32,8,256]{2,0,1:T(8,128)} %tile.50), calls=%async_computation.5 | async-start | bytes 524288 | tf_op jit(solution)/shard_map/all_to_all | solution.py:17
  113.2 11.8 %all-to-all-start.7 = ((f32[48,16,128]{2,0,1:T(8,128)}), f32[48,16,128]{2,0,1:T(8,128)S(1)}, u32[]{:S(2)}, u32[]{:S(2)}) async-start(f32[48,16,128]{2,0,1:T(8,128)} %tile.51), calls=%async_computation.7 | async-start | bytes 786432 | tf_op jit(solution)/shard_map/all_to_all | solution.py:110
  117.7 72.5 %copy-start.1 = (f32[24,2048]{1,0:T(8,128)S(1)}, f32[24,2048]{1,0:T(8,128)}, u32[]{:S(2)}) copy-start(f32[24,2048]{1,0:T(8,128)} %get-tuple-element.365.d_ref) | copy-start | bytes 589828
  126.1 87.8 %copy-start.9 = (f32[2,24,2048]{2,1,0:T(8,128)S(1)}, f32[2,24,2048]{2,1,0:T(8,128)}, u32[]{:S(2)}) copy-start(f32[2,24,2048]{2,1,0:T(8,128)} %multiply_add_fusion.6.di_ref) | copy-start | bytes 1179652
  201.7 12.0 %all-to-all-start.13 = ((f32[48,16,128]{2,0,1:T(8,128)}), f32[48,16,128]{2,0,1:T(8,128)S(1)}, u32[]{:S(2)}, u32[]{:S(2)}) async-start(f32[48,16,128]{2,0,1:T(8,128)} %tile.54), calls=%async_computation.13 | async-start | bytes 786432 | tf_op jit(solution)/shard_map/all_to_all | solution.py:110
  206.4 72.5 %copy-start.2 = (f32[24,2048]{1,0:T(8,128)S(1)}, f32[24,2048]{1,0:T(8,128)}, u32[]{:S(2)}) copy-start(f32[24,2048]{1,0:T(8,128)} %get-tuple-element.361.d_ref) | copy-start | bytes 589828
  214.7 87.6 %copy-start.10 = (f32[2,24,2048]{2,1,0:T(8,128)S(1)}, f32[2,24,2048]{2,1,0:T(8,128)}, u32[]{:S(2)}) copy-start(f32[2,24,2048]{2,1,0:T(8,128)} %multiply_add_fusion.5.di_ref) | copy-start | bytes 1179652
  290.4 11.8 %all-to-all-start.19 = ((f32[48,16,128]{2,0,1:T(8,128)}), f32[48,16,128]{2,0,1:T(8,128)S(1)}, u32[]{:S(2)}, u32[]{:S(2)}) async-start(f32[48,16,128]{2,0,1:T(8,128)} %tile.57), calls=%async_computation.19 | async-start | bytes 786432 | tf_op jit(solution)/shard_map/all_to_all | solution.py:110
  294.9 72.5 %copy-start.3 = (f32[24,2048]{1,0:T(8,128)S(1)}, f32[24,2048]{1,0:T(8,128)}, u32[]{:S(2)}) copy-start(f32[24,2048]{1,0:T(8,128)} %get-tuple-element.357.d_ref) | copy-start | bytes 589828
  303.2 87.8 %copy-start.11 = (f32[2,24,2048]{2,1,0:T(8,128)S(1)}, f32[2,24,2048]{2,1,0:T(8,128)}, u32[]{:S(2)}) copy-start(f32[2,24,2048]{2,1,0:T(8,128)} %multiply_add_fusion.4.di_ref) | copy-start | bytes 1179652
  378.8 12.0 %all-to-all-start.25 = ((f32[48,16,128]{2,0,1:T(8,128)}), f32[48,16,128]{2,0,1:T(8,128)S(1)}, u32[]{:S(2)}, u32[]{:S(2)}) async-start(f32[48,16,128]{2,0,1:T(8,128)} %tile.60), calls=%async_computation.25 | async-start | bytes 786432 | tf_op jit(solution)/shard_map/all_to_all | solution.py:110
  383.5 72.5 %copy-start.4 = (f32[24,2048]{1,0:T(8,128)S(1)}, f32[24,2048]{1,0:T(8,128)}, u32[]{:S(2)}) copy-start(f32[24,2048]{1,0:T(8,128)} %get-tuple-element.353.d_ref) | copy-start | bytes 589828
  391.9 87.6 %copy-start.12 = (f32[2,24,2048]{2,1,0:T(8,128)S(1)}, f32[2,24,2048]{2,1,0:T(8,128)}, u32[]{:S(2)}) copy-start(f32[2,24,2048]{2,1,0:T(8,128)} %multiply_add_fusion.3.di_ref) | copy-start | bytes 1179652
  467.5 11.8 %all-to-all-start.31 = ((f32[48,16,128]{2,0,1:T(8,128)}), f32[48,16,128]{2,0,1:T(8,128)S(1)}, u32[]{:S(2)}, u32[]{:S(2)}) async-start(f32[48,16,128]{2,0,1:T(8,128)} %tile.63), calls=%async_computation.31 | async-start | bytes 786432 | tf_op jit(solution)/shard_map/all_to_all | solution.py:110
  472.0 72.5 %copy-start.5 = (f32[24,2048]{1,0:T(8,128)S(1)}, f32[24,2048]{1,0:T(8,128)}, u32[]{:S(2)}) copy-start(f32[24,2048]{1,0:T(8,128)} %get-tuple-element.349.d_ref) | copy-start | bytes 589828
  480.4 87.9 %copy-start.13 = (f32[2,24,2048]{2,1,0:T(8,128)S(1)}, f32[2,24,2048]{2,1,0:T(8,128)}, u32[]{:S(2)}) copy-start(f32[2,24,2048]{2,1,0:T(8,128)} %multiply_add_fusion.2.di_ref) | copy-start | bytes 1179652
  556.0 12.0 %all-to-all-start.37 = ((f32[48,16,128]{2,0,1:T(8,128)}), f32[48,16,128]{2,0,1:T(8,128)S(1)}, u32[]{:S(2)}, u32[]{:S(2)}) async-start(f32[48,16,128]{2,0,1:T(8,128)} %tile.66), calls=%async_computation.37 | async-start | bytes 786432 | tf_op jit(solution)/shard_map/all_to_all | solution.py:110
  560.8 72.5 %copy-start.6 = (f32[24,2048]{1,0:T(8,128)S(1)}, f32[24,2048]{1,0:T(8,128)}, u32[]{:S(2)}) copy-start(f32[24,2048]{1,0:T(8,128)} %get-tuple-element.345.d_ref) | copy-start | bytes 589828
  569.1 87.6 %copy-start.8 = (f32[2,24,2048]{2,1,0:T(8,128)S(1)}, f32[2,24,2048]{2,1,0:T(8,128)}, u32[]{:S(2)}) copy-start(f32[2,24,2048]{2,1,0:T(8,128)} %multiply_add_fusion.1.di_ref) | copy-start | bytes 1179652
  644.8 11.8 %all-to-all-start.43 = ((f32[48,16,128]{2,0,1:T(8,128)}), f32[48,16,128]{2,0,1:T(8,128)S(1)}, u32[]{:S(2)}, u32[]{:S(2)}) async-start(f32[48,16,128]{2,0,1:T(8,128)} %tile.69), calls=%async_computation.43 | async-start | bytes 786432 | tf_op jit(solution)/shard_map/all_to_all | solution.py:110
  649.3 72.4 %copy-start.15 = (f32[24,2048]{1,0:T(8,128)S(1)}, f32[24,2048]{1,0:T(8,128)}, u32[]{:S(2)}) copy-start(f32[24,2048]{1,0:T(8,128)} %get-tuple-element.341.d_ref) | copy-start | bytes 589828
